TPU v7x, 256 devices: a whole 4x4x8 slice. The times are simulated.
256 devices in a mesh: dp: 2 (over z_lo), expert: 32 (over y, z_hi, core), tensor: 4 (over x).
Axes of the slice: x: 4, y: 4, z: 8 (z_hi: 4, z_lo: 2; z = z_hi * 2 + z_lo), core: 2. Of those that a mesh axis runs over, the one named last changes fastest.
Arguments:
- context: bfloat16 [8192, 2048], P(('dp', 'expert'), 'tensor'), may hold values from -6 to 6
- residual: bfloat16 [8192, 2048], P(('dp', 'expert')), may hold values from -6 to 6
- wo_rows: bfloat16 [2048, 2048], P('tensor'), may hold values from -0.125 to 0.125
- norm_gain: float32 [2048], replicated, may hold values from 0.25 to 1.75
- analyzer_out: bfloat16 [8192, 2048], P(('dp', 'expert'), 'tensor'), may hold values from -6 to 6
- gate_probs: float32 [8192, 6], P(('dp', 'expert')), may hold values from 0.05 to 0.5
- expert_ids: int32 [8192, 6], P(('dp', 'expert')), may hold values from 0 to 63, all different within a row; in each aligned block of 128 rows (0 to 127, 128 to 255, ...) at most 14 rows name the same one
- w_gate_up: bfloat16 [64, 2, 2048, 1408], P('expert', None, 'dp', 'tensor'), may hold values from -0.125 to 0.125
- w_down: bfloat16 [64, 1408, 2048], P('expert', 'tensor', 'dp'), may hold values from -0.15625 to 0.15625
Outputs:
- block_out: bfloat16 [8192, 2048], P(('dp', 'expert'), 'tensor')
- context_grad: bfloat16 [8192, 2048], P(('dp', 'expert'), 'tensor')
- gate_prob_grad: float32 [8192, 6], P(('dp', 'expert'))
- gate_up_grad: bfloat16 [64, 2, 2048, 1408], P('expert', None, 'dp', 'tensor')
- down_grad: bfloat16 [64, 1408, 2048], P('expert', 'tensor', 'dp')
Inputs may be any that keep to these rules, and one draw needn't show every extreme that they name: `expert_ids`: each row names 6 different experts; within each device's rows (aligned blocks of 128 rows) no expert is named more than 14 times, a bound that some block reaches.
All inputs are finite; a program needn't handle non-finite values.
Results may differ from a plain program's by a relative error of at most 0.024.
Values may be sent and summed in bfloat16 or wider, within the bound.
No kernel may reach another device: no remote copies, remote signals or barrier semaphores. Data moves between devices by JAX's collectives and lax.ppermute only.
A program may use at most 128 MiB of HBM per device.

v0:
```python
import jax
import jax.numpy as jnp
from jax import lax
from jax.sharding import PartitionSpec as P

EXPERTS = 64
CAP = 14


NORM_EPS = 1e-06
LOSS_WEIGHT = 0.25


def to_experts(outgoing):
    return lax.all_to_all(outgoing, "expert", split_axis=1, concat_axis=1, tiled=True)


def to_tokens(outgoing):
    return lax.all_to_all(outgoing, "expert", split_axis=1, concat_axis=1, tiled=True)


def weight_terms(arrived, activation, grad_in, d_gate_pre, d_up_pre):
    down_part = jnp.einsum(
        "escf,escd->efd", activation, grad_in, preferred_element_type=jnp.float32
    )
    gate_part = jnp.einsum(
        "escd,escf->edf", arrived, d_gate_pre, preferred_element_type=jnp.float32
    )
    up_part = jnp.einsum("escd,escf->edf", arrived, d_up_pre, preferred_element_type=jnp.float32)
    return (jnp.stack([gate_part, up_part], axis=1), down_part)


def per_device(
    context, residual, wo_rows, norm_gain, analyzer_out, gate_probs, expert_ids, w_gate_up, w_down
):
    tok_count, top_count = expert_ids.shape
    feature_count = residual.shape[1]
    tensor_count = lax.axis_size("tensor")
    expert_ranks = lax.axis_size("expert")
    col_count = feature_count // tensor_count
    col_start = lax.axis_index("tensor") * col_count
    local_experts = w_gate_up.shape[0]
    slot_count = EXPERTS * CAP
    expert_range = jnp.arange(EXPERTS, dtype=jnp.int32)
    slot_order = expert_range % local_experts * expert_ranks + expert_range // local_experts
    gate_up_full, down_full = (
        lax.all_gather(w_gate_up, "dp", axis=2, tiled=True),
        lax.all_gather(w_down, "dp", axis=2, tiled=True),
    )
    partial_attn = jnp.dot(context, wo_rows, preferred_element_type=jnp.float32)
    hidden_in = residual.astype(jnp.float32) + lax.psum(
        partial_attn.astype(jnp.bfloat16), "tensor"
    ).astype(jnp.float32)
    inv_rms = lax.rsqrt(jnp.mean(hidden_in * hidden_in, axis=1, keepdims=True) + NORM_EPS)
    normed = (norm_gain * hidden_in * inv_rms).astype(jnp.bfloat16)
    flat_ids = expert_ids.reshape(-1)
    onehot = (flat_ids[:, None] == expert_range[None, :]).astype(jnp.int32)
    slot_index = jnp.sum((jnp.cumsum(onehot, axis=0) - onehot) * onehot, axis=1)
    expert_slot = jnp.sum(onehot * slot_order[None, :], axis=1)
    dest_row = expert_slot * CAP + slot_index
    sentinel = tok_count * top_count
    row_entry = (
        jnp.full((slot_count,), sentinel, jnp.int32)
        .at[dest_row]
        .set(jnp.arange(sentinel, dtype=jnp.int32))
    )
    row_token = row_entry // top_count
    gate_pad = jnp.concatenate([gate_probs.reshape(-1), jnp.zeros((1,), jnp.float32)])
    row_gate = gate_pad[row_entry]
    normed_pad = jnp.concatenate([normed, jnp.zeros((1, feature_count), jnp.bfloat16)], axis=0)
    outgoing = normed_pad[row_token].reshape(local_experts, expert_ranks, CAP, feature_count)
    arrived = to_experts(outgoing)
    gate_full = gate_up_full[:, 0]
    up_full = gate_up_full[:, 1]
    pre_gate = jnp.einsum("escd,edf->escf", arrived, gate_full, preferred_element_type=jnp.float32)
    pre_up = jnp.einsum("escd,edf->escf", arrived, up_full, preferred_element_type=jnp.float32)
    activation = (jax.nn.silu(pre_gate) * pre_up).astype(jnp.bfloat16)
    partial_out = jnp.einsum(
        "escf,efd->escd", activation, down_full, preferred_element_type=jnp.float32
    )
    summed_out = lax.psum_scatter(
        partial_out.astype(jnp.bfloat16), "tensor", scatter_dimension=3, tiled=True
    )
    returned = to_tokens(summed_out).reshape(slot_count, col_count)
    entry_out = returned[dest_row].reshape(tok_count, top_count, col_count).astype(jnp.float32)
    hidden_cols = lax.dynamic_slice_in_dim(hidden_in, col_start, col_count, 1)
    block_out = (hidden_cols + jnp.sum(gate_probs[:, :, None] * entry_out, axis=1)).astype(
        jnp.bfloat16
    )
    error = (
        LOSS_WEIGHT * (block_out.astype(jnp.float32) - analyzer_out.astype(jnp.float32))
    ).astype(jnp.bfloat16)
    gate_partial = jnp.sum(error.astype(jnp.float32)[:, None, :] * entry_out, axis=2)
    error_full = lax.all_gather(error, "tensor", axis=1, tiled=True)
    error_pad = jnp.concatenate([error_full, jnp.zeros((1, feature_count), jnp.bfloat16)], axis=0)
    grad_slot = (row_gate[:, None] * error_pad[row_token].astype(jnp.float32)).astype(jnp.bfloat16)
    grad_slot = grad_slot.reshape(local_experts, expert_ranks, CAP, feature_count)
    grad_in = to_experts(grad_slot)
    d_act = jnp.einsum("escd,efd->escf", grad_in, down_full, preferred_element_type=jnp.float32)
    sigmoid_pre = jax.nn.sigmoid(pre_gate)
    d_gate_pre = (d_act * pre_up * sigmoid_pre * (1.0 + pre_gate * (1.0 - sigmoid_pre))).astype(
        jnp.bfloat16
    )
    d_up_pre = (d_act * pre_gate * sigmoid_pre).astype(jnp.bfloat16)
    d_entry_part = jnp.einsum(
        "escf,edf->escd", d_gate_pre, gate_full, preferred_element_type=jnp.float32
    )
    d_entry_part = d_entry_part + jnp.einsum(
        "escf,edf->escd", d_up_pre, up_full, preferred_element_type=jnp.float32
    )
    d_entry_sum = lax.psum_scatter(
        d_entry_part.astype(jnp.bfloat16), "tensor", scatter_dimension=3, tiled=True
    )
    d_returned = to_tokens(d_entry_sum).reshape(slot_count, col_count)
    d_normed = jnp.sum(
        d_returned[dest_row].reshape(tok_count, top_count, col_count).astype(jnp.float32), axis=1
    )
    gain_cols = lax.dynamic_slice_in_dim(norm_gain, col_start, col_count, 0)
    scaled = gain_cols * d_normed
    norm_partial = jnp.sum(scaled * hidden_cols, axis=1)
    norm_dots, gate_prob_grad = lax.psum((norm_partial, gate_partial), "tensor")
    cubed = inv_rms * inv_rms * inv_rms
    d_hidden = (
        error.astype(jnp.float32)
        + inv_rms * scaled
        - hidden_cols * cubed * norm_dots[:, None] / feature_count
    ).astype(jnp.bfloat16)
    context_grad = lax.dot_general(
        lax.all_gather(d_hidden, "tensor", axis=1, tiled=True),
        wo_rows,
        (((1,), (1,)), ((), ())),
        preferred_element_type=jnp.float32,
    ).astype(jnp.bfloat16)
    gate_up_part, down_part = weight_terms(arrived, activation, grad_in, d_gate_pre, d_up_pre)
    gate_up_grad, down_grad = (
        lax.psum_scatter(
            gate_up_part.astype(jnp.bfloat16), "dp", scatter_dimension=2, tiled=True
        ).astype(jnp.float32),
        lax.psum_scatter(
            down_part.astype(jnp.bfloat16), "dp", scatter_dimension=2, tiled=True
        ).astype(jnp.float32),
    )
    return (
        block_out,
        context_grad,
        gate_prob_grad,
        gate_up_grad.astype(jnp.bfloat16),
        down_grad.astype(jnp.bfloat16),
    )


def solution(mesh):
    in_specs = (
        P(("dp", "expert"), "tensor"),
        P(("dp", "expert"), None),
        P("tensor", None),
        P(),
        P(("dp", "expert"), "tensor"),
        P(("dp", "expert"), None),
        P(("dp", "expert"), None),
        P("expert", None, "dp", "tensor"),
        P("expert", "tensor", "dp"),
    )
    out_specs = (
        P(("dp", "expert"), "tensor"),
        P(("dp", "expert"), "tensor"),
        P(("dp", "expert"), None),
        P("expert", None, "dp", "tensor"),
        P("expert", "tensor", "dp"),
    )
    return jax.shard_map(
        per_device, mesh=mesh, in_specs=in_specs, out_specs=out_specs, check_vma=False
    )
```

profile of v0, /device:TPU:32, one launch (start us, length us, event | category | flops | bytes accessed | tf_op | source)
XLA Modules:
  0.0 651.0 jit_solution(14605199587444355152)
XLA Ops:
  22.3 40.5 %all-reduce.5.cloned.1.call-done = bf16[128,2048]{1,0:T(8,128)(2,1)} async-done(((bf16[128,2048]{1,0:T(8,128)(2,1)}), bf16[128,2048]{1,0:T(8,128)(2,1)}) %all-reduce.5.cloned.1.call-update) | async-done | bytes 524304 | tf_op jit(solution)/shard_map/psum | solution.py:51
  71.4 6.0 reshape.133
  77.4 7.8 %copy.53 = bf16[2,32,14,2048]{3,0,2,1:T(2,128)(2,1)} copy(bf16[2,32,14,2048]{3,2,1,0:T(8,128)(2,1)} %reshape.133) | data formatting | bytes 7340032 | tf_op jit(solution)/shard_map/reshape | solution.py:71
  85.2 9.1 %all-to-all-start = ((bf16[2,32,14,2048]{3,0,2,1:T(2,128)(2,1)}), bf16[2,32,14,2048]{3,0,2,1:T(2,128)(2,1)}, u32[]{:S(2)}, u32[]{:S(2)}) async-start(bf16[2,32,14,2048]{3,0,2,1:T(2,128)(2,1)} %copy.53), calls=%async_computation | async-start | bytes 7340032 | tf_op jit(solution)/shard_map/all_to_all | solution.py:15
  96.4 103.7 %all-to-all-done = bf16[2,32,14,2048]{3,0,2,1:T(2,128)(2,1)} async-done(((bf16[2,32,14,2048]{3,0,2,1:T(2,128)(2,1)}), bf16[2,32,14,2048]{3,0,2,1:T(2,128)(2,1)}, u32[]{:S(2)}, u32[]{:S(2)}) %all-to-all-start) | async-done | bytes 3670048 | tf_op jit(solution)/shard_map/all_to_all | solution.py:15
  200.1 7.4 %fusion.8 = f32[2,32,14,352]{3,1,2,0:T(8,128)S(1)} fusion(bf16[2,2,2048,352]{2,3,0,1:T(8,128)(2,1)} %all-gather.3.cloned.1.call-done, bf16[2,32,14,2048]{3,0,2,1:T(2,128)(2,1)} %all-to-all-done), kind=kOutput, calls=%fused_computation.23 | convolution fusion | flops 1291845632 | bytes 7815168 | tf_op jit(solution)/shard_map/escd,edf->escf/dot_general | solution.py:75
  208.7 7.7 %multiply_convert_fusion.3 = (bf16[2,32,14,352]{3,1,2,0:T(8,128)(2,1)S(1)}, f32[2,32,14,352]{3,1,2,0:T(8,128)}) fusion(f32[2,32,14,352]{3,1,2,0:T(8,128)S(1)} %fusion.8, bf16[2,2,2048,352]{2,3,0,1:T(8,128)(2,1)S(1)} %copy-done.1, bf16[2,32,14,2048]{3,0,2,1:T(2,128)(2,1)} %all-to-all-done), kind=kOutput, calls=%fused_computation.34 | convolution fusion | flops 1293737984 | bytes 9822208 | tf_op jit(solution)/shard_map/escd,edf->escf/dot_general | solution.py:76
  216.5 5.9 convolution_convert_fusion
  222.4 48.6 %reduce-scatter.5.cloned.1.call-done = bf16[2,32,14,512]{3,1,2,0:T(8,128)(2,1)} async-done(((bf16[2,32,14,2048]{3,1,2,0:T(8,128)(2,1)}), bf16[2,32,14,512]{3,1,2,0:T(8,128)(2,1)}) %reduce-scatter.5.cloned.1.call-update) | async-done | bytes 917520 | tf_op jit(solution)/shard_map/reduce_scatter | solution.py:81
  274.1 9.3 %all-to-all-start.1 = ((bf16[2,32,14,512]{3,0,2,1:T(2,128)(2,1)}), bf16[2,32,14,512]{3,0,2,1:T(2,128)(2,1)S(1)}, u32[]{:S(2)}, u32[]{:S(2)}) async-start(bf16[2,32,14,512]{3,0,2,1:T(2,128)(2,1)} %copy.57), calls=%async_computation.2 | async-start | bytes 1835008 | tf_op jit(solution)/shard_map/all_to_all | solution.py:19
  287.6 19.1 %all-to-all-done.1 = bf16[2,32,14,512]{3,0,2,1:T(2,128)(2,1)S(1)} async-done(((bf16[2,32,14,512]{3,0,2,1:T(2,128)(2,1)}), bf16[2,32,14,512]{3,0,2,1:T(2,128)(2,1)S(1)}, u32[]{:S(2)}, u32[]{:S(2)}) %all-to-all-start.1) | async-done | bytes 917536 | tf_op jit(solution)/shard_map/all_to_all | solution.py:19
  319.1 13.4 %all_gather.14 = bf16[128,2048]{1,0:T(8,128)(2,1)S(1)} all-gather(bf16[128,512]{1,0:T(8,128)(2,1)S(1)} %get-tuple-element.30), channel_id=1, replica_groups=mesh['dp'=2,'expert'=32,'tensor'=4] {'tensor'}, dimensions={1}, use_global_device_ids=true | all-gather | bytes 655360 | tf_op jit(solution)/shard_map/all_gather | solution.py:94
  337.5 6.3 reshape.138
  351.6 72.6 %all_to_all.20 = bf16[2,32,14,2048]{3,0,2,1:T(2,128)(2,1)S(1)} all-to-all(bf16[2,32,14,2048]{3,0,2,1:T(2,128)(2,1)S(1)} %copy.60), channel_id=1, replica_groups=mesh['dp'=2,'expert'=32,'tensor'=4] {'expert'}, dimensions={1} | all-to-all | bytes 7340032 | tf_op jit(solution)/shard_map/all_to_all | solution.py:15
  424.2 7.9 %multiply_convert_fusion.1 = (bf16[2,32,14,352]{3,1,2,0:T(8,128)(2,1)S(1)}, bf16[2,32,14,352]{3,1,2,0:T(8,128)(2,1)S(1)}) fusion(f32[2,32,14,352]{3,1,2,0:T(8,128)} %copy-done.14, f32[2,32,14,352]{3,1,2,0:T(8,128)} %get-tuple-element.41, bf16[2,352,2048]{2,1,0:T(8,128)(2,1)S(1)} %copy-done.4, bf16[2,32,14,2048]{3,0,2,1:T(2,128)(2,1)S(1)} %all_to_all.20), kind=kOutput, calls=%fused_computation.32 | convolution fusion | flops 1295945728 | bytes 10338304 | tf_op jit(solution)/shard_map/escd,efd->escf/dot_general | solution.py:99
  438.5 6.8 %fusion.4 = bf16[2,1,2048,352]{2,3,0,1:T(8,128)(2,1)S(1)} fusion(bf16[2,32,14,352]{3,1,2,0:T(8,128)(2,1)S(1)} %get-tuple-element.32, bf16[2,32,14,2048]{3,0,2,1:T(2,128)(2,1)} %all-to-all-done), kind=kOutput, calls=%fused_computation.17 | convolution fusion | flops 1293287424 | bytes 7184384 | tf_op jit(solution)/shard_map/escd,escf->edf/dot_general | solution.py:29
  445.4 6.8 %fusion.3 = bf16[2,1,2048,352]{2,3,0,1:T(8,128)(2,1)S(1)} fusion(bf16[2,32,14,352]{3,1,2,0:T(8,128)(2,1)S(1)} %copy-done.9, bf16[2,32,14,2048]{3,0,2,1:T(2,128)(2,1)} %all-to-all-done), kind=kOutput, calls=%fused_computation.16 | convolution fusion | flops 1293287424 | bytes 7184384 | tf_op jit(solution)/shard_map/escd,escf->edf/dot_general | solution.py:26
  456.2 8.3 %bitcast_convert_fusion = bf16[2,352,2048]{2,1,0:T(8,128)(2,1)} fusion(bf16[2,32,14,352]{3,1,2,0:T(8,128)(2,1)S(1)} %copy-done.7, bf16[2,32,14,2048]{3,0,2,1:T(2,128)(2,1)} %copy-done.2), kind=kOutput, calls=%fused_computation.9 | convolution fusion | flops 1293287424 | bytes 7184384 | tf_op jit(solution)/shard_map/escf,escd->efd/dot_general | solution.py:23
  464.6 34.0 %reduce-scatter.7.cloned.1.call-done = bf16[2,32,14,512]{3,1,2,0:T(8,128)(2,1)} async-done(((bf16[2,32,14,2048]{3,1,2,0:T(8,128)(2,1)}), bf16[2,32,14,512]{3,1,2,0:T(8,128)(2,1)}) %reduce-scatter.7.cloned.1.call-update) | async-done | bytes 917520 | tf_op jit(solution)/shard_map/reduce_scatter | solution.py:111
  501.7 9.0 %all-to-all-start.3 = ((bf16[2,32,14,512]{3,0,2,1:T(2,128)(2,1)}), bf16[2,32,14,512]{3,0,2,1:T(2,128)(2,1)S(1)}, u32[]{:S(2)}, u32[]{:S(2)}) async-start(bf16[2,32,14,512]{3,0,2,1:T(2,128)(2,1)} %copy.62), calls=%async_computation.5 | async-start | bytes 1835008 | tf_op jit(solution)/shard_map/all_to_all | solution.py:19
  513.4 35.3 %all-to-all-done.3 = bf16[2,32,14,512]{3,0,2,1:T(2,128)(2,1)S(1)} async-done(((bf16[2,32,14,512]{3,0,2,1:T(2,128)(2,1)}), bf16[2,32,14,512]{3,0,2,1:T(2,128)(2,1)S(1)}, u32[]{:S(2)}, u32[]{:S(2)}) %all-to-all-start.3) | async-done | bytes 917536 | tf_op jit(solution)/shard_map/all_to_all | solution.py:19
  559.8 16.1 %all-reduce.2 = (f32[128]{0:T(128)}, f32[128,6]{1,0:T(8,128)}) all-reduce(f32[128]{0:T(128)S(1)} %multiply_reduce_fusion.3, f32[128,6]{1,0:T(8,128)} %multiply_reduce_fusion), channel_id=1, replica_groups=mesh['dp'=2,'expert'=32,'tensor'=4] {'tensor'}, use_global_device_ids=true, to_apply=%region_12.13 | all-reduce | flops 896 | bytes 7168 | tf_op jit(solution)/shard_map/psum | solution.py:121
  578.2 12.8 %all_gather.15 = bf16[128,2048]{1,0:T(8,128)(2,1)S(1)} all-gather(bf16[128,512]{1,0:T(8,128)(2,1)S(1)} %subtract_convert_fusion), channel_id=1, replica_groups=mesh['dp'=2,'expert'=32,'tensor'=4] {'tensor'}, dimensions={1}, use_global_device_ids=true | all-gather | bytes 655360 | tf_op jit(solution)/shard_map/all_gather | solution.py:129
  599.5 43.9 %reduce-scatter.11.cloned.1.call-done = bf16[2,352,1024]{2,1,0:T(8,128)(2,1)} async-done(((bf16[2,352,2048]{2,1,0:T(8,128)(2,1)}), bf16[2,352,1024]{2,1,0:T(8,128)(2,1)}) %reduce-scatter.11.cloned.1.call-update) | async-done | bytes 1441808 | tf_op jit(solution)/shard_map/reduce_scatter | solution.py:139
  (107 shorter events, 96.4 us)
Async XLA Ops:
  8.0 1.6 copy-start
  8.0 54.8 %all-reduce.5.cloned.1.call-start = ((), (), s32[]{:S(2)}) async-start(), calls=%async_computation.8 | async-start | bytes 1048576 | tf_op jit(solution)/shard_map/psum | solution.py:51
  11.8 84.7 %all-gather.3.cloned.1.call-start = ((), (), s32[]{:S(2)}) async-start(), calls=%async_computation.9 | async-start | bytes 8650752 | tf_op jit(solution)/shard_map/all_gather | solution.py:47
  15.5 47.3 %copy-start.5 = (bf16[128,2048]{1,0:T(8,128)(2,1)S(1)}, bf16[128,2048]{1,0:T(8,128)(2,1)}, u32[]{:S(2)}) copy-start(bf16[128,2048]{1,0:T(8,128)(2,1)} %param.10) | copy-start | bytes 1572868
  15.5 48.6 %copy-start.11 = (f32[2048]{0:T(1024)S(1)}, f32[2048]{0:T(1024)}, u32[]{:S(2)}) copy-start(f32[2048]{0:T(1024)} %param.12) | copy-start | bytes 24580
  85.2 114.9 %all-to-all-start = ((bf16[2,32,14,2048]{3,0,2,1:T(2,128)(2,1)}), bf16[2,32,14,2048]{3,0,2,1:T(2,128)(2,1)}, u32[]{:S(2)}, u32[]{:S(2)}) async-start(bf16[2,32,14,2048]{3,0,2,1:T(2,128)(2,1)} %copy.53), calls=%async_computation | async-start | bytes 7340032 | tf_op jit(solution)/shard_map/all_to_all | solution.py:15
  94.3 122.2 %all-gather.5.cloned.1.call-start = ((), (), s32[]{:S(2)}) async-start(), calls=%async_computation.10 | async-start | bytes 4325376 | tf_op jit(solution)/shard_map/all_gather | solution.py:48
  94.9 176.2 %reduce-scatter.5.cloned.1.call-start = ((), (), s32[]{:S(2)}) async-start(), calls=%async_computation.11 | async-start | bytes 4587520 | tf_op jit(solution)/shard_map/reduce_scatter | solution.py:81
  200.1 8.6 %copy-start.1 = (bf16[2,2,2048,352]{2,3,0,1:T(8,128)(2,1)S(1)}, bf16[2,2,2048,352]{2,3,0,1:T(8,128)(2,1)}, u32[]{:S(2)}) copy-start(bf16[2,2,2048,352]{2,3,0,1:T(8,128)(2,1)} %all-gather.3.cloned.1.call-done) | copy-start | bytes 17301508
  216.4 5.9 copy-start.6
  222.4 61.1 %copy-start.13 = (f32[128,6]{0,1:T(8,128)S(1)}, f32[128,6]{0,1:T(8,128)}, u32[]{:S(2)}) copy-start(f32[128,6]{0,1:T(8,128)} %param.14) | copy-start | bytes 9220
  274.1 32.6 %all-to-all-start.1 = ((bf16[2,32,14,512]{3,0,2,1:T(2,128)(2,1)}), bf16[2,32,14,512]{3,0,2,1:T(2,128)(2,1)S(1)}, u32[]{:S(2)}, u32[]{:S(2)}) async-start(bf16[2,32,14,512]{3,0,2,1:T(2,128)(2,1)} %copy.57), calls=%async_computation.2 | async-start | bytes 1835008 | tf_op jit(solution)/shard_map/all_to_all | solution.py:19
  283.5 215.1 %reduce-scatter.7.cloned.1.call-start = ((), (), s32[]{:S(2)}) async-start(), calls=%async_computation.12 | async-start | bytes 4587520 | tf_op jit(solution)/shard_map/reduce_scatter | solution.py:111
  312.6 4.8 copy-start.10
  351.5 72.7 %copy-start.4 = (bf16[2,352,2048]{2,1,0:T(8,128)(2,1)S(1)}, bf16[2,352,2048]{2,1,0:T(8,128)(2,1)}, u32[]{:S(2)}) copy-start(bf16[2,352,2048]{2,1,0:T(8,128)(2,1)} %all-gather.5.cloned.1.call-done) | copy-start | bytes 8650756
  351.5 80.6 %slice-start = ((s8[5767168]{0:T(1024)(128)(4,1)}), s8[4194304]{0:T(1024)(128)(4,1)S(1)}, s32[]{:S(2)}) async-start(s8[5767168]{0:T(1024)(128)(4,1)} %bitcast.73), calls=%async_computation.15 | async-start | bytes 8388608
  424.2 7.9 %copy-start.2 = (bf16[2,32,14,2048]{3,0,2,1:T(2,128)(2,1)}, bf16[2,32,14,2048]{3,0,2,1:T(2,128)(2,1)S(1)}, u32[]{:S(2)}) copy-start(bf16[2,32,14,2048]{3,0,2,1:T(2,128)(2,1)S(1)} %all_to_all.20) | copy-start | bytes 11010052
  424.2 7.9 %slice-start.1 = ((s8[5767168]{0:T(1024)(128)(4,1)}), s8[1572864]{0:T(1024)(128)(4,1)S(1)}, s32[]{:S(2)}) async-start(s8[5767168]{0:T(1024)(128)(4,1)} %bitcast.73), calls=%async_computation.16 | async-start | bytes 3145728
  432.1 2.1 copy-start.8
  438.3 157.5 %reduce-scatter.9.cloned.1.call-start = ((), (), s32[]{:S(2)}) async-start(), calls=%async_computation.13 | async-start | bytes 8650752 | tf_op jit(solution)/shard_map/reduce_scatter | solution.py:136
  438.5 6.8 %copy-start.9 = (bf16[2,32,14,352]{3,1,2,0:T(8,128)(2,1)S(1)}, bf16[2,32,14,352]{3,1,2,0:T(8,128)(2,1)}, u32[]{:S(2)}) copy-start(bf16[2,32,14,352]{3,1,2,0:T(8,128)(2,1)} %copy-done.8) | copy-start | bytes 1892356
  455.2 188.2 %reduce-scatter.11.cloned.1.call-start = ((), (), s32[]{:S(2)}) async-start(), calls=%async_computation.14 | async-start | bytes 4325376 | tf_op jit(solution)/shard_map/reduce_scatter | solution.py:139
  501.7 47.1 %all-to-all-start.3 = ((bf16[2,32,14,512]{3,0,2,1:T(2,128)(2,1)}), bf16[2,32,14,512]{3,0,2,1:T(2,128)(2,1)S(1)}, u32[]{:S(2)}, u32[]{:S(2)}) async-start(bf16[2,32,14,512]{3,0,2,1:T(2,128)(2,1)} %copy.62), calls=%async_computation.5 | async-start | bytes 1835008 | tf_op jit(solution)/shard_map/all_to_all | solution.py:19
  554.7 5.0 copy-start.3
  (3 other events, 3.0 us)
Sparse Core Ops, SparseCore 0:
  11.9 50.8 all-reduce.4
  222.5 48.4 reduce-scatter.4
  438.4 60.1 reduce-scatter.6
  501.0 94.7 reduce-scatter.8
  598.7 44.6 reduce-scatter.10
Sparse Core Ops, SparseCore 1:
  15.6 80.8 all-gather.2
  98.1 108.5 all-gather.4
where the time goes:
time: 661 us; the launch traced here: 651 us
  waiting for transfers between devices  330 us (50%)
  blocking collectives  115 us (17%)
  local copies, waits for them, and re-layouts  78.1 us (12%)
  matrix products  60.6 us (9%)
  starting transfers between devices  28.3 us (4%)
  other arithmetic  22.5 us (3%)
  between operations  16.1 us (2%)
    all_to_all x1, waiting for transfers between devices, to_experts(): lax.all_to_all(outgoing, 'expert', split_axis=1, concat_axis=1, tiled=True)  104 us
    all_to_all x1, blocking collectives, to_experts(): lax.all_to_all(outgoing, 'expert', split_axis=1, concat_axis=1, tiled=True)  72.6 us
    all_to_all x2, waiting for transfers between devices, to_tokens(): lax.all_to_all(outgoing, 'expert', split_axis=1, concat_axis=1, tiled=True)  54.5 us
    reduce_scatter x1, waiting for transfers between devices, per_device(): lax.psum_scatter(partial_out.astype(jnp.bfloat16), 'tensor', scatter_dime...  48.6 us
    reduce_scatter x1, waiting for transfers between devices, per_device(): lax.psum_scatter(down_part.astype(jnp.bfloat16), 'dp', scatter_dimension=...  43.9 us
    psum x1, waiting for transfers between devices, per_device(): lax.psum(partial_attn.astype(jnp.bfloat16), 'tensor').astype(jnp.float32)  40.5 us
    reduce_scatter x1, waiting for transfers between devices, per_device(): lax.psum_scatter(d_entry_part.astype(jnp.bfloat16), 'tensor', scatter_dim...  34 us
    all_to_all x2, starting transfers between devices, to_tokens(): lax.all_to_all(outgoing, 'expert', split_axis=1, concat_axis=1, tiled=True)  18.3 us
  transfers between devices with their start and end apart: 10, of which 9 were waited for; matrix products, arithmetic and copies ran while one was open for 15% of the time, Pallas kernels for 0%

commit v1 on v0

--- a/solution.py
+++ b/solution.py
@@ -48,11 +48,16 @@
         lax.all_gather(w_down, "dp", axis=2, tiled=True),
     )
     partial_attn = jnp.dot(context, wo_rows, preferred_element_type=jnp.float32)
-    hidden_in = residual.astype(jnp.float32) + lax.psum(
-        partial_attn.astype(jnp.bfloat16), "tensor"
-    ).astype(jnp.float32)
-    inv_rms = lax.rsqrt(jnp.mean(hidden_in * hidden_in, axis=1, keepdims=True) + NORM_EPS)
-    normed = (norm_gain * hidden_in * inv_rms).astype(jnp.bfloat16)
+    attn_cols = lax.psum_scatter(
+        partial_attn.astype(jnp.bfloat16), "tensor", scatter_dimension=1, tiled=True
+    )
+    hidden_cols = lax.dynamic_slice_in_dim(residual, col_start, col_count, 1).astype(
+        jnp.float32
+    ) + attn_cols.astype(jnp.float32)
+    square_sum = lax.psum(jnp.sum(hidden_cols * hidden_cols, axis=1, keepdims=True), "tensor")
+    inv_rms = lax.rsqrt(square_sum / feature_count + NORM_EPS)
+    gain_cols = lax.dynamic_slice_in_dim(norm_gain, col_start, col_count, 0)
+    normed = (gain_cols * hidden_cols * inv_rms).astype(jnp.bfloat16)
     flat_ids = expert_ids.reshape(-1)
     onehot = (flat_ids[:, None] == expert_range[None, :]).astype(jnp.int32)
     slot_index = jnp.sum((jnp.cumsum(onehot, axis=0) - onehot) * onehot, axis=1)
@@ -67,9 +72,9 @@
     row_token = row_entry // top_count
     gate_pad = jnp.concatenate([gate_probs.reshape(-1), jnp.zeros((1,), jnp.float32)])
     row_gate = gate_pad[row_entry]
-    normed_pad = jnp.concatenate([normed, jnp.zeros((1, feature_count), jnp.bfloat16)], axis=0)
-    outgoing = normed_pad[row_token].reshape(local_experts, expert_ranks, CAP, feature_count)
-    arrived = to_experts(outgoing)
+    normed_pad = jnp.concatenate([normed, jnp.zeros((1, col_count), jnp.bfloat16)], axis=0)
+    outgoing = normed_pad[row_token].reshape(local_experts, expert_ranks, CAP, col_count)
+    arrived = lax.all_gather(to_experts(outgoing), "tensor", axis=3, tiled=True)
     gate_full = gate_up_full[:, 0]
     up_full = gate_up_full[:, 1]
     pre_gate = jnp.einsum("escd,edf->escf", arrived, gate_full, preferred_element_type=jnp.float32)
@@ -83,7 +88,6 @@
     )
     returned = to_tokens(summed_out).reshape(slot_count, col_count)
     entry_out = returned[dest_row].reshape(tok_count, top_count, col_count).astype(jnp.float32)
-    hidden_cols = lax.dynamic_slice_in_dim(hidden_in, col_start, col_count, 1)
     block_out = (hidden_cols + jnp.sum(gate_probs[:, :, None] * entry_out, axis=1)).astype(
         jnp.bfloat16
     )
@@ -91,11 +95,10 @@
         LOSS_WEIGHT * (block_out.astype(jnp.float32) - analyzer_out.astype(jnp.float32))
     ).astype(jnp.bfloat16)
     gate_partial = jnp.sum(error.astype(jnp.float32)[:, None, :] * entry_out, axis=2)
-    error_full = lax.all_gather(error, "tensor", axis=1, tiled=True)
-    error_pad = jnp.concatenate([error_full, jnp.zeros((1, feature_count), jnp.bfloat16)], axis=0)
+    error_pad = jnp.concatenate([error, jnp.zeros((1, col_count), jnp.bfloat16)], axis=0)
     grad_slot = (row_gate[:, None] * error_pad[row_token].astype(jnp.float32)).astype(jnp.bfloat16)
-    grad_slot = grad_slot.reshape(local_experts, expert_ranks, CAP, feature_count)
-    grad_in = to_experts(grad_slot)
+    grad_slot = grad_slot.reshape(local_experts, expert_ranks, CAP, col_count)
+    grad_in = lax.all_gather(to_experts(grad_slot), "tensor", axis=3, tiled=True)
     d_act = jnp.einsum("escd,efd->escf", grad_in, down_full, preferred_element_type=jnp.float32)
     sigmoid_pre = jax.nn.sigmoid(pre_gate)
     d_gate_pre = (d_act * pre_up * sigmoid_pre * (1.0 + pre_gate * (1.0 - sigmoid_pre))).astype(
@@ -115,7 +118,6 @@
     d_normed = jnp.sum(
         d_returned[dest_row].reshape(tok_count, top_count, col_count).astype(jnp.float32), axis=1
     )
-    gain_cols = lax.dynamic_slice_in_dim(norm_gain, col_start, col_count, 0)
     scaled = gain_cols * d_normed
     norm_partial = jnp.sum(scaled * hidden_cols, axis=1)
     norm_dots, gate_prob_grad = lax.psum((norm_partial, gate_partial), "tensor")

time: 661 us -> 618 us (0.935)
  local copies, waits for them, and re-layouts: 78.1 us -> 58.7 us
  matrix products: 60.6 us -> 44.7 us
  waiting for transfers between devices: 330 us -> 345 us
  starting transfers between devices: 28.3 us -> 18.7 us
    all_to_all x1 -> x0, waiting for transfers between devices: 104 us -> none  [to_experts(): lax.all_to_all(outgoing, 'expert', split_axis=1, concat_axis=1, tiled=True)]
    all_gather x0 -> x2, waiting for transfers between devices: none -> 96.6 us  [the longest x1 50.2 us: per_device(): arrived = lax.all_gather(to_experts(outgoing), 'tensor', axis=3, tiled=True)]
    psum x1 -> x0, waiting for transfers between devices: 40.5 us -> none  [per_device(): lax.psum(partial_attn.astype(jnp.bfloat16), 'tensor').astype(jnp.float32)]
    all_gather x1, waiting for transfers between devices: 0.01 us -> 38.3 us  [per_device(): lax.all_gather(w_down, 'dp', axis=2, tiled=True)]
    reduce_scatter x0 -> x1, waiting for transfers between devices: none -> 15.7 us  [per_device(): lax.psum_scatter(partial_attn.astype(jnp.bfloat16), 'tensor', scatter_dim...]
    all_gather x1 -> x0, blocking collectives: 13.4 us -> none  [per_device(): error_full = lax.all_gather(error, 'tensor', axis=1, tiled=True)]
    reshape x2, local copies, waits for them, and re-layouts: 13.8 us -> 2.3 us  [per_device(): normed_pad[row_token].reshape(local_experts, expert_ranks, CAP, col_count)]
    all_gather x1, waiting for transfers between devices: 1.28 us -> 11.6 us  [per_device(): lax.all_gather(w_gate_up, 'dp', axis=2, tiled=True)]
  transfers between devices with their start and end apart: 10 -> 11, of which waited for: 9 -> 11; matrix products, arithmetic and copies ran while one was open for 15% -> 11% of each run, Pallas kernels for 0% -> 0%
where the time goes in v1:
time: 618 us; the launch traced here: 614 us
  waiting for transfers between devices  345 us (56%)
  blocking collectives  114 us (18%)
  local copies, waits for them, and re-layouts  58.7 us (9%)
  matrix products  44.7 us (7%)
  starting transfers between devices  18.7 us (3%)
  other arithmetic  17.8 us (3%)
  between operations  16.1 us (3%)
    all_to_all x2, blocking collectives, to_experts(): lax.all_to_all(outgoing, 'expert', split_axis=1, concat_axis=1, tiled=True)  77.4 us
    all_to_all x2, waiting for transfers between devices, to_tokens(): lax.all_to_all(outgoing, 'expert', split_axis=1, concat_axis=1, tiled=True)  55.4 us
    all_gather x1, waiting for transfers between devices, per_device(): arrived = lax.all_gather(to_experts(outgoing), 'tensor', axis=3, tiled=True)  50.2 us
    reduce_scatter x1, waiting for transfers between devices, per_device(): lax.psum_scatter(partial_out.astype(jnp.bfloat16), 'tensor', scatter_dime...  46.9 us
    all_gather x1, waiting for transfers between devices, per_device(): lax.all_gather(to_experts(grad_slot), 'tensor', axis=3, tiled=True)  46.4 us
    reduce_scatter x1, waiting for transfers between devices, per_device(): lax.psum_scatter(down_part.astype(jnp.bfloat16), 'dp', scatter_dimension=...  44.1 us
    all_gather x1, waiting for transfers between devices, per_device(): lax.all_gather(w_down, 'dp', axis=2, tiled=True)  38.3 us
    reduce_scatter x1, waiting for transfers between devices, per_device(): lax.psum_scatter(d_entry_part.astype(jnp.bfloat16), 'tensor', scatter_dim...  30 us
  transfers between devices with their start and end apart: 11, of which 11 were waited for; matrix products, arithmetic and copies ran while one was open for 11% of the time, Pallas kernels for 0%

profile of v1, /device:TPU:32, one launch (start us, length us, event | category | flops | bytes accessed | tf_op | source)
XLA Modules:
  0.0 614.3 jit_solution(1875440948989554557)
XLA Ops:
  23.1 15.7 %reduce-scatter.6.cloned.1.call-done = bf16[128,512]{1,0:T(8,128)(2,1)} async-done(((bf16[128,2048]{1,0:T(8,128)(2,1)}), bf16[128,512]{1,0:T(8,128)(2,1)}) %reduce-scatter.6.cloned.1.call-update) | async-done | bytes 131088 | tf_op jit(solution)/shard_map/reduce_scatter | solution.py:51
  39.8 8.3 %psum.21 = f32[128,1]{0,1:T(1,128)S(1)} all-reduce(f32[128,1]{0,1:T(1,128)S(1)} %bitcast.85), channel_id=1, replica_groups=mesh['dp'=2,'expert'=32,'tensor'=4] {'tensor'}, use_global_device_ids=true, to_apply=%region_2.3 | all-reduce | flops 128 | bytes 1024 | tf_op jit(solution)/shard_map/psum | solution.py:57
  55.4 47.3 %all_to_all.20 = bf16[2,32,14,512]{3,0,2,1:T(2,128)(2,1)S(1)} all-to-all(bf16[2,32,14,512]{3,0,2,1:T(2,128)(2,1)S(1)} %copy.49), channel_id=1, replica_groups=mesh['dp'=2,'expert'=32,'tensor'=4] {'expert'}, dimensions={1} | all-to-all | bytes 1835008 | tf_op jit(solution)/shard_map/all_to_all | solution.py:15
  104.5 11.6 %all-gather.7.cloned.1.call-done = bf16[2,2,2048,352]{2,3,0,1:T(8,128)(2,1)} async-done(((bf16[2,2,1024,352]{2,3,0,1:T(8,128)(2,1)}), bf16[2,2,2048,352]{2,3,0,1:T(8,128)(2,1)}) %all-gather.7.cloned.1.call-update) | async-done | bytes 5767184 | tf_op jit(solution)/shard_map/all_gather | solution.py:47
  116.1 50.2 %all-gather.5.cloned.1.call-done = bf16[2,32,14,2048]{3,1,2,0:T(8,128)(2,1)} async-done(((bf16[2,32,14,512]{3,1,2,0:T(8,128)(2,1)}), bf16[2,32,14,2048]{3,1,2,0:T(8,128)(2,1)}) %all-gather.5.cloned.1.call-update) | async-done | bytes 3670032 | tf_op jit(solution)/shard_map/all_gather | solution.py:77
  166.3 5.1 fusion.6
  175.7 38.3 %all-gather.9.cloned.1.call-done = bf16[2,352,2048]{2,1,0:T(8,128)(2,1)} async-done(((bf16[2,352,1024]{2,1,0:T(8,128)(2,1)}), bf16[2,352,2048]{2,1,0:T(8,128)(2,1)}) %all-gather.9.cloned.1.call-update) | async-done | bytes 2883600 | tf_op jit(solution)/shard_map/all_gather | solution.py:48
  214.0 5.7 convolution_convert_fusion
  219.7 46.9 %reduce-scatter.8.cloned.1.call-done = bf16[2,32,14,512]{3,1,2,0:T(8,128)(2,1)} async-done(((bf16[2,32,14,2048]{3,1,2,0:T(8,128)(2,1)}), bf16[2,32,14,512]{3,1,2,0:T(8,128)(2,1)}) %reduce-scatter.8.cloned.1.call-update) | async-done | bytes 917520 | tf_op jit(solution)/shard_map/reduce_scatter | solution.py:86
  269.7 9.1 %all-to-all-start.1 = ((bf16[2,32,14,512]{3,0,2,1:T(2,128)(2,1)}), bf16[2,32,14,512]{3,0,2,1:T(2,128)(2,1)S(1)}, u32[]{:S(2)}, u32[]{:S(2)}) async-start(bf16[2,32,14,512]{3,0,2,1:T(2,128)(2,1)} %copy.52), calls=%async_computation.3 | async-start | bytes 1835008 | tf_op jit(solution)/shard_map/all_to_all | solution.py:19
  283.0 19.3 %all-to-all-done.1 = bf16[2,32,14,512]{3,0,2,1:T(2,128)(2,1)S(1)} async-done(((bf16[2,32,14,512]{3,0,2,1:T(2,128)(2,1)}), bf16[2,32,14,512]{3,0,2,1:T(2,128)(2,1)S(1)}, u32[]{:S(2)}, u32[]{:S(2)}) %all-to-all-start.1) | async-done | bytes 917536 | tf_op jit(solution)/shard_map/all_to_all | solution.py:19
  322.6 30.1 %all_to_all.21 = bf16[2,32,14,512]{3,0,2,1:T(2,128)(2,1)S(1)} all-to-all(bf16[2,32,14,512]{3,0,2,1:T(2,128)(2,1)S(1)} %copy.55), channel_id=1, replica_groups=mesh['dp'=2,'expert'=32,'tensor'=4] {'expert'}, dimensions={1} | all-to-all | bytes 1835008 | tf_op jit(solution)/shard_map/all_to_all | solution.py:15
  353.9 46.4 %all-gather.11.cloned.1.call-done = bf16[2,32,14,2048]{3,1,2,0:T(8,128)(2,1)} async-done(((bf16[2,32,14,512]{3,1,2,0:T(8,128)(2,1)}), bf16[2,32,14,2048]{3,1,2,0:T(8,128)(2,1)}) %all-gather.11.cloned.1.call-update) | async-done | bytes 3670032 | tf_op jit(solution)/shard_map/all_gather | solution.py:101
  400.3 6.0 multiply_convert_fusion.1
  406.3 4.2 fusion.5
  410.5 5.8 add_convert_fusion
  426.3 5.5 bitcast_convert_fusion
  431.8 30.0 %reduce-scatter.10.cloned.1.call-done = bf16[2,32,14,512]{3,1,2,0:T(8,128)(2,1)} async-done(((bf16[2,32,14,2048]{3,1,2,0:T(8,128)(2,1)}), bf16[2,32,14,512]{3,1,2,0:T(8,128)(2,1)}) %reduce-scatter.10.cloned.1.call-update) | async-done | bytes 917520 | tf_op jit(solution)/shard_map/reduce_scatter | solution.py:114
  464.9 8.9 %all-to-all-start.3 = ((bf16[2,32,14,512]{3,0,2,1:T(2,128)(2,1)}), bf16[2,32,14,512]{3,0,2,1:T(2,128)(2,1)S(1)}, u32[]{:S(2)}, u32[]{:S(2)}) async-start(bf16[2,32,14,512]{3,0,2,1:T(2,128)(2,1)} %copy.57), calls=%async_computation.6 | async-start | bytes 1835008 | tf_op jit(solution)/shard_map/all_to_all | solution.py:19
  476.1 36.1 %all-to-all-done.3 = bf16[2,32,14,512]{3,0,2,1:T(2,128)(2,1)S(1)} async-done(((bf16[2,32,14,512]{3,0,2,1:T(2,128)(2,1)}), bf16[2,32,14,512]{3,0,2,1:T(2,128)(2,1)S(1)}, u32[]{:S(2)}, u32[]{:S(2)}) %all-to-all-start.3) | async-done | bytes 917536 | tf_op jit(solution)/shard_map/all_to_all | solution.py:19
  523.1 15.1 %all-reduce.2 = (f32[128]{0:T(128)S(1)}, f32[128,6]{1,0:T(8,128)S(1)}) all-reduce(f32[128]{0:T(128)S(1)} %multiply_reduce_fusion.2, f32[128,6]{1,0:T(8,128)S(1)} %multiply_reduce_fusion), channel_id=1, replica_groups=mesh['dp'=2,'expert'=32,'tensor'=4] {'tensor'}, use_global_device_ids=true, to_apply=%region_13.14 | all-reduce | flops 896 | bytes 7168 | tf_op jit(solution)/shard_map/psum | solution.py:123
  539.0 12.8 %all_gather.19 = bf16[128,2048]{1,0:T(8,128)(2,1)S(1)} all-gather(bf16[128,512]{1,0:T(8,128)(2,1)S(1)} %subtract_convert_fusion), channel_id=1, replica_groups=mesh['dp'=2,'expert'=32,'tensor'=4] {'tensor'}, dimensions={1}, use_global_device_ids=true | all-gather | bytes 655360 | tf_op jit(solution)/shard_map/all_gather | solution.py:131
  553.3 5.7 reduce-scatter.12.cloned.1.call-done
  562.6 44.1 %reduce-scatter.14.cloned.1.call-done = bf16[2,352,1024]{2,1,0:T(8,128)(2,1)} async-done(((bf16[2,352,2048]{2,1,0:T(8,128)(2,1)}), bf16[2,352,1024]{2,1,0:T(8,128)(2,1)}) %reduce-scatter.14.cloned.1.call-update) | async-done | bytes 1441808 | tf_op jit(solution)/shard_map/reduce_scatter | solution.py:141
  (110 shorter events, 90.1 us)
Async XLA Ops:
  8.0 1.6 copy-start
  8.0 30.7 %reduce-scatter.6.cloned.1.call-start = ((), (), s32[]{:S(2)}) async-start(), calls=%async_computation.9 | async-start | bytes 655360 | tf_op jit(solution)/shard_map/reduce_scatter | solution.py:51
  11.8 104.3 %all-gather.7.cloned.1.call-start = ((), (), s32[]{:S(2)}) async-start(), calls=%async_computation.11 | async-start | bytes 8650752 | tf_op jit(solution)/shard_map/all_gather | solution.py:47
  15.5 23.3 %copy-start.3 = (bf16[128,2048]{1,0:T(8,128)(2,1)S(1)}, bf16[128,2048]{1,0:T(8,128)(2,1)}, u32[]{:S(2)}) copy-start(bf16[128,2048]{1,0:T(8,128)(2,1)} %param.10) | copy-start | bytes 1572868
  15.5 150.7 %all-gather.5.cloned.1.call-start = ((), (), s32[]{:S(2)}) async-start(), calls=%async_computation.10 | async-start | bytes 4587520 | tf_op jit(solution)/shard_map/all_gather | solution.py:77
  103.9 110.1 %all-gather.9.cloned.1.call-start = ((), (), s32[]{:S(2)}) async-start(), calls=%async_computation.12 | async-start | bytes 4325376 | tf_op jit(solution)/shard_map/all_gather | solution.py:48
  104.5 162.2 %reduce-scatter.8.cloned.1.call-start = ((), (), s32[]{:S(2)}) async-start(), calls=%async_computation.13 | async-start | bytes 4587520 | tf_op jit(solution)/shard_map/reduce_scatter | solution.py:86
  166.3 6.2 %copy-start.1 = (bf16[2,2,2048,352]{2,3,0,1:T(8,128)(2,1)S(1)}, bf16[2,2,2048,352]{2,3,0,1:T(8,128)(2,1)}, u32[]{:S(2)}) copy-start(bf16[2,2,2048,352]{2,3,0,1:T(8,128)(2,1)} %all-gather.7.cloned.1.call-done) | copy-start | bytes 17301508
  166.3 6.2 %copy-start.12 = (bf16[2,32,14,2048]{3,1,2,0:T(8,128)(2,1)S(1)}, bf16[2,32,14,2048]{3,1,2,0:T(8,128)(2,1)}, u32[]{:S(2)}) copy-start(bf16[2,32,14,2048]{3,1,2,0:T(8,128)(2,1)} %all-gather.5.cloned.1.call-done) | copy-start | bytes 11010052
  175.6 44.0 %copy-start.5 = (bf16[2,32,14,352]{3,1,2,0:T(8,128)(2,1)}, bf16[2,32,14,352]{3,1,2,0:T(8,128)(2,1)S(1)}, u32[]{:S(2)}) copy-start(bf16[2,32,14,352]{3,1,2,0:T(8,128)(2,1)S(1)} %get-tuple-element.38) | copy-start | bytes 1892356
  219.7 59.2 %copy-start.11 = (f32[128,6]{0,1:T(8,128)S(1)}, f32[128,6]{0,1:T(8,128)}, u32[]{:S(2)}) copy-start(f32[128,6]{0,1:T(8,128)} %param.14) | copy-start | bytes 9220
  269.7 32.6 %all-to-all-start.1 = ((bf16[2,32,14,512]{3,0,2,1:T(2,128)(2,1)}), bf16[2,32,14,512]{3,0,2,1:T(2,128)(2,1)S(1)}, u32[]{:S(2)}, u32[]{:S(2)}) async-start(bf16[2,32,14,512]{3,0,2,1:T(2,128)(2,1)} %copy.52), calls=%async_computation.3 | async-start | bytes 1835008 | tf_op jit(solution)/shard_map/all_to_all | solution.py:19
  278.8 121.5 %all-gather.11.cloned.1.call-start = ((), (), s32[]{:S(2)}) async-start(), calls=%async_computation.14 | async-start | bytes 4587520 | tf_op jit(solution)/shard_map/all_gather | solution.py:101
  308.2 4.8 copy-start.2
  308.2 4.8 copy-start.9
  353.9 107.9 %reduce-scatter.10.cloned.1.call-start = ((), (), s32[]{:S(2)}) async-start(), calls=%async_computation.15 | async-start | bytes 4587520 | tf_op jit(solution)/shard_map/reduce_scatter | solution.py:114
  406.3 4.2 copy-start.7
  416.3 142.7 %reduce-scatter.12.cloned.1.call-start = ((), (), s32[]{:S(2)}) async-start(), calls=%async_computation.16 | async-start | bytes 8650752 | tf_op jit(solution)/shard_map/reduce_scatter | solution.py:138
  416.5 3.9 copy-start.8
  416.6 3.9 copy-start.13
  425.2 1.1 copy-start.6
  425.2 181.5 %reduce-scatter.14.cloned.1.call-start = ((), (), s32[]{:S(2)}) async-start(), calls=%async_computation.17 | async-start | bytes 4325376 | tf_op jit(solution)/shard_map/reduce_scatter | solution.py:141
  464.9 47.2 %all-to-all-start.3 = ((bf16[2,32,14,512]{3,0,2,1:T(2,128)(2,1)}), bf16[2,32,14,512]{3,0,2,1:T(2,128)(2,1)S(1)}, u32[]{:S(2)}, u32[]{:S(2)}) async-start(bf16[2,32,14,512]{3,0,2,1:T(2,128)(2,1)} %copy.57), calls=%async_computation.6 | async-start | bytes 1835008 | tf_op jit(solution)/shard_map/all_to_all | solution.py:19
  518.1 4.9 copy-start.4
  (2 other events, 1.8 us)
Sparse Core Ops, SparseCore 0:
  11.9 26.7 reduce-scatter.5
  219.8 46.7 reduce-scatter.7
  354.0 46.2 all-gather.10
  416.4 45.3 reduce-scatter.9
  464.2 94.7 reduce-scatter.11
  561.9 44.7 reduce-scatter.13
Sparse Core Ops, SparseCore 1:
  15.6 100.4 all-gather.6
  118.3 47.9 all-gather.4
  167.9 46.0 all-gather.8

commit v2 on v1

--- a/solution.py
+++ b/solution.py
@@ -17,6 +17,27 @@
 
 def to_tokens(outgoing):
     return lax.all_to_all(outgoing, "expert", split_axis=1, concat_axis=1, tiled=True)
+
+
+DP_SWAP = [(0, 1), (1, 0)]
+
+
+def dp_joined(own, dp_first, axis):
+    other = lax.ppermute(own, "dp", DP_SWAP)
+    return jnp.where(
+        dp_first,
+        jnp.concatenate([own, other], axis=axis),
+        jnp.concatenate([other, own], axis=axis),
+    )
+
+
+def dp_halves_summed(part, dp_first, axis):
+    half = part.shape[axis] // 2
+    low = lax.slice_in_dim(part, 0, half, axis=axis).astype(jnp.bfloat16)
+    high = lax.slice_in_dim(part, half, 2 * half, axis=axis).astype(jnp.bfloat16)
+    kept = jnp.where(dp_first, low, high)
+    arrived = lax.ppermute(jnp.where(dp_first, high, low), "dp", DP_SWAP)
+    return kept.astype(jnp.float32) + arrived.astype(jnp.float32)
 
 
 def weight_terms(arrived, activation, grad_in, d_gate_pre, d_up_pre):
@@ -43,9 +64,10 @@
     slot_count = EXPERTS * CAP
     expert_range = jnp.arange(EXPERTS, dtype=jnp.int32)
     slot_order = expert_range % local_experts * expert_ranks + expert_range // local_experts
+    dp_first = lax.axis_index("dp") == 0
     gate_up_full, down_full = (
-        lax.all_gather(w_gate_up, "dp", axis=2, tiled=True),
-        lax.all_gather(w_down, "dp", axis=2, tiled=True),
+        dp_joined(w_gate_up, dp_first, 2),
+        dp_joined(w_down, dp_first, 2),
     )
     partial_attn = jnp.dot(context, wo_rows, preferred_element_type=jnp.float32)
     attn_cols = lax.psum_scatter(
@@ -135,12 +157,8 @@
     ).astype(jnp.bfloat16)
     gate_up_part, down_part = weight_terms(arrived, activation, grad_in, d_gate_pre, d_up_pre)
     gate_up_grad, down_grad = (
-        lax.psum_scatter(
-            gate_up_part.astype(jnp.bfloat16), "dp", scatter_dimension=2, tiled=True
-        ).astype(jnp.float32),
-        lax.psum_scatter(
-            down_part.astype(jnp.bfloat16), "dp", scatter_dimension=2, tiled=True
-        ).astype(jnp.float32),
+        dp_halves_summed(gate_up_part, dp_first, 2),
+        dp_halves_summed(down_part, dp_first, 2),
     )
     return (
         block_out,

time: 618 us -> 573 us (0.927)
  waiting for transfers between devices: 345 us -> 288 us
  other arithmetic: 17.8 us -> 36.8 us
  blocking collectives: 114 us -> 99.7 us
  starting transfers between devices: 18.7 us -> 25.4 us
    ppermute x0 -> x4, waiting for transfers between devices: none -> 128 us  [the longest x2 75.1 us: dp_joined(): other = lax.ppermute(own, 'dp', DP_SWAP)]
    all_gather x1, waiting for transfers between devices: 50.2 us -> 0.01 us  [per_device(): arrived = lax.all_gather(to_experts(outgoing), 'tensor', axis=3, tiled=True)]
    all_gather x2 -> x0, waiting for transfers between devices: 49.9 us -> none  [the longest x1 38.3 us: per_device(): lax.all_gather(w_down, 'dp', axis=2, tiled=True)]
    reduce_scatter x2 -> x0, waiting for transfers between devices: 49.7 us -> none  [the longest x1 44.1 us: per_device(): lax.psum_scatter(down_part.astype(jnp.bfloat16), 'dp', scatter_dimension=...]
    all_to_all x2, waiting for transfers between devices: 55.4 us -> 24.3 us  [to_tokens(): lax.all_to_all(outgoing, 'expert', split_axis=1, concat_axis=1, tiled=True)]
    all_to_all x2, blocking collectives: 77.4 us -> 62.4 us  [to_experts(): lax.all_to_all(outgoing, 'expert', split_axis=1, concat_axis=1, tiled=True)]
    select_n x0 -> x3, other arithmetic: none -> 11.8 us  [the longest x1 8.67 us: dp_joined(): jnp.where(dp_first, jnp.concatenate([own, other], axis=axis), jnp.concate...]
    convert_element_type x0 -> x2, other arithmetic: none -> 10 us  [the longest x1 5.72 us: per_device(): gate_up_grad.astype(jnp.bfloat16)]
  transfers between devices with their start and end apart: 11 -> 11, of which waited for: 11 -> 9; matrix products, arithmetic and copies ran while one was open for 11% -> 10% of each run, Pallas kernels for 0% -> 0%
where the time goes in v2:
time: 573 us; the launch traced here: 567 us
  waiting for transfers between devices  288 us (50%)
  blocking collectives  99.7 us (17%)
  local copies, waits for them, and re-layouts  59.1 us (10%)
  matrix products  43.1 us (8%)
  other arithmetic  36.8 us (6%)
  starting transfers between devices  25.4 us (4%)
  between operations  14.7 us (3%)
    ppermute x2, waiting for transfers between devices, dp_joined(): other = lax.ppermute(own, 'dp', DP_SWAP)  75.1 us
    all_to_all x2, blocking collectives, to_experts(): lax.all_to_all(outgoing, 'expert', split_axis=1, concat_axis=1, tiled=True)  62.4 us
    ppermute x2, waiting for transfers between devices, dp_halves_summed(): arrived = lax.ppermute(jnp.where(dp_first, high, low), 'dp', DP_SWAP)  52.4 us
    all_gather x1, waiting for transfers between devices, per_device(): lax.all_gather(to_experts(grad_slot), 'tensor', axis=3, tiled=True)  46.2 us
    reduce_scatter x1, waiting for transfers between devices, per_device(): lax.psum_scatter(partial_out.astype(jnp.bfloat16), 'tensor', scatter_dime...  41.9 us
    reduce_scatter x1, waiting for transfers between devices, per_device(): lax.psum_scatter(d_entry_part.astype(jnp.bfloat16), 'tensor', scatter_dim...  28.2 us
    all_to_all x2, waiting for transfers between devices, to_tokens(): lax.all_to_all(outgoing, 'expert', split_axis=1, concat_axis=1, tiled=True)  24.3 us
    reduce_scatter x1, waiting for transfers between devices, per_device(): lax.psum_scatter(partial_attn.astype(jnp.bfloat16), 'tensor', scatter_dim...  20 us
  transfers between devices with their start and end apart: 11, of which 9 were waited for; matrix products, arithmetic and copies ran while one was open for 10% of the time, Pallas kernels for 0%

profile of v2, /device:TPU:32, one launch (start us, length us, event | category | flops | bytes accessed | tf_op | source)
XLA Modules:
  0.0 567.0 jit_solution(843453106897900228)
XLA Ops:
  17.9 20.0 %reduce-scatter.4.cloned.1.call-done = bf16[128,512]{1,0:T(8,128)(2,1)} async-done(((bf16[128,2048]{1,0:T(8,128)(2,1)}), bf16[128,512]{1,0:T(8,128)(2,1)}) %reduce-scatter.4.cloned.1.call-update) | async-done | bytes 131088 | tf_op jit(solution)/shard_map/reduce_scatter | solution.py:73
  39.0 8.3 %psum.21 = f32[128,1]{0,1:T(1,128)S(1)} all-reduce(f32[128,1]{0,1:T(1,128)S(1)} %bitcast.78), channel_id=1, replica_groups=mesh['dp'=2,'expert'=32,'tensor'=4] {'tensor'}, use_global_device_ids=true, to_apply=%region_2.3 | all-reduce | flops 128 | bytes 1024 | tf_op jit(solution)/shard_map/psum | solution.py:79
  54.6 32.1 %all_to_all.20 = bf16[2,32,14,512]{3,0,2,1:T(2,128)(2,1)S(1)} all-to-all(bf16[2,32,14,512]{3,0,2,1:T(2,128)(2,1)S(1)} %copy.55), channel_id=1, replica_groups=mesh['dp'=2,'expert'=32,'tensor'=4] {'expert'}, dimensions={1} | all-to-all | bytes 1835008 | tf_op jit(solution)/shard_map/all_to_all | solution.py:15
  91.6 5.2 collective-permute-start
  96.9 63.5 %collective-permute-done = bf16[2,2,1024,352]{2,3,0,1:T(8,128)(2,1)} collective-permute-done((bf16[2,2,1024,352]{2,3,0,1:T(8,128)(2,1)}, bf16[2,2,1024,352]{2,3,0,1:T(8,128)(2,1)}, u32[]{:S(2)}, u32[]{:S(2)}) %collective-permute-start) | collective-permute-done | bytes 2883616 | tf_op jit(solution)/shard_map/ppermute | solution.py:26
  160.4 8.7 %maximum_select_fusion = bf16[2,2,2048,352]{2,3,0,1:T(8,128)(2,1)} fusion(bf16[2,2,1024,352]{2,3,0,1:T(8,128)(2,1)} %collective-permute-done, pred[]{:T(512)S(6)} %eq.38, bf16[2,2,1024,352]{2,3,1,0:T(8,128)(2,1)} %param.16), kind=kLoop, calls=%fused_computation.8 | loop fusion | flops 25952256 | bytes 11534337 | tf_op jit(solution)/shard_map/jit(_where)/select_n | solution.py:27
  169.1 5.1 fusion.1
  177.9 11.6 %collective-permute-done.1 = bf16[2,352,1024]{2,1,0:T(8,128)(2,1)} collective-permute-done((bf16[2,352,1024]{2,1,0:T(8,128)(2,1)}, bf16[2,352,1024]{2,1,0:T(8,128)(2,1)}, u32[]{:S(2)}, u32[]{:S(2)}) %collective-permute-start.1) | collective-permute-done | bytes 1441824 | tf_op jit(solution)/shard_map/ppermute | solution.py:26
  189.5 6.9 %convolution_convert_fusion = bf16[2,32,14,2048]{3,1,2,0:T(8,128)(2,1)} fusion(bf16[2,32,14,352]{3,1,2,0:T(8,128)(2,1)S(1)} %get-tuple-element.38, bf16[2,352,1024]{2,1,0:T(8,128)(2,1)} %collective-permute-done.1, bf16[2,352,1024]{2,1,0:T(8,128)(2,1)} %param.17, pred[]{:T(512)S(6)} %eq.38), kind=kOutput, calls=%fused_computation.13 | convolution fusion | flops 1306656768 | bytes 7184385 | tf_op jit(solution)/shard_map/escf,efd->escd/dot_general | solution.py:105
  196.5 41.9 %reduce-scatter.6.cloned.1.call-done = bf16[2,32,14,512]{3,1,2,0:T(8,128)(2,1)} async-done(((bf16[2,32,14,2048]{3,1,2,0:T(8,128)(2,1)}), bf16[2,32,14,512]{3,1,2,0:T(8,128)(2,1)}) %reduce-scatter.6.cloned.1.call-update) | async-done | bytes 917520 | tf_op jit(solution)/shard_map/reduce_scatter | solution.py:108
  241.4 8.9 %all-to-all-start.1 = ((bf16[2,32,14,512]{3,0,2,1:T(2,128)(2,1)}), bf16[2,32,14,512]{3,0,2,1:T(2,128)(2,1)S(1)}, u32[]{:S(2)}, u32[]{:S(2)}) async-start(bf16[2,32,14,512]{3,0,2,1:T(2,128)(2,1)} %copy.60), calls=%async_computation.3 | async-start | bytes 1835008 | tf_op jit(solution)/shard_map/all_to_all | solution.py:19
  254.5 19.2 %all-to-all-done.1 = bf16[2,32,14,512]{3,0,2,1:T(2,128)(2,1)S(1)} async-done(((bf16[2,32,14,512]{3,0,2,1:T(2,128)(2,1)}), bf16[2,32,14,512]{3,0,2,1:T(2,128)(2,1)S(1)}, u32[]{:S(2)}, u32[]{:S(2)}) %all-to-all-start.1) | async-done | bytes 917536 | tf_op jit(solution)/shard_map/all_to_all | solution.py:19
  294.1 30.3 %all_to_all.21 = bf16[2,32,14,512]{3,0,2,1:T(2,128)(2,1)S(1)} all-to-all(bf16[2,32,14,512]{3,0,2,1:T(2,128)(2,1)S(1)} %copy.63), channel_id=1, replica_groups=mesh['dp'=2,'expert'=32,'tensor'=4] {'expert'}, dimensions={1} | all-to-all | bytes 1835008 | tf_op jit(solution)/shard_map/all_to_all | solution.py:15
  325.7 46.2 %all-gather.5.cloned.1.call-done = bf16[2,32,14,2048]{3,1,2,0:T(8,128)(2,1)} async-done(((bf16[2,32,14,512]{3,1,2,0:T(8,128)(2,1)}), bf16[2,32,14,2048]{3,1,2,0:T(8,128)(2,1)}) %all-gather.5.cloned.1.call-update) | async-done | bytes 3670032 | tf_op jit(solution)/shard_map/all_gather | solution.py:123
  371.9 7.0 %multiply_convert_fusion.2 = (bf16[2,32,14,352]{3,1,2,0:T(8,128)(2,1)S(1)}, bf16[2,32,14,352]{3,1,2,0:T(8,128)(2,1)S(1)}) fusion(f32[2,32,14,352]{3,1,2,0:T(8,128)} %copy-done.15, f32[2,32,14,352]{3,1,2,0:T(8,128)} %get-tuple-element.39, bf16[2,32,14,2048]{3,1,2,0:T(8,128)(2,1)} %all-gather.5.cloned.1.call-done, ...), kind=kOutput, calls=%fused_computation.30 | convolution fusion | flops 1308921856 | bytes 10338305 | tf_op jit(solution)/shard_map/escd,efd->escf/dot_general | solution.py:124
  383.1 5.8 %add_convert_fusion = bf16[2,32,14,2048]{3,1,2,0:T(8,128)(2,1)} fusion(f32[2,32,14,2048]{3,1,2,0:T(8,128)S(1)} %fusion.2, bf16[2,32,14,352]{3,1,2,0:T(8,128)(2,1)S(1)} %get-tuple-element.32, bf16[2,2,2048,352]{2,3,0,1:T(8,128)(2,1)} %maximum_select_fusion), kind=kOutput, calls=%fused_computation.7 | convolution fusion | flops 1295515648 | bytes 14524416 | tf_op jit(solution)/shard_map/escf,edf->escd/dot_general | solution.py:130
  406.3 28.2 %reduce-scatter.8.cloned.1.call-done = bf16[2,32,14,512]{3,1,2,0:T(8,128)(2,1)} async-done(((bf16[2,32,14,2048]{3,1,2,0:T(8,128)(2,1)}), bf16[2,32,14,512]{3,1,2,0:T(8,128)(2,1)}) %reduce-scatter.8.cloned.1.call-update) | async-done | bytes 917520 | tf_op jit(solution)/shard_map/reduce_scatter | solution.py:136
  437.6 9.0 %all-to-all-start.3 = ((bf16[2,32,14,512]{3,0,2,1:T(2,128)(2,1)}), bf16[2,32,14,512]{3,0,2,1:T(2,128)(2,1)S(1)}, u32[]{:S(2)}, u32[]{:S(2)}) async-start(bf16[2,32,14,512]{3,0,2,1:T(2,128)(2,1)} %copy.65), calls=%async_computation.6 | async-start | bytes 1835008 | tf_op jit(solution)/shard_map/all_to_all | solution.py:19
  448.5 52.4 %collective-permute-done.3 = bf16[2,352,1024]{2,1,0:T(8,128)(2,1)} collective-permute-done((bf16[2,352,1024]{2,1,0:T(8,128)(2,1)}, bf16[2,352,1024]{2,1,0:T(8,128)(2,1)}, u32[]{:S(2)}, u32[]{:S(2)}) %collective-permute-start.3) | collective-permute-done | bytes 1441824 | tf_op jit(solution)/shard_map/ppermute | solution.py:39
  500.9 4.3 add_convert_fusion.2
  505.2 5.7 %add_convert_fusion.1 = bf16[2,2,1024,352]{2,3,0,1:T(8,128)(2,1)S(1)} fusion(bf16[2,2,1024,352]{2,3,0,1:T(8,128)(2,1)} %collective-permute-done.2, pred[]{:T(512)S(6)} %eq.38, bf16[2,2,2048,352]{2,3,0,1:T(8,128)(2,1)} %copy-done.1), kind=kLoop, calls=%fused_computation.10 | loop fusion | flops 7208960 | bytes 11534337 | tf_op jit(solution)/shard_map/convert_element_type | solution.py:167
  512.8 5.1 all-to-all-done.3
  528.7 16.2 %all-reduce.2 = (f32[128]{0:T(128)S(1)}, f32[128,6]{1,0:T(8,128)S(1)}) all-reduce(f32[128]{0:T(128)S(1)} %multiply_reduce_fusion.2, f32[128,6]{1,0:T(8,128)S(1)} %multiply_reduce_fusion), channel_id=1, replica_groups=mesh['dp'=2,'expert'=32,'tensor'=4] {'tensor'}, use_global_device_ids=true, to_apply=%region_13.14 | all-reduce | flops 896 | bytes 7168 | tf_op jit(solution)/shard_map/psum | solution.py:145
  545.8 12.8 %all_gather.11 = bf16[128,2048]{1,0:T(8,128)(2,1)S(1)} all-gather(bf16[128,512]{1,0:T(8,128)(2,1)S(1)} %subtract_convert_fusion), channel_id=1, replica_groups=mesh['dp'=2,'expert'=32,'tensor'=4] {'tensor'}, dimensions={1}, use_global_device_ids=true | all-gather | bytes 655360 | tf_op jit(solution)/shard_map/all_gather | solution.py:153
  (117 shorter events, 98.0 us)
Async XLA Ops:
  7.2 30.7 %copy-start.5 = (bf16[128,2048]{1,0:T(8,128)(2,1)S(1)}, bf16[128,2048]{1,0:T(8,128)(2,1)}, u32[]{:S(2)}) copy-start(bf16[128,2048]{1,0:T(8,128)(2,1)} %param.10) | copy-start | bytes 1572868
  7.2 30.7 %reduce-scatter.4.cloned.1.call-start = ((), (), s32[]{:S(2)}) async-start(), calls=%async_computation.7 | async-start | bytes 655360 | tf_op jit(solution)/shard_map/reduce_scatter | solution.py:73
  10.9 158.1 %all-gather.3.cloned.1.call-start = ((), (), s32[]{:S(2)}) async-start(), calls=%async_computation.8 | async-start | bytes 4587520 | tf_op jit(solution)/shard_map/all_gather | solution.py:99
  87.9 150.5 %reduce-scatter.6.cloned.1.call-start = ((), (), s32[]{:S(2)}) async-start(), calls=%async_computation.9 | async-start | bytes 4587520 | tf_op jit(solution)/shard_map/reduce_scatter | solution.py:108
  91.6 68.8 %collective-permute-start = (bf16[2,2,1024,352]{2,3,0,1:T(8,128)(2,1)}, bf16[2,2,1024,352]{2,3,0,1:T(8,128)(2,1)}, u32[]{:S(2)}, u32[]{:S(2)}) collective-permute-start(bf16[2,2,1024,352]{2,3,0,1:T(8,128)(2,1)} %copy.58), channel_id=1, source_target_pairs={{0,128},{128,0},{1,129},{129,1},{2,130},{130,2},{3,131},{131,3},{4... | collective-permute-start | bytes 8650760 | tf_op jit(solution)/shard_map/ppermute | solution.py:26
  96.8 92.8 %collective-permute-start.1 = (bf16[2,352,1024]{2,1,0:T(8,128)(2,1)}, bf16[2,352,1024]{2,1,0:T(8,128)(2,1)}, u32[]{:S(2)}, u32[]{:S(2)}) collective-permute-start(bf16[2,352,1024]{2,1,0:T(8,128)(2,1)} %param.17), channel_id=1, source_target_pairs={{0,128},{128,0},{1,129},{129,1},{2,130},{130,2},{3,131},{131,3},{4... | collective-permute-start | bytes 4325384 | tf_op jit(solution)/shard_map/ppermute | solution.py:26
  169.1 5.1 copy-start.2
  169.1 5.7 copy-start.12
  177.9 11.6 %copy-start.16 = (bf16[2,32,14,352]{3,1,2,0:T(8,128)(2,1)}, bf16[2,32,14,352]{3,1,2,0:T(8,128)(2,1)S(1)}, u32[]{:S(2)}) copy-start(bf16[2,32,14,352]{3,1,2,0:T(8,128)(2,1)S(1)} %get-tuple-element.38) | copy-start | bytes 1892356
  196.4 54.0 %copy-start.11 = (f32[128,6]{0,1:T(8,128)S(1)}, f32[128,6]{0,1:T(8,128)}, u32[]{:S(2)}) copy-start(f32[128,6]{0,1:T(8,128)} %param.14) | copy-start | bytes 9220
  241.4 32.3 %all-to-all-start.1 = ((bf16[2,32,14,512]{3,0,2,1:T(2,128)(2,1)}), bf16[2,32,14,512]{3,0,2,1:T(2,128)(2,1)S(1)}, u32[]{:S(2)}, u32[]{:S(2)}) async-start(bf16[2,32,14,512]{3,0,2,1:T(2,128)(2,1)} %copy.60), calls=%async_computation.3 | async-start | bytes 1835008 | tf_op jit(solution)/shard_map/all_to_all | solution.py:19
  250.4 121.5 %all-gather.5.cloned.1.call-start = ((), (), s32[]{:S(2)}) async-start(), calls=%async_computation.10 | async-start | bytes 4587520 | tf_op jit(solution)/shard_map/all_gather | solution.py:123
  279.6 4.9 copy-start.4
  279.6 4.9 copy-start.9
  325.5 109.0 %reduce-scatter.8.cloned.1.call-start = ((), (), s32[]{:S(2)}) async-start(), calls=%async_computation.11 | async-start | bytes 4587520 | tf_op jit(solution)/shard_map/reduce_scatter | solution.py:136
  378.9 4.2 copy-start.7
  388.9 3.9 copy-start.8
  395.1 4.3 copy-start.1
  395.1 4.8 copy-start.14
  395.1 5.2 copy-start.17
  399.4 105.8 %collective-permute-start.2 = (bf16[2,2,1024,352]{2,3,0,1:T(8,128)(2,1)}, bf16[2,2,1024,352]{2,3,0,1:T(8,128)(2,1)}, u32[]{:S(2)}, u32[]{:S(2)}) collective-permute-start(bf16[2,2,1024,352]{2,3,0,1:T(8,128)(2,1)} %broadcast_select_fusion), channel_id=1, source_target_pairs={{0,128},{128,0},{1,129},{129,1},{2,130},{130,2},{3,131},{131,3},{4... | collective-permute-start | bytes 8650760 | tf_op jit(solution)/shard_map/ppermute | solution.py:39
  404.9 96.0 %collective-permute-start.3 = (bf16[2,352,1024]{2,1,0:T(8,128)(2,1)}, bf16[2,352,1024]{2,1,0:T(8,128)(2,1)}, u32[]{:S(2)}, u32[]{:S(2)}) collective-permute-start(bf16[2,352,1024]{2,1,0:T(8,128)(2,1)} %broadcast_select_fusion.1), channel_id=1, source_target_pairs={{0,128},{128,0},{1,129},{129,1},{2,130},{130,2},{3,131},{131,3},{4... | collective-permute-start | bytes 4325384 | tf_op jit(solution)/shard_map/ppermute | solution.py:39
  437.6 80.3 %all-to-all-start.3 = ((bf16[2,32,14,512]{3,0,2,1:T(2,128)(2,1)}), bf16[2,32,14,512]{3,0,2,1:T(2,128)(2,1)S(1)}, u32[]{:S(2)}, u32[]{:S(2)}) async-start(bf16[2,32,14,512]{3,0,2,1:T(2,128)(2,1)} %copy.65), calls=%async_computation.6 | async-start | bytes 1835008 | tf_op jit(solution)/shard_map/all_to_all | solution.py:19
  523.8 4.8 copy-start.6
  (5 other events, 14.1 us)
Sparse Core Ops, SparseCore 0:
  11.1 26.7 reduce-scatter.3
  88.0 45.4 all-gather.2
  196.6 41.7 reduce-scatter.5
  325.6 46.2 all-gather.4
  389.0 45.3 reduce-scatter.7

commit v3 on v2

--- a/solution.py
+++ b/solution.py
@@ -31,13 +31,17 @@
     )
 
 
-def dp_halves_summed(part, dp_first, axis):
+def dp_halves_sent(part, dp_first, axis):
     half = part.shape[axis] // 2
     low = lax.slice_in_dim(part, 0, half, axis=axis).astype(jnp.bfloat16)
     high = lax.slice_in_dim(part, half, 2 * half, axis=axis).astype(jnp.bfloat16)
     kept = jnp.where(dp_first, low, high)
     arrived = lax.ppermute(jnp.where(dp_first, high, low), "dp", DP_SWAP)
-    return kept.astype(jnp.float32) + arrived.astype(jnp.float32)
+    return kept, arrived
+
+
+def halves_added(kept, arrived):
+    return (kept.astype(jnp.float32) + arrived.astype(jnp.float32)).astype(jnp.bfloat16)
 
 
 def weight_terms(arrived, activation, grad_in, d_gate_pre, d_up_pre):
@@ -156,16 +160,17 @@
         preferred_element_type=jnp.float32,
     ).astype(jnp.bfloat16)
     gate_up_part, down_part = weight_terms(arrived, activation, grad_in, d_gate_pre, d_up_pre)
-    gate_up_grad, down_grad = (
-        dp_halves_summed(gate_up_part, dp_first, 2),
-        dp_halves_summed(down_part, dp_first, 2),
+    gate_up_kept, gate_up_arrived = dp_halves_sent(gate_up_part, dp_first, 2)
+    down_kept, down_arrived = dp_halves_sent(down_part, dp_first, 2)
+    gate_up_arrived, down_arrived, context_grad = lax.optimization_barrier(
+        (gate_up_arrived, down_arrived, context_grad)
     )
     return (
         block_out,
         context_grad,
         gate_prob_grad,
-        gate_up_grad.astype(jnp.bfloat16),
-        down_grad.astype(jnp.bfloat16),
+        halves_added(gate_up_kept, gate_up_arrived),
+        halves_added(down_kept, down_arrived),
     )
 
 

time: 573 us -> 553 us (0.965)
  waiting for transfers between devices: 288 us -> 268 us
    ppermute x2, waiting for transfers between devices: 52.4 us -> 0.01 us  [dp_halves_sent(): arrived = lax.ppermute(jnp.where(dp_first, high, low), 'dp', DP_SWAP)]
    all_to_all x2, waiting for transfers between devices: 24.3 us -> 49.8 us  [to_tokens(): lax.all_to_all(outgoing, 'expert', split_axis=1, concat_axis=1, tiled=True)]
    reduce_scatter x1, waiting for transfers between devices: 28.2 us -> 35.4 us  [per_device(): lax.psum_scatter(d_entry_part.astype(jnp.bfloat16), 'tensor', scatter_dim...]
    unnamed x41 -> x43, local copies, waits for them, and re-layouts: 13 us -> 11.5 us
  transfers between devices with their start and end apart: 11 -> 11, of which waited for: 9 -> 8; matrix products, arithmetic and copies ran while one was open for 10% -> 11% of each run, Pallas kernels for 0% -> 0%
where the time goes in v3:
time: 553 us; the launch traced here: 547 us
  waiting for transfers between devices  268 us (48%)
  blocking collectives  101 us (18%)
  local copies, waits for them, and re-layouts  57.7 us (10%)
  matrix products  45.4 us (8%)
  other arithmetic  34.4 us (6%)
  starting transfers between devices  26.2 us (5%)
  between operations  14.5 us (3%)
    ppermute x2, waiting for transfers between devices, dp_joined(): other = lax.ppermute(own, 'dp', DP_SWAP)  74.9 us
    all_to_all x2, blocking collectives, to_experts(): lax.all_to_all(outgoing, 'expert', split_axis=1, concat_axis=1, tiled=True)  62.4 us
    all_to_all x2, waiting for transfers between devices, to_tokens(): lax.all_to_all(outgoing, 'expert', split_axis=1, concat_axis=1, tiled=True)  49.8 us
    all_gather x1, waiting for transfers between devices, per_device(): lax.all_gather(to_experts(grad_slot), 'tensor', axis=3, tiled=True)  46.2 us
    reduce_scatter x1, waiting for transfers between devices, per_device(): lax.psum_scatter(partial_out.astype(jnp.bfloat16), 'tensor', scatter_dime...  41.9 us
    reduce_scatter x1, waiting for transfers between devices, per_device(): lax.psum_scatter(d_entry_part.astype(jnp.bfloat16), 'tensor', scatter_dim...  35.4 us
    reduce_scatter x1, waiting for transfers between devices, per_device(): lax.psum_scatter(partial_attn.astype(jnp.bfloat16), 'tensor', scatter_dim...  20 us
    all_to_all x2, starting transfers between devices, to_tokens(): lax.all_to_all(outgoing, 'expert', split_axis=1, concat_axis=1, tiled=True)  18.1 us
  transfers between devices with their start and end apart: 11, of which 8 were waited for; matrix products, arithmetic and copies ran while one was open for 11% of the time, Pallas kernels for 0%

profile of v3, /device:TPU:32, one launch (start us, length us, event | category | flops | bytes accessed | tf_op | source)
XLA Modules:
  0.0 547.1 jit_solution(17985678699325240766)
XLA Ops:
  17.9 20.0 %reduce-scatter.4.cloned.1.call-done = bf16[128,512]{1,0:T(8,128)(2,1)} async-done(((bf16[128,2048]{1,0:T(8,128)(2,1)}), bf16[128,512]{1,0:T(8,128)(2,1)}) %reduce-scatter.4.cloned.1.call-update) | async-done | bytes 131088 | tf_op jit(solution)/shard_map/reduce_scatter | solution.py:77
  39.0 8.3 %psum.21 = f32[128,1]{0,1:T(1,128)S(1)} all-reduce(f32[128,1]{0,1:T(1,128)S(1)} %bitcast.77), channel_id=1, replica_groups=mesh['dp'=2,'expert'=32,'tensor'=4] {'tensor'}, use_global_device_ids=true, to_apply=%region_2.3 | all-reduce | flops 128 | bytes 1024 | tf_op jit(solution)/shard_map/psum | solution.py:83
  48.3 4.0 gather_fusion
  54.6 32.1 %all_to_all.20 = bf16[2,32,14,512]{3,0,2,1:T(2,128)(2,1)S(1)} all-to-all(bf16[2,32,14,512]{3,0,2,1:T(2,128)(2,1)S(1)} %copy.55), channel_id=1, replica_groups=mesh['dp'=2,'expert'=32,'tensor'=4] {'expert'}, dimensions={1} | all-to-all | bytes 1835008 | tf_op jit(solution)/shard_map/all_to_all | solution.py:15
  91.6 5.2 collective-permute-start
  97.3 63.1 %collective-permute-done = bf16[2,2,1024,352]{2,3,0,1:T(8,128)(2,1)} collective-permute-done((bf16[2,2,1024,352]{2,3,0,1:T(8,128)(2,1)}, bf16[2,2,1024,352]{2,3,0,1:T(8,128)(2,1)}, u32[]{:S(2)}, u32[]{:S(2)}) %collective-permute-start) | collective-permute-done | bytes 2883616 | tf_op jit(solution)/shard_map/ppermute | solution.py:26
  160.4 8.5 %maximum_select_fusion = bf16[2,2,2048,352]{2,3,0,1:T(8,128)(2,1)} fusion(bf16[2,2,1024,352]{2,3,0,1:T(8,128)(2,1)} %collective-permute-done, pred[]{:T(512)S(6)} %eq.38, bf16[2,2,1024,352]{2,3,1,0:T(8,128)(2,1)} %param.16), kind=kLoop, calls=%fused_computation.8 | loop fusion | flops 25952256 | bytes 11534337 | tf_op jit(solution)/shard_map/jit(_where)/select_n | solution.py:27
  168.9 5.1 fusion.1
  177.8 11.7 %collective-permute-done.1 = bf16[2,352,1024]{2,1,0:T(8,128)(2,1)} collective-permute-done((bf16[2,352,1024]{2,1,0:T(8,128)(2,1)}, bf16[2,352,1024]{2,1,0:T(8,128)(2,1)}, u32[]{:S(2)}, u32[]{:S(2)}) %collective-permute-start.1) | collective-permute-done | bytes 1441824 | tf_op jit(solution)/shard_map/ppermute | solution.py:26
  189.5 7.0 %convolution_convert_fusion = bf16[2,32,14,2048]{3,1,2,0:T(8,128)(2,1)} fusion(bf16[2,32,14,352]{3,1,2,0:T(8,128)(2,1)S(1)} %get-tuple-element.44, bf16[2,352,1024]{2,1,0:T(8,128)(2,1)} %collective-permute-done.1, bf16[2,352,1024]{2,1,0:T(8,128)(2,1)} %param.17, pred[]{:T(512)S(6)} %eq.38), kind=kOutput, calls=%fused_computation.13 | convolution fusion | flops 1306656768 | bytes 7184385 | tf_op jit(solution)/shard_map/escf,efd->escd/dot_general | solution.py:109
  196.5 41.9 %reduce-scatter.6.cloned.1.call-done = bf16[2,32,14,512]{3,1,2,0:T(8,128)(2,1)} async-done(((bf16[2,32,14,2048]{3,1,2,0:T(8,128)(2,1)}), bf16[2,32,14,512]{3,1,2,0:T(8,128)(2,1)}) %reduce-scatter.6.cloned.1.call-update) | async-done | bytes 917520 | tf_op jit(solution)/shard_map/reduce_scatter | solution.py:112
  241.5 8.9 %all-to-all-start.1 = ((bf16[2,32,14,512]{3,0,2,1:T(2,128)(2,1)}), bf16[2,32,14,512]{3,0,2,1:T(2,128)(2,1)S(1)}, u32[]{:S(2)}, u32[]{:S(2)}) async-start(bf16[2,32,14,512]{3,0,2,1:T(2,128)(2,1)} %copy.60), calls=%async_computation.3 | async-start | bytes 1835008 | tf_op jit(solution)/shard_map/all_to_all | solution.py:19
  254.8 19.0 %all-to-all-done.1 = bf16[2,32,14,512]{3,0,2,1:T(2,128)(2,1)S(1)} async-done(((bf16[2,32,14,512]{3,0,2,1:T(2,128)(2,1)}), bf16[2,32,14,512]{3,0,2,1:T(2,128)(2,1)S(1)}, u32[]{:S(2)}, u32[]{:S(2)}) %all-to-all-start.1) | async-done | bytes 917536 | tf_op jit(solution)/shard_map/all_to_all | solution.py:19
  294.1 30.3 %all_to_all.21 = bf16[2,32,14,512]{3,0,2,1:T(2,128)(2,1)S(1)} all-to-all(bf16[2,32,14,512]{3,0,2,1:T(2,128)(2,1)S(1)} %copy.63), channel_id=1, replica_groups=mesh['dp'=2,'expert'=32,'tensor'=4] {'expert'}, dimensions={1} | all-to-all | bytes 1835008 | tf_op jit(solution)/shard_map/all_to_all | solution.py:15
  325.8 46.2 %all-gather.5.cloned.1.call-done = bf16[2,32,14,2048]{3,1,2,0:T(8,128)(2,1)} async-done(((bf16[2,32,14,512]{3,1,2,0:T(8,128)(2,1)}), bf16[2,32,14,2048]{3,1,2,0:T(8,128)(2,1)}) %all-gather.5.cloned.1.call-update) | async-done | bytes 3670032 | tf_op jit(solution)/shard_map/all_gather | solution.py:127
  372.0 7.0 %multiply_convert_fusion.2 = (bf16[2,32,14,352]{3,1,2,0:T(8,128)(2,1)S(1)}, bf16[2,32,14,352]{3,1,2,0:T(8,128)(2,1)S(1)}) fusion(f32[2,32,14,352]{3,1,2,0:T(8,128)} %copy-done.17, f32[2,32,14,352]{3,1,2,0:T(8,128)} %get-tuple-element.45, bf16[2,32,14,2048]{3,1,2,0:T(8,128)(2,1)} %all-gather.5.cloned.1.call-done, ...), kind=kOutput, calls=%fused_computation.30 | convolution fusion | flops 1308921856 | bytes 10338305 | tf_op jit(solution)/shard_map/escd,efd->escf/dot_general | solution.py:128
  379.0 4.2 fusion.2
  383.2 5.8 %add_convert_fusion = bf16[2,32,14,2048]{3,1,2,0:T(8,128)(2,1)} fusion(f32[2,32,14,2048]{3,1,2,0:T(8,128)S(1)} %fusion.2, bf16[2,32,14,352]{3,1,2,0:T(8,128)(2,1)S(1)} %get-tuple-element.38, bf16[2,2,2048,352]{2,3,0,1:T(8,128)(2,1)} %maximum_select_fusion), kind=kOutput, calls=%fused_computation.7 | convolution fusion | flops 1295515648 | bytes 14524416 | tf_op jit(solution)/shard_map/escf,edf->escd/dot_general | solution.py:134
  399.1 35.4 %reduce-scatter.8.cloned.1.call-done = bf16[2,32,14,512]{3,1,2,0:T(8,128)(2,1)} async-done(((bf16[2,32,14,2048]{3,1,2,0:T(8,128)(2,1)}), bf16[2,32,14,512]{3,1,2,0:T(8,128)(2,1)}) %reduce-scatter.8.cloned.1.call-update) | async-done | bytes 917520 | tf_op jit(solution)/shard_map/reduce_scatter | solution.py:140
  437.6 9.2 %all-to-all-start.3 = ((bf16[2,32,14,512]{3,0,2,1:T(2,128)(2,1)}), bf16[2,32,14,512]{3,0,2,1:T(2,128)(2,1)S(1)}, u32[]{:S(2)}, u32[]{:S(2)}) async-start(bf16[2,32,14,512]{3,0,2,1:T(2,128)(2,1)} %copy.65), calls=%async_computation.6 | async-start | bytes 1835008 | tf_op jit(solution)/shard_map/all_to_all | solution.py:19
  455.4 30.8 %all-to-all-done.3 = bf16[2,32,14,512]{3,0,2,1:T(2,128)(2,1)S(1)} async-done(((bf16[2,32,14,512]{3,0,2,1:T(2,128)(2,1)}), bf16[2,32,14,512]{3,0,2,1:T(2,128)(2,1)S(1)}, u32[]{:S(2)}, u32[]{:S(2)}) %all-to-all-start.3) | async-done | bytes 917536 | tf_op jit(solution)/shard_map/all_to_all | solution.py:19
  497.2 16.2 %all-reduce.2 = (f32[128]{0:T(128)S(1)}, f32[128,6]{1,0:T(8,128)S(1)}) all-reduce(f32[128]{0:T(128)S(1)} %multiply_reduce_fusion.2, f32[128,6]{1,0:T(8,128)S(1)} %multiply_reduce_fusion), channel_id=1, replica_groups=mesh['dp'=2,'expert'=32,'tensor'=4] {'tensor'}, use_global_device_ids=true, to_apply=%region_13.14 | all-reduce | flops 896 | bytes 7168 | tf_op jit(solution)/shard_map/psum | solution.py:149
  513.6 13.6 %all_gather.11 = bf16[128,2048]{1,0:T(8,128)(2,1)S(1)} all-gather(bf16[128,512]{1,0:T(8,128)(2,1)S(1)} %subtract_convert_fusion), channel_id=1, replica_groups=mesh['dp'=2,'expert'=32,'tensor'=4] {'tensor'}, dimensions={1}, use_global_device_ids=true | all-gather | bytes 655360 | tf_op jit(solution)/shard_map/all_gather | solution.py:157
  532.1 5.7 %add_convert_fusion.1 = bf16[2,2,1024,352]{2,3,0,1:T(8,128)(2,1)S(1)} fusion(bf16[2,2,1024,352]{2,3,0,1:T(8,128)(2,1)} %collective-permute-done.2, pred[]{:T(512)S(6)} %eq.38, bf16[2,2,2048,352]{2,3,0,1:T(8,128)(2,1)} %copy-done.1), kind=kLoop, calls=%fused_computation.10 | loop fusion | flops 7208960 | bytes 11534337 | tf_op jit(solution)/shard_map/convert_element_type | solution.py:44
  (119 shorter events, 93.2 us)
Async XLA Ops:
  7.2 3.8 copy-start.13
  7.2 30.7 %copy-start.8 = (bf16[128,2048]{1,0:T(8,128)(2,1)S(1)}, bf16[128,2048]{1,0:T(8,128)(2,1)}, u32[]{:S(2)}) copy-start(bf16[128,2048]{1,0:T(8,128)(2,1)} %param.10) | copy-start | bytes 1572868
  7.2 30.7 %reduce-scatter.4.cloned.1.call-start = ((), (), s32[]{:S(2)}) async-start(), calls=%async_computation.7 | async-start | bytes 655360 | tf_op jit(solution)/shard_map/reduce_scatter | solution.py:77
  10.9 158.0 %all-gather.3.cloned.1.call-start = ((), (), s32[]{:S(2)}) async-start(), calls=%async_computation.8 | async-start | bytes 4587520 | tf_op jit(solution)/shard_map/all_gather | solution.py:103
  87.9 150.5 %reduce-scatter.6.cloned.1.call-start = ((), (), s32[]{:S(2)}) async-start(), calls=%async_computation.9 | async-start | bytes 4587520 | tf_op jit(solution)/shard_map/reduce_scatter | solution.py:112
  91.6 68.8 %collective-permute-start = (bf16[2,2,1024,352]{2,3,0,1:T(8,128)(2,1)}, bf16[2,2,1024,352]{2,3,0,1:T(8,128)(2,1)}, u32[]{:S(2)}, u32[]{:S(2)}) collective-permute-start(bf16[2,2,1024,352]{2,3,0,1:T(8,128)(2,1)} %copy.58), channel_id=1, source_target_pairs={{0,128},{128,0},{1,129},{129,1},{2,130},{130,2},{3,131},{131,3},{4... | collective-permute-start | bytes 8650760 | tf_op jit(solution)/shard_map/ppermute | solution.py:26
  96.8 92.8 %collective-permute-start.1 = (bf16[2,352,1024]{2,1,0:T(8,128)(2,1)}, bf16[2,352,1024]{2,1,0:T(8,128)(2,1)}, u32[]{:S(2)}, u32[]{:S(2)}) collective-permute-start(bf16[2,352,1024]{2,1,0:T(8,128)(2,1)} %param.17), channel_id=1, source_target_pairs={{0,128},{128,0},{1,129},{129,1},{2,130},{130,2},{3,131},{131,3},{4... | collective-permute-start | bytes 4325384 | tf_op jit(solution)/shard_map/ppermute | solution.py:26
  168.9 5.1 copy-start.2
  168.9 5.7 %copy-start.15 = (bf16[2,32,14,2048]{3,1,2,0:T(8,128)(2,1)S(1)}, bf16[2,32,14,2048]{3,1,2,0:T(8,128)(2,1)}, u32[]{:S(2)}) copy-start(bf16[2,32,14,2048]{3,1,2,0:T(8,128)(2,1)} %all-gather.3.cloned.1.call-done) | copy-start | bytes 11010052
  177.8 11.8 %copy-start.18 = (bf16[2,32,14,352]{3,1,2,0:T(8,128)(2,1)}, bf16[2,32,14,352]{3,1,2,0:T(8,128)(2,1)S(1)}, u32[]{:S(2)}) copy-start(bf16[2,32,14,352]{3,1,2,0:T(8,128)(2,1)S(1)} %get-tuple-element.44) | copy-start | bytes 1892356
  196.5 54.1 %copy-start.14 = (f32[128,6]{0,1:T(8,128)S(1)}, f32[128,6]{0,1:T(8,128)}, u32[]{:S(2)}) copy-start(f32[128,6]{0,1:T(8,128)} %param.14) | copy-start | bytes 9220
  241.5 32.3 %all-to-all-start.1 = ((bf16[2,32,14,512]{3,0,2,1:T(2,128)(2,1)}), bf16[2,32,14,512]{3,0,2,1:T(2,128)(2,1)S(1)}, u32[]{:S(2)}, u32[]{:S(2)}) async-start(bf16[2,32,14,512]{3,0,2,1:T(2,128)(2,1)} %copy.60), calls=%async_computation.3 | async-start | bytes 1835008 | tf_op jit(solution)/shard_map/all_to_all | solution.py:19
  250.4 121.6 %all-gather.5.cloned.1.call-start = ((), (), s32[]{:S(2)}) async-start(), calls=%async_computation.10 | async-start | bytes 4587520 | tf_op jit(solution)/shard_map/all_gather | solution.py:127
  279.6 4.9 copy-start.6
  279.6 4.9 copy-start.12
  325.5 109.0 %reduce-scatter.8.cloned.1.call-start = ((), (), s32[]{:S(2)}) async-start(), calls=%async_computation.11 | async-start | bytes 4587520 | tf_op jit(solution)/shard_map/reduce_scatter | solution.py:140
  379.0 4.2 copy-start.10
  389.0 3.9 copy-start.11
  389.0 3.9 copy-start.16
  398.6 130.0 %collective-permute-start.2 = (bf16[2,2,1024,352]{2,3,0,1:T(8,128)(2,1)}, bf16[2,2,1024,352]{2,3,0,1:T(8,128)(2,1)}, u32[]{:S(2)}, u32[]{:S(2)}) collective-permute-start(bf16[2,2,1024,352]{2,3,0,1:T(8,128)(2,1)} %broadcast_select_fusion), channel_id=1, source_target_pairs={{0,128},{128,0},{1,129},{129,1},{2,130},{130,2},{3,131},{131,3},{4... | collective-permute-start | bytes 8650760 | tf_op jit(solution)/shard_map/ppermute | solution.py:39
  437.6 48.7 %all-to-all-start.3 = ((bf16[2,32,14,512]{3,0,2,1:T(2,128)(2,1)}), bf16[2,32,14,512]{3,0,2,1:T(2,128)(2,1)S(1)}, u32[]{:S(2)}, u32[]{:S(2)}) async-start(bf16[2,32,14,512]{3,0,2,1:T(2,128)(2,1)} %copy.65), calls=%async_computation.6 | async-start | bytes 1835008 | tf_op jit(solution)/shard_map/all_to_all | solution.py:19
  453.7 75.0 %collective-permute-start.3 = (bf16[2,352,1024]{2,1,0:T(8,128)(2,1)}, bf16[2,352,1024]{2,1,0:T(8,128)(2,1)}, u32[]{:S(2)}, u32[]{:S(2)}) collective-permute-start(bf16[2,352,1024]{2,1,0:T(8,128)(2,1)} %broadcast_select_fusion.1), channel_id=1, source_target_pairs={{0,128},{128,0},{1,129},{129,1},{2,130},{130,2},{3,131},{131,3},{4... | collective-permute-start | bytes 4325384 | tf_op jit(solution)/shard_map/ppermute | solution.py:39
  492.1 4.9 copy-start.9
  513.4 15.2 %copy-start.5 = (bf16[2,352,2048]{2,1,0:T(8,128)(2,1)S(1)}, bf16[2,352,2048]{2,1,0:T(8,128)(2,1)}, u32[]{:S(2)}) copy-start(bf16[2,352,2048]{2,1,0:T(8,128)(2,1)} %copy-done.4) | copy-start | bytes 8650756
  (6 other events, 15.1 us)
Sparse Core Ops, SparseCore 0:
  11.1 26.7 reduce-scatter.3
  88.0 45.4 all-gather.2
  196.7 41.7 reduce-scatter.5
  325.6 46.2 all-gather.4
  389.1 45.3 reduce-scatter.7

commit v4 on v3

--- a/solution.py
+++ b/solution.py
@@ -20,6 +20,49 @@
 
 
 DP_SWAP = [(0, 1), (1, 0)]
+
+
+def tensor_shift(value, shift, count):
+    return lax.ppermute(value, "tensor", [(j, (j + shift) % count) for j in range(count)])
+
+
+def by_source(received, count):
+    order = (lax.axis_index("tensor") - jnp.arange(count)) % count
+    return jnp.take(jnp.stack(received), order, axis=0)
+
+
+def tensor_pieces(value):
+    count = lax.axis_size("tensor")
+    received = [value] + [tensor_shift(value, shift, count) for shift in range(1, count)]
+    return by_source(received, count)
+
+
+def tensor_total(value):
+    pieces = tensor_pieces(value)
+    total = pieces[0]
+    for member in range(1, pieces.shape[0]):
+        total = total + pieces[member]
+    return total
+
+
+def tensor_joined(value):
+    pieces = tensor_pieces(value)
+    return jnp.concatenate([pieces[member] for member in range(pieces.shape[0])], axis=1)
+
+
+def tensor_scattered(value):
+    count = lax.axis_size("tensor")
+    width = value.shape[1] // count
+    me = lax.axis_index("tensor")
+    received = [lax.dynamic_slice_in_dim(value, me * width, width, 1)]
+    for shift in range(1, count):
+        sent = lax.dynamic_slice_in_dim(value, (me + shift) % count * width, width, 1)
+        received.append(tensor_shift(sent, shift, count))
+    pieces = by_source(received, count).astype(jnp.float32)
+    total = pieces[0]
+    for member in range(1, count):
+        total = total + pieces[member]
+    return total
 
 
 def dp_joined(own, dp_first, axis):
@@ -74,13 +117,11 @@
         dp_joined(w_down, dp_first, 2),
     )
     partial_attn = jnp.dot(context, wo_rows, preferred_element_type=jnp.float32)
-    attn_cols = lax.psum_scatter(
-        partial_attn.astype(jnp.bfloat16), "tensor", scatter_dimension=1, tiled=True
-    )
+    attn_cols = tensor_scattered(partial_attn.astype(jnp.bfloat16))
     hidden_cols = lax.dynamic_slice_in_dim(residual, col_start, col_count, 1).astype(
         jnp.float32
-    ) + attn_cols.astype(jnp.float32)
-    square_sum = lax.psum(jnp.sum(hidden_cols * hidden_cols, axis=1, keepdims=True), "tensor")
+    ) + attn_cols
+    square_sum = tensor_total(jnp.sum(hidden_cols * hidden_cols, axis=1, keepdims=True))
     inv_rms = lax.rsqrt(square_sum / feature_count + NORM_EPS)
     gain_cols = lax.dynamic_slice_in_dim(norm_gain, col_start, col_count, 0)
     normed = (gain_cols * hidden_cols * inv_rms).astype(jnp.bfloat16)
@@ -146,7 +187,8 @@
     )
     scaled = gain_cols * d_normed
     norm_partial = jnp.sum(scaled * hidden_cols, axis=1)
-    norm_dots, gate_prob_grad = lax.psum((norm_partial, gate_partial), "tensor")
+    dots_total = tensor_total(jnp.concatenate([norm_partial[:, None], gate_partial], axis=1))
+    norm_dots, gate_prob_grad = dots_total[:, 0], dots_total[:, 1:]
     cubed = inv_rms * inv_rms * inv_rms
     d_hidden = (
         error.astype(jnp.float32)
@@ -154,7 +196,7 @@
         - hidden_cols * cubed * norm_dots[:, None] / feature_count
     ).astype(jnp.bfloat16)
     context_grad = lax.dot_general(
-        lax.all_gather(d_hidden, "tensor", axis=1, tiled=True),
+        tensor_joined(d_hidden),
         wo_rows,
         (((1,), (1,)), ((), ())),
         preferred_element_type=jnp.float32,

time: 553 us -> 577 us (1.043)
  blocking collectives: 101 us -> 67.1 us
  waiting for transfers between devices: 268 us -> 299 us
  starting transfers between devices: 26.2 us -> 41.4 us
    ppermute x2, waiting for transfers between devices: 0.01 us -> 60.1 us  [dp_halves_sent(): arrived = lax.ppermute(jnp.where(dp_first, high, low), 'dp', DP_SWAP)]
    psum x2 -> x0, blocking collectives: 24.6 us -> none  [the longest x1 16.2 us: per_device(): norm_dots, gate_prob_grad = lax.psum((norm_partial, gate_partial), 'tensor')]
    reduce_scatter x1 -> x0, waiting for transfers between devices: 20 us -> none  [per_device(): lax.psum_scatter(partial_attn.astype(jnp.bfloat16), 'tensor', scatter_dim...]
    all_to_all x2, waiting for transfers between devices: 49.8 us -> 31.3 us  [to_tokens(): lax.all_to_all(outgoing, 'expert', split_axis=1, concat_axis=1, tiled=True)]
    ppermute x0 -> x12, starting transfers between devices: none -> 18.3 us  [tensor_shift(): lax.ppermute(value, 'tensor', [(j, (j + shift) % count) for j in range(co...]
    all_gather x1 -> x0, blocking collectives: 13.6 us -> none  [per_device(): lax.all_gather(d_hidden, 'tensor', axis=1, tiled=True)]
    ppermute x0 -> x12, waiting for transfers between devices: none -> 11.6 us  [tensor_shift(): lax.ppermute(value, 'tensor', [(j, (j + shift) % count) for j in range(co...]
  transfers between devices with their start and end apart: 11 -> 22, of which waited for: 8 -> 16; matrix products, arithmetic and copies ran while one was open for 11% -> 11% of each run, Pallas kernels for 0% -> 0%
where the time goes in v4:
time: 577 us; the launch traced here: 567 us
  waiting for transfers between devices  299 us (52%)
  blocking collectives  67.1 us (12%)
  local copies, waits for them, and re-layouts  63.2 us (11%)
  matrix products  42.6 us (7%)
  starting transfers between devices  41.4 us (7%)
  other arithmetic  39 us (7%)
  between operations  14.6 us (3%)
    ppermute x2, waiting for transfers between devices, dp_joined(): other = lax.ppermute(own, 'dp', DP_SWAP)  75.7 us
    all_to_all x2, blocking collectives, to_experts(): lax.all_to_all(outgoing, 'expert', split_axis=1, concat_axis=1, tiled=True)  67.1 us
    ppermute x2, waiting for transfers between devices, dp_halves_sent(): arrived = lax.ppermute(jnp.where(dp_first, high, low), 'dp', DP_SWAP)  60.1 us
    all_gather x1, waiting for transfers between devices, per_device(): lax.all_gather(to_experts(grad_slot), 'tensor', axis=3, tiled=True)  46.2 us
    reduce_scatter x1, waiting for transfers between devices, per_device(): lax.psum_scatter(partial_out.astype(jnp.bfloat16), 'tensor', scatter_dime...  39.4 us
    reduce_scatter x1, waiting for transfers between devices, per_device(): lax.psum_scatter(d_entry_part.astype(jnp.bfloat16), 'tensor', scatter_dim...  34.7 us
    all_to_all x2, waiting for transfers between devices, to_tokens(): lax.all_to_all(outgoing, 'expert', split_axis=1, concat_axis=1, tiled=True)  31.3 us
    ppermute x12, starting transfers between devices, tensor_shift(): lax.ppermute(value, 'tensor', [(j, (j + shift) % count) for j in range(co...  18.3 us
  transfers between devices with their start and end apart: 22, of which 16 were waited for; matrix products, arithmetic and copies ran while one was open for 11% of the time, Pallas kernels for 0%

profile of v4, /device:TPU:32, one launch (start us, length us, event | category | flops | bytes accessed | tf_op | source)
XLA Modules:
  0.0 566.8 jit_solution(11504425598200140937)
XLA Ops:
  32.9 4.0 gather_fusion.1
  41.3 36.8 %all_to_all.20 = bf16[2,32,14,512]{3,0,2,1:T(2,128)(2,1)S(1)} all-to-all(bf16[2,32,14,512]{3,0,2,1:T(2,128)(2,1)S(1)} %copy.72), channel_id=1, replica_groups=mesh['dp'=2,'expert'=32,'tensor'=4] {'expert'}, dimensions={1} | all-to-all | bytes 1835008 | tf_op jit(solution)/shard_map/all_to_all | solution.py:15
  85.4 63.2 %collective-permute-done.6 = bf16[2,2,1024,352]{2,3,0,1:T(8,128)(2,1)} collective-permute-done((bf16[2,2,1024,352]{2,3,0,1:T(8,128)(2,1)}, bf16[2,2,1024,352]{2,3,0,1:T(8,128)(2,1)}, u32[]{:S(2)}, u32[]{:S(2)}) %collective-permute-start.6) | collective-permute-done | bytes 2883616 | tf_op jit(solution)/shard_map/ppermute | solution.py:69
  148.6 8.7 %maximum_select_fusion = bf16[2,2,2048,352]{2,3,0,1:T(8,128)(2,1)} fusion(bf16[2,2,1024,352]{2,3,0,1:T(8,128)(2,1)} %collective-permute-done.6, pred[]{:T(512)S(6)} %eq.47, bf16[2,2,1024,352]{2,3,1,0:T(8,128)(2,1)} %param.18), kind=kLoop, calls=%fused_computation.12 | loop fusion | flops 25952256 | bytes 11534337 | tf_op jit(solution)/shard_map/jit(_where)/select_n | solution.py:70
  157.3 5.1 fusion.1
  166.2 12.5 %collective-permute-done.7 = bf16[2,352,1024]{2,1,0:T(8,128)(2,1)} collective-permute-done((bf16[2,352,1024]{2,1,0:T(8,128)(2,1)}, bf16[2,352,1024]{2,1,0:T(8,128)(2,1)}, u32[]{:S(2)}, u32[]{:S(2)}) %collective-permute-start.7) | collective-permute-done | bytes 1441824 | tf_op jit(solution)/shard_map/ppermute | solution.py:69
  178.7 6.9 %convolution_convert_fusion = bf16[2,32,14,2048]{3,1,2,0:T(8,128)(2,1)} fusion(bf16[2,32,14,352]{3,1,2,0:T(8,128)(2,1)S(1)} %get-tuple-element.53, bf16[2,352,1024]{2,1,0:T(8,128)(2,1)} %collective-permute-done.7, bf16[2,352,1024]{2,1,0:T(8,128)(2,1)} %param.19, pred[]{:T(512)S(6)} %eq.47), kind=kOutput, calls=%fused_computation.17 | convolution fusion | flops 1306656768 | bytes 7184385 | tf_op jit(solution)/shard_map/escf,efd->escd/dot_general | solution.py:150
  185.6 39.4 %reduce-scatter.3.cloned.1.call-done = bf16[2,32,14,512]{3,1,2,0:T(8,128)(2,1)} async-done(((bf16[2,32,14,2048]{3,1,2,0:T(8,128)(2,1)}), bf16[2,32,14,512]{3,1,2,0:T(8,128)(2,1)}) %reduce-scatter.3.cloned.1.call-update) | async-done | bytes 917520 | tf_op jit(solution)/shard_map/reduce_scatter | solution.py:153
  228.0 9.1 %all-to-all-start.1 = ((bf16[2,32,14,512]{3,0,2,1:T(2,128)(2,1)}), bf16[2,32,14,512]{3,0,2,1:T(2,128)(2,1)}, u32[]{:S(2)}, u32[]{:S(2)}) async-start(bf16[2,32,14,512]{3,0,2,1:T(2,128)(2,1)} %copy.77), calls=%async_computation.2 | async-start | bytes 1835008 | tf_op jit(solution)/shard_map/all_to_all | solution.py:19
  241.3 19.2 %all-to-all-done.1 = bf16[2,32,14,512]{3,0,2,1:T(2,128)(2,1)} async-done(((bf16[2,32,14,512]{3,0,2,1:T(2,128)(2,1)}), bf16[2,32,14,512]{3,0,2,1:T(2,128)(2,1)}, u32[]{:S(2)}, u32[]{:S(2)}) %all-to-all-start.1) | async-done | bytes 917536 | tf_op jit(solution)/shard_map/all_to_all | solution.py:19
  273.1 4.0 gather_fusion.4
  282.3 30.2 %all_to_all.21 = bf16[2,32,14,512]{3,0,2,1:T(2,128)(2,1)S(1)} all-to-all(bf16[2,32,14,512]{3,0,2,1:T(2,128)(2,1)S(1)} %copy.80), channel_id=1, replica_groups=mesh['dp'=2,'expert'=32,'tensor'=4] {'expert'}, dimensions={1} | all-to-all | bytes 1835008 | tf_op jit(solution)/shard_map/all_to_all | solution.py:15
  313.9 46.2 %all-gather.5.cloned.1.call-done = bf16[2,32,14,2048]{3,1,2,0:T(8,128)(2,1)} async-done(((bf16[2,32,14,512]{3,1,2,0:T(8,128)(2,1)}), bf16[2,32,14,2048]{3,1,2,0:T(8,128)(2,1)}) %all-gather.5.cloned.1.call-update) | async-done | bytes 3670032 | tf_op jit(solution)/shard_map/all_gather | solution.py:168
  360.2 6.9 %multiply_convert_fusion.2 = (bf16[2,32,14,352]{3,1,2,0:T(8,128)(2,1)S(1)}, bf16[2,32,14,352]{3,1,2,0:T(8,128)(2,1)S(1)}) fusion(f32[2,32,14,352]{3,1,2,0:T(8,128)} %copy-done.12, f32[2,32,14,352]{3,1,2,0:T(8,128)} %get-tuple-element.54, bf16[2,32,14,2048]{3,1,2,0:T(8,128)(2,1)} %all-gather.5.cloned.1.call-done, ...), kind=kOutput, calls=%fused_computation.34 | convolution fusion | flops 1308921856 | bytes 10338305 | tf_op jit(solution)/shard_map/escd,efd->escf/dot_general | solution.py:169
  367.1 4.4 fusion.2
  371.5 5.7 %add_convert_fusion = bf16[2,32,14,2048]{3,1,2,0:T(8,128)(2,1)} fusion(f32[2,32,14,2048]{3,1,2,0:T(8,128)S(1)} %fusion.2, bf16[2,32,14,352]{3,1,2,0:T(8,128)(2,1)S(1)} %get-tuple-element.41, bf16[2,2,2048,352]{2,3,0,1:T(8,128)(2,1)} %maximum_select_fusion), kind=kOutput, calls=%fused_computation.11 | convolution fusion | flops 1295515648 | bytes 14524416 | tf_op jit(solution)/shard_map/escf,edf->escd/dot_general | solution.py:175
  379.3 4.1 convolution_bitcast_fusion.1
  388.1 34.7 %reduce-scatter.5.cloned.1.call-done = bf16[2,32,14,512]{3,1,2,0:T(8,128)(2,1)} async-done(((bf16[2,32,14,2048]{3,1,2,0:T(8,128)(2,1)}), bf16[2,32,14,512]{3,1,2,0:T(8,128)(2,1)}) %reduce-scatter.5.cloned.1.call-update) | async-done | bytes 917520 | tf_op jit(solution)/shard_map/reduce_scatter | solution.py:181
  425.8 8.9 %all-to-all-start.3 = ((bf16[2,32,14,512]{3,0,2,1:T(2,128)(2,1)}), bf16[2,32,14,512]{3,0,2,1:T(2,128)(2,1)S(1)}, u32[]{:S(2)}, u32[]{:S(2)}) async-start(bf16[2,32,14,512]{3,0,2,1:T(2,128)(2,1)} %copy.82), calls=%async_computation.5 | async-start | bytes 1835008 | tf_op jit(solution)/shard_map/all_to_all | solution.py:19
  434.8 4.7 broadcast_select_fusion
  446.3 12.0 %all-to-all-done.3 = bf16[2,32,14,512]{3,0,2,1:T(2,128)(2,1)S(1)} async-done(((bf16[2,32,14,512]{3,0,2,1:T(2,128)(2,1)}), bf16[2,32,14,512]{3,0,2,1:T(2,128)(2,1)S(1)}, u32[]{:S(2)}, u32[]{:S(2)}) %all-to-all-start.3) | async-done | bytes 917536 | tf_op jit(solution)/shard_map/all_to_all | solution.py:19
  482.6 4.5 collective-permute-done.14
  489.9 60.1 %collective-permute-done.9 = bf16[2,352,1024]{2,1,0:T(8,128)(2,1)} collective-permute-done((bf16[2,352,1024]{2,1,0:T(8,128)(2,1)}, bf16[2,352,1024]{2,1,0:T(8,128)(2,1)}, u32[]{:S(2)}, u32[]{:S(2)}) %collective-permute-start.9) | collective-permute-done | bytes 1441824 | tf_op jit(solution)/shard_map/ppermute | solution.py:82
  549.9 4.3 add_convert_fusion.2
  (157 shorter events, 116.5 us)
Async XLA Ops:
  7.2 150.1 %all-gather.3.cloned.1.call-start = ((), (), s32[]{:S(2)}) async-start(), calls=%async_computation.6 | async-start | bytes 4587520 | tf_op jit(solution)/shard_map/all_gather | solution.py:144
  10.2 12.0 %collective-permute-start = (bf16[128,512]{1,0:T(8,128)(2,1)S(1)}, bf16[128,512]{1,0:T(8,128)(2,1)S(1)}, u32[]{:S(2)}, u32[]{:S(2)}) collective-permute-start(bf16[128,512]{1,0:T(8,128)(2,1)S(1)} %get-tuple-element.50), channel_id=1, source_target_pairs={{0,1},{1,2},{2,3},{3,0},{4,5},{5,6},{6,7},{7,4},{8,9},{9,10},{10,1... | collective-permute-start | bytes 393224 | tf_op jit(solution)/shard_map/ppermute | solution.py:26
  11.7 10.4 %collective-permute-start.1 = (bf16[128,512]{1,0:T(8,128)(2,1)S(1)}, bf16[128,512]{1,0:T(8,128)(2,1)S(1)}, u32[]{:S(2)}, u32[]{:S(2)}) collective-permute-start(bf16[128,512]{1,0:T(8,128)(2,1)S(1)} %get-tuple-element.49), channel_id=1, source_target_pairs={{0,2},{1,3},{2,0},{3,1},{4,6},{5,7},{6,4},{7,5},{8,10},{9,11},{10,... | collective-permute-start | bytes 393224 | tf_op jit(solution)/shard_map/ppermute | solution.py:26
  14.5 7.7 %collective-permute-start.2 = (bf16[128,512]{1,0:T(8,128)(2,1)S(1)}, bf16[128,512]{1,0:T(8,128)(2,1)S(1)}, u32[]{:S(2)}, u32[]{:S(2)}) collective-permute-start(bf16[128,512]{1,0:T(8,128)(2,1)S(1)} %get-tuple-element.48), channel_id=1, source_target_pairs={{0,3},{1,0},{2,1},{3,2},{4,7},{5,4},{6,5},{7,6},{8,11},{9,8},{10,9... | collective-permute-start | bytes 393224 | tf_op jit(solution)/shard_map/ppermute | solution.py:26
  24.0 5.2 collective-permute-start.4
  25.1 4.1 collective-permute-start.5
  27.4 4.8 collective-permute-start.3
  79.2 145.8 %reduce-scatter.3.cloned.1.call-start = ((), (), s32[]{:S(2)}) async-start(), calls=%async_computation.7 | async-start | bytes 4587520 | tf_op jit(solution)/shard_map/reduce_scatter | solution.py:153
  82.9 65.7 %collective-permute-start.6 = (bf16[2,2,1024,352]{2,3,0,1:T(8,128)(2,1)}, bf16[2,2,1024,352]{2,3,0,1:T(8,128)(2,1)}, u32[]{:S(2)}, u32[]{:S(2)}) collective-permute-start(bf16[2,2,1024,352]{2,3,0,1:T(8,128)(2,1)} %copy.75), channel_id=1, source_target_pairs={{0,128},{128,0},{1,129},{129,1},{2,130},{130,2},{3,131},{131,3},{4... | collective-permute-start | bytes 8650760 | tf_op jit(solution)/shard_map/ppermute | solution.py:69
  84.0 94.7 %collective-permute-start.7 = (bf16[2,352,1024]{2,1,0:T(8,128)(2,1)}, bf16[2,352,1024]{2,1,0:T(8,128)(2,1)}, u32[]{:S(2)}, u32[]{:S(2)}) collective-permute-start(bf16[2,352,1024]{2,1,0:T(8,128)(2,1)} %param.19), channel_id=1, source_target_pairs={{0,128},{128,0},{1,129},{129,1},{2,130},{130,2},{3,131},{131,3},{4... | collective-permute-start | bytes 4325384 | tf_op jit(solution)/shard_map/ppermute | solution.py:69
  228.0 32.4 %all-to-all-start.1 = ((bf16[2,32,14,512]{3,0,2,1:T(2,128)(2,1)}), bf16[2,32,14,512]{3,0,2,1:T(2,128)(2,1)}, u32[]{:S(2)}, u32[]{:S(2)}) async-start(bf16[2,32,14,512]{3,0,2,1:T(2,128)(2,1)} %copy.77), calls=%async_computation.2 | async-start | bytes 1835008 | tf_op jit(solution)/shard_map/all_to_all | solution.py:19
  237.1 123.0 %all-gather.5.cloned.1.call-start = ((), (), s32[]{:S(2)}) async-start(), calls=%async_computation.8 | async-start | bytes 4587520 | tf_op jit(solution)/shard_map/all_gather | solution.py:168
  313.7 109.1 %reduce-scatter.5.cloned.1.call-start = ((), (), s32[]{:S(2)}) async-start(), calls=%async_computation.9 | async-start | bytes 4587520 | tf_op jit(solution)/shard_map/reduce_scatter | solution.py:181
  425.8 32.6 %all-to-all-start.3 = ((bf16[2,32,14,512]{3,0,2,1:T(2,128)(2,1)}), bf16[2,32,14,512]{3,0,2,1:T(2,128)(2,1)S(1)}, u32[]{:S(2)}, u32[]{:S(2)}) async-start(bf16[2,32,14,512]{3,0,2,1:T(2,128)(2,1)} %copy.82), calls=%async_computation.5 | async-start | bytes 1835008 | tf_op jit(solution)/shard_map/all_to_all | solution.py:19
  439.5 110.4 %collective-permute-start.8 = (bf16[2,2,1024,352]{2,3,0,1:T(8,128)(2,1)}, bf16[2,2,1024,352]{2,3,0,1:T(8,128)(2,1)}, u32[]{:S(2)}, u32[]{:S(2)}) collective-permute-start(bf16[2,2,1024,352]{2,3,0,1:T(8,128)(2,1)} %broadcast_select_fusion), channel_id=1, source_target_pairs={{0,128},{128,0},{1,129},{129,1},{2,130},{130,2},{3,131},{131,3},{4... | collective-permute-start | bytes 8650760 | tf_op jit(solution)/shard_map/ppermute | solution.py:82
  445.7 104.3 %collective-permute-start.9 = (bf16[2,352,1024]{2,1,0:T(8,128)(2,1)}, bf16[2,352,1024]{2,1,0:T(8,128)(2,1)}, u32[]{:S(2)}, u32[]{:S(2)}) collective-permute-start(bf16[2,352,1024]{2,1,0:T(8,128)(2,1)} %broadcast_select_fusion.1), channel_id=1, source_target_pairs={{0,128},{128,0},{1,129},{129,1},{2,130},{130,2},{3,131},{131,3},{4... | collective-permute-start | bytes 4325384 | tf_op jit(solution)/shard_map/ppermute | solution.py:82
  469.3 4.9 collective-permute-start.10
  469.6 5.1 collective-permute-start.11
  472.0 3.6 collective-permute-start.12
  476.4 6.3 %collective-permute-start.13 = (bf16[128,512]{1,0:T(8,128)(2,1)S(1)}, bf16[128,512]{1,0:T(8,128)(2,1)S(1)}, u32[]{:S(2)}, u32[]{:S(2)}) collective-permute-start(bf16[128,512]{1,0:T(8,128)(2,1)S(1)} %subtract_convert_fusion), channel_id=1, source_target_pairs={{0,1},{1,2},{2,3},{3,0},{4,5},{5,6},{6,7},{7,4},{8,9},{9,10},{10,1... | collective-permute-start | bytes 393224 | tf_op jit(solution)/shard_map/ppermute | solution.py:26
  477.9 9.2 %collective-permute-start.14 = (bf16[128,512]{1,0:T(8,128)(2,1)S(1)}, bf16[128,512]{1,0:T(8,128)(2,1)S(1)}, u32[]{:S(2)}, u32[]{:S(2)}) collective-permute-start(bf16[128,512]{1,0:T(8,128)(2,1)S(1)} %subtract_convert_fusion), channel_id=1, source_target_pairs={{0,2},{1,3},{2,0},{3,1},{4,6},{5,7},{6,4},{7,5},{8,10},{9,11},{10,... | collective-permute-start | bytes 393224 | tf_op jit(solution)/shard_map/ppermute | solution.py:26
  480.9 6.6 %collective-permute-start.15 = (bf16[128,512]{1,0:T(8,128)(2,1)S(1)}, bf16[128,512]{1,0:T(8,128)(2,1)S(1)}, u32[]{:S(2)}, u32[]{:S(2)}) collective-permute-start(bf16[128,512]{1,0:T(8,128)(2,1)S(1)} %subtract_convert_fusion), channel_id=1, source_target_pairs={{0,3},{1,0},{2,1},{3,2},{4,7},{5,4},{6,5},{7,6},{8,11},{9,8},{10,9... | collective-permute-start | bytes 393224 | tf_op jit(solution)/shard_map/ppermute | solution.py:26
  488.2 66.0 %slice-start = ((s8[5767168]{0:T(1024)(128)(4,1)}), s8[4194304]{0:T(1024)(128)(4,1)S(1)}, s32[]{:S(2)}) async-start(s8[5767168]{0:T(1024)(128)(4,1)} %bitcast.124), calls=%async_computation.10 | async-start | bytes 8388608
  488.3 65.9 %slice-start.1 = ((s8[5767168]{0:T(1024)(128)(4,1)}), s8[1572864]{0:T(1024)(128)(4,1)S(1)}, s32[]{:S(2)}) async-start(s8[5767168]{0:T(1024)(128)(4,1)} %bitcast.124), calls=%async_computation.11 | async-start | bytes 3145728
  (15 other events, 124.5 us)
Sparse Core Ops, SparseCore 0:
  79.3 40.7 all-gather.2
  185.8 39.1 reduce-scatter.2
  313.8 46.2 all-gather.4
  377.3 45.3 reduce-scatter.4

commit v5 on v4

--- a/solution.py
+++ b/solution.py
@@ -43,11 +43,6 @@
     for member in range(1, pieces.shape[0]):
         total = total + pieces[member]
     return total
-
-
-def tensor_joined(value):
-    pieces = tensor_pieces(value)
-    return jnp.concatenate([pieces[member] for member in range(pieces.shape[0])], axis=1)
 
 
 def tensor_scattered(value):
@@ -187,8 +182,7 @@
     )
     scaled = gain_cols * d_normed
     norm_partial = jnp.sum(scaled * hidden_cols, axis=1)
-    dots_total = tensor_total(jnp.concatenate([norm_partial[:, None], gate_partial], axis=1))
-    norm_dots, gate_prob_grad = dots_total[:, 0], dots_total[:, 1:]
+    norm_dots, gate_prob_grad = lax.psum((norm_partial, gate_partial), "tensor")
     cubed = inv_rms * inv_rms * inv_rms
     d_hidden = (
         error.astype(jnp.float32)
@@ -196,7 +190,7 @@
         - hidden_cols * cubed * norm_dots[:, None] / feature_count
     ).astype(jnp.bfloat16)
     context_grad = lax.dot_general(
-        tensor_joined(d_hidden),
+        lax.all_gather(d_hidden, "tensor", axis=1, tiled=True),
         wo_rows,
         (((1,), (1,)), ((), ())),
         preferred_element_type=jnp.float32,

time: 577 us -> 544 us (0.943)
  waiting for transfers between devices: 299 us -> 250 us
  blocking collectives: 67.1 us -> 97 us
  starting transfers between devices: 41.4 us -> 32.1 us
  other arithmetic: 39 us -> 32.9 us
    ppermute x2, waiting for transfers between devices: 60.1 us -> 0.01 us  [dp_halves_sent(): arrived = lax.ppermute(jnp.where(dp_first, high, low), 'dp', DP_SWAP)]
    all_to_all x2, waiting for transfers between devices: 31.3 us -> 49.9 us  [to_tokens(): lax.all_to_all(outgoing, 'expert', split_axis=1, concat_axis=1, tiled=True)]
    psum x0 -> x1, blocking collectives: none -> 16.3 us  [per_device(): norm_dots, gate_prob_grad = lax.psum((norm_partial, gate_partial), 'tensor')]
    all_gather x0 -> x1, blocking collectives: none -> 13.6 us  [per_device(): lax.all_gather(d_hidden, 'tensor', axis=1, tiled=True)]
    ppermute x12 -> x6, waiting for transfers between devices: 11.6 us -> 1.26 us  [tensor_shift(): lax.ppermute(value, 'tensor', [(j, (j + shift) % count) for j in range(co...]
    ppermute x12 -> x6, starting transfers between devices: 18.3 us -> 9.45 us  [tensor_shift(): lax.ppermute(value, 'tensor', [(j, (j + shift) % count) for j in range(co...]
  transfers between devices with their start and end apart: 22 -> 16, of which waited for: 16 -> 9; matrix products, arithmetic and copies ran while one was open for 11% -> 11% of each run, Pallas kernels for 0% -> 0%
where the time goes in v5:
time: 544 us; the launch traced here: 535 us
  waiting for transfers between devices  250 us (46%)
  blocking collectives  97 us (18%)
  local copies, waits for them, and re-layouts  63.4 us (12%)
  matrix products  44.7 us (8%)
  other arithmetic  32.9 us (6%)
  starting transfers between devices  32.1 us (6%)
  between operations  14.7 us (3%)
    ppermute x2, waiting for transfers between devices, dp_joined(): other = lax.ppermute(own, 'dp', DP_SWAP)  76.2 us
    all_to_all x2, blocking collectives, to_experts(): lax.all_to_all(outgoing, 'expert', split_axis=1, concat_axis=1, tiled=True)  67.2 us
    all_to_all x2, waiting for transfers between devices, to_tokens(): lax.all_to_all(outgoing, 'expert', split_axis=1, concat_axis=1, tiled=True)  49.9 us
    all_gather x1, waiting for transfers between devices, per_device(): lax.all_gather(to_experts(grad_slot), 'tensor', axis=3, tiled=True)  46.2 us
    reduce_scatter x1, waiting for transfers between devices, per_device(): lax.psum_scatter(partial_out.astype(jnp.bfloat16), 'tensor', scatter_dime...  41.3 us
    reduce_scatter x1, waiting for transfers between devices, per_device(): lax.psum_scatter(d_entry_part.astype(jnp.bfloat16), 'tensor', scatter_dim...  35.4 us
    all_to_all x2, starting transfers between devices, to_tokens(): lax.all_to_all(outgoing, 'expert', split_axis=1, concat_axis=1, tiled=True)  18.2 us
    psum x1, blocking collectives, per_device(): norm_dots, gate_prob_grad = lax.psum((norm_partial, gate_partial), 'tensor')  16.3 us
  transfers between devices with their start and end apart: 16, of which 9 were waited for; matrix products, arithmetic and copies ran while one was open for 11% of the time, Pallas kernels for 0%

profile of v5, /device:TPU:32, one launch (start us, length us, event | category | flops | bytes accessed | tf_op | source)
XLA Modules:
  0.0 535.2 jit_solution(11647149795722473198)
XLA Ops:
  30.5 4.0 gather_fusion.2
  38.8 36.9 %all_to_all.20 = bf16[2,32,14,512]{3,0,2,1:T(2,128)(2,1)S(1)} all-to-all(bf16[2,32,14,512]{3,0,2,1:T(2,128)(2,1)S(1)} %copy.71), channel_id=1, replica_groups=mesh['dp'=2,'expert'=32,'tensor'=4] {'expert'}, dimensions={1} | all-to-all | bytes 1835008 | tf_op jit(solution)/shard_map/all_to_all | solution.py:15
  82.8 63.5 %collective-permute-done.6 = bf16[2,2,1024,352]{2,3,0,1:T(8,128)(2,1)} collective-permute-done((bf16[2,2,1024,352]{2,3,0,1:T(8,128)(2,1)}, bf16[2,2,1024,352]{2,3,0,1:T(8,128)(2,1)}, u32[]{:S(2)}, u32[]{:S(2)}) %collective-permute-start.6) | collective-permute-done | bytes 2883616 | tf_op jit(solution)/shard_map/ppermute | solution.py:64
  146.2 8.5 %maximum_select_fusion = bf16[2,2,2048,352]{2,3,0,1:T(8,128)(2,1)} fusion(bf16[2,2,1024,352]{2,3,0,1:T(8,128)(2,1)} %collective-permute-done.6, pred[]{:T(512)S(6)} %eq.45, bf16[2,2,1024,352]{2,3,1,0:T(8,128)(2,1)} %param.16), kind=kLoop, calls=%fused_computation.10 | loop fusion | flops 25952256 | bytes 11534337 | tf_op jit(solution)/shard_map/jit(_where)/select_n | solution.py:65
  154.8 5.1 fusion.1
  163.6 12.7 %collective-permute-done.7 = bf16[2,352,1024]{2,1,0:T(8,128)(2,1)} collective-permute-done((bf16[2,352,1024]{2,1,0:T(8,128)(2,1)}, bf16[2,352,1024]{2,1,0:T(8,128)(2,1)}, u32[]{:S(2)}, u32[]{:S(2)}) %collective-permute-start.7) | collective-permute-done | bytes 1441824 | tf_op jit(solution)/shard_map/ppermute | solution.py:64
  176.3 7.0 %convolution_convert_fusion = bf16[2,32,14,2048]{3,1,2,0:T(8,128)(2,1)} fusion(bf16[2,32,14,352]{3,1,2,0:T(8,128)(2,1)S(1)} %get-tuple-element.50, bf16[2,352,1024]{2,1,0:T(8,128)(2,1)} %collective-permute-done.7, bf16[2,352,1024]{2,1,0:T(8,128)(2,1)} %param.17, pred[]{:T(512)S(6)} %eq.45), kind=kOutput, calls=%fused_computation.15 | convolution fusion | flops 1306656768 | bytes 7184385 | tf_op jit(solution)/shard_map/escf,efd->escd/dot_general | solution.py:145
  183.4 41.3 %reduce-scatter.3.cloned.1.call-done = bf16[2,32,14,512]{3,1,2,0:T(8,128)(2,1)} async-done(((bf16[2,32,14,2048]{3,1,2,0:T(8,128)(2,1)}), bf16[2,32,14,512]{3,1,2,0:T(8,128)(2,1)}) %reduce-scatter.3.cloned.1.call-update) | async-done | bytes 917520 | tf_op jit(solution)/shard_map/reduce_scatter | solution.py:148
  227.7 9.0 %all-to-all-start.1 = ((bf16[2,32,14,512]{3,0,2,1:T(2,128)(2,1)}), bf16[2,32,14,512]{3,0,2,1:T(2,128)(2,1)}, u32[]{:S(2)}, u32[]{:S(2)}) async-start(bf16[2,32,14,512]{3,0,2,1:T(2,128)(2,1)} %copy.76), calls=%async_computation.2 | async-start | bytes 1835008 | tf_op jit(solution)/shard_map/all_to_all | solution.py:19
  240.9 19.2 %all-to-all-done.1 = bf16[2,32,14,512]{3,0,2,1:T(2,128)(2,1)} async-done(((bf16[2,32,14,512]{3,0,2,1:T(2,128)(2,1)}), bf16[2,32,14,512]{3,0,2,1:T(2,128)(2,1)}, u32[]{:S(2)}, u32[]{:S(2)}) %all-to-all-start.1) | async-done | bytes 917536 | tf_op jit(solution)/shard_map/all_to_all | solution.py:19
  272.8 4.0 gather_fusion.5
  282.0 30.3 %all_to_all.21 = bf16[2,32,14,512]{3,0,2,1:T(2,128)(2,1)S(1)} all-to-all(bf16[2,32,14,512]{3,0,2,1:T(2,128)(2,1)S(1)} %copy.79), channel_id=1, replica_groups=mesh['dp'=2,'expert'=32,'tensor'=4] {'expert'}, dimensions={1} | all-to-all | bytes 1835008 | tf_op jit(solution)/shard_map/all_to_all | solution.py:15
  313.7 46.2 %all-gather.5.cloned.1.call-done = bf16[2,32,14,2048]{3,1,2,0:T(8,128)(2,1)} async-done(((bf16[2,32,14,512]{3,1,2,0:T(8,128)(2,1)}), bf16[2,32,14,2048]{3,1,2,0:T(8,128)(2,1)}) %all-gather.5.cloned.1.call-update) | async-done | bytes 3670032 | tf_op jit(solution)/shard_map/all_gather | solution.py:163
  359.9 7.0 %multiply_convert_fusion.2 = (bf16[2,32,14,352]{3,1,2,0:T(8,128)(2,1)S(1)}, bf16[2,32,14,352]{3,1,2,0:T(8,128)(2,1)S(1)}) fusion(f32[2,32,14,352]{3,1,2,0:T(8,128)} %copy-done.14, f32[2,32,14,352]{3,1,2,0:T(8,128)} %get-tuple-element.51, bf16[2,32,14,2048]{3,1,2,0:T(8,128)(2,1)} %all-gather.5.cloned.1.call-done, ...), kind=kOutput, calls=%fused_computation.32 | convolution fusion | flops 1308921856 | bytes 10338305 | tf_op jit(solution)/shard_map/escd,efd->escf/dot_general | solution.py:164
  367.0 4.2 fusion.2
  371.1 5.7 %add_convert_fusion = bf16[2,32,14,2048]{3,1,2,0:T(8,128)(2,1)} fusion(f32[2,32,14,2048]{3,1,2,0:T(8,128)S(1)} %fusion.2, bf16[2,32,14,352]{3,1,2,0:T(8,128)(2,1)S(1)} %get-tuple-element.42, bf16[2,2,2048,352]{2,3,0,1:T(8,128)(2,1)} %maximum_select_fusion), kind=kOutput, calls=%fused_computation.9 | convolution fusion | flops 1295515648 | bytes 14524416 | tf_op jit(solution)/shard_map/escf,edf->escd/dot_general | solution.py:170
  376.9 3.9 convolution_bitcast_fusion.1
  387.0 35.4 %reduce-scatter.5.cloned.1.call-done = bf16[2,32,14,512]{3,1,2,0:T(8,128)(2,1)} async-done(((bf16[2,32,14,2048]{3,1,2,0:T(8,128)(2,1)}), bf16[2,32,14,512]{3,1,2,0:T(8,128)(2,1)}) %reduce-scatter.5.cloned.1.call-update) | async-done | bytes 917520 | tf_op jit(solution)/shard_map/reduce_scatter | solution.py:176
  425.5 9.2 %all-to-all-start.3 = ((bf16[2,32,14,512]{3,0,2,1:T(2,128)(2,1)}), bf16[2,32,14,512]{3,0,2,1:T(2,128)(2,1)S(1)}, u32[]{:S(2)}, u32[]{:S(2)}) async-start(bf16[2,32,14,512]{3,0,2,1:T(2,128)(2,1)} %copy.81), calls=%async_computation.5 | async-start | bytes 1835008 | tf_op jit(solution)/shard_map/all_to_all | solution.py:19
  434.7 4.0 bitcast_convert_fusion
  443.3 30.8 %all-to-all-done.3 = bf16[2,32,14,512]{3,0,2,1:T(2,128)(2,1)S(1)} async-done(((bf16[2,32,14,512]{3,0,2,1:T(2,128)(2,1)}), bf16[2,32,14,512]{3,0,2,1:T(2,128)(2,1)S(1)}, u32[]{:S(2)}, u32[]{:S(2)}) %all-to-all-start.3) | async-done | bytes 917536 | tf_op jit(solution)/shard_map/all_to_all | solution.py:19
  485.0 16.3 %all-reduce.2 = (f32[128]{0:T(128)S(1)}, f32[128,6]{1,0:T(8,128)S(1)}) all-reduce(f32[128]{0:T(128)S(1)} %multiply_reduce_fusion.2, f32[128,6]{1,0:T(8,128)S(1)} %multiply_reduce_fusion), channel_id=1, replica_groups=mesh['dp'=2,'expert'=32,'tensor'=4] {'tensor'}, use_global_device_ids=true, to_apply=%region_11.12 | all-reduce | flops 896 | bytes 7168 | tf_op jit(solution)/shard_map/psum | solution.py:185
  501.4 13.6 %all_gather.11 = bf16[128,2048]{1,0:T(8,128)(2,1)S(1)} all-gather(bf16[128,512]{1,0:T(8,128)(2,1)S(1)} %subtract_convert_fusion), channel_id=1, replica_groups=mesh['dp'=2,'expert'=32,'tensor'=4] {'tensor'}, dimensions={1}, use_global_device_ids=true | all-gather | bytes 655360 | tf_op jit(solution)/shard_map/all_gather | solution.py:193
  519.9 5.7 %add_convert_fusion.1 = bf16[2,2,1024,352]{2,3,0,1:T(8,128)(2,1)S(1)} fusion(bf16[2,2,1024,352]{2,3,0,1:T(8,128)(2,1)} %collective-permute-done.8, pred[]{:T(512)S(6)} %eq.45, bf16[2,2,2048,352]{2,3,0,1:T(8,128)(2,1)} %copy-done.1), kind=kLoop, calls=%fused_computation.12 | loop fusion | flops 7208960 | bytes 11534337 | tf_op jit(solution)/shard_map/convert_element_type | solution.py:82
  (130 shorter events, 97.0 us)
Async XLA Ops:
  7.2 8.7 %copy-start.10 = (s32[128,6]{0,1:T(8,128)S(1)}, s32[128,6]{0,1:T(8,128)}, u32[]{:S(2)}) copy-start(s32[128,6]{0,1:T(8,128)} %param.15) | copy-start | bytes 9220
  7.2 147.6 %all-gather.3.cloned.1.call-start = ((), (), s32[]{:S(2)}) async-start(), calls=%async_computation.6 | async-start | bytes 4587520 | tf_op jit(solution)/shard_map/all_gather | solution.py:139
  10.2 11.9 %collective-permute-start = (bf16[128,512]{1,0:T(8,128)(2,1)S(1)}, bf16[128,512]{1,0:T(8,128)(2,1)S(1)}, u32[]{:S(2)}, u32[]{:S(2)}) collective-permute-start(bf16[128,512]{1,0:T(8,128)(2,1)S(1)} %get-tuple-element.47), channel_id=1, source_target_pairs={{0,1},{1,2},{2,3},{3,0},{4,5},{5,6},{6,7},{7,4},{8,9},{9,10},{10,1... | collective-permute-start | bytes 393224 | tf_op jit(solution)/shard_map/ppermute | solution.py:26
  11.7 10.4 %collective-permute-start.1 = (bf16[128,512]{1,0:T(8,128)(2,1)S(1)}, bf16[128,512]{1,0:T(8,128)(2,1)S(1)}, u32[]{:S(2)}, u32[]{:S(2)}) collective-permute-start(bf16[128,512]{1,0:T(8,128)(2,1)S(1)} %get-tuple-element.46), channel_id=1, source_target_pairs={{0,2},{1,3},{2,0},{3,1},{4,6},{5,7},{6,4},{7,5},{8,10},{9,11},{10,... | collective-permute-start | bytes 393224 | tf_op jit(solution)/shard_map/ppermute | solution.py:26
  14.5 7.7 %collective-permute-start.2 = (bf16[128,512]{1,0:T(8,128)(2,1)S(1)}, bf16[128,512]{1,0:T(8,128)(2,1)S(1)}, u32[]{:S(2)}, u32[]{:S(2)}) collective-permute-start(bf16[128,512]{1,0:T(8,128)(2,1)S(1)} %get-tuple-element.45), channel_id=1, source_target_pairs={{0,3},{1,0},{2,1},{3,2},{4,7},{5,4},{6,5},{7,6},{8,11},{9,8},{10,9... | collective-permute-start | bytes 393224 | tf_op jit(solution)/shard_map/ppermute | solution.py:26
  24.0 4.8 collective-permute-start.3
  24.7 5.1 collective-permute-start.4
  26.2 3.6 collective-permute-start.5
  76.9 147.8 %reduce-scatter.3.cloned.1.call-start = ((), (), s32[]{:S(2)}) async-start(), calls=%async_computation.7 | async-start | bytes 4587520 | tf_op jit(solution)/shard_map/reduce_scatter | solution.py:148
  80.6 65.7 %collective-permute-start.6 = (bf16[2,2,1024,352]{2,3,0,1:T(8,128)(2,1)}, bf16[2,2,1024,352]{2,3,0,1:T(8,128)(2,1)}, u32[]{:S(2)}, u32[]{:S(2)}) collective-permute-start(bf16[2,2,1024,352]{2,3,0,1:T(8,128)(2,1)} %copy.74), channel_id=1, source_target_pairs={{0,128},{128,0},{1,129},{129,1},{2,130},{130,2},{3,131},{131,3},{4... | collective-permute-start | bytes 8650760 | tf_op jit(solution)/shard_map/ppermute | solution.py:64
  81.5 94.9 %collective-permute-start.7 = (bf16[2,352,1024]{2,1,0:T(8,128)(2,1)}, bf16[2,352,1024]{2,1,0:T(8,128)(2,1)}, u32[]{:S(2)}, u32[]{:S(2)}) collective-permute-start(bf16[2,352,1024]{2,1,0:T(8,128)(2,1)} %param.17), channel_id=1, source_target_pairs={{0,128},{128,0},{1,129},{129,1},{2,130},{130,2},{3,131},{131,3},{4... | collective-permute-start | bytes 4325384 | tf_op jit(solution)/shard_map/ppermute | solution.py:64
  154.8 5.1 copy-start.2
  154.8 5.7 %copy-start.12 = (bf16[2,32,14,2048]{3,1,2,0:T(8,128)(2,1)S(1)}, bf16[2,32,14,2048]{3,1,2,0:T(8,128)(2,1)}, u32[]{:S(2)}) copy-start(bf16[2,32,14,2048]{3,1,2,0:T(8,128)(2,1)} %all-gather.3.cloned.1.call-done) | copy-start | bytes 11010052
  163.6 12.7 %copy-start.15 = (bf16[2,32,14,352]{3,1,2,0:T(8,128)(2,1)}, bf16[2,32,14,352]{3,1,2,0:T(8,128)(2,1)S(1)}, u32[]{:S(2)}) copy-start(bf16[2,32,14,352]{3,1,2,0:T(8,128)(2,1)S(1)} %get-tuple-element.50) | copy-start | bytes 1892356
  183.4 53.4 %copy-start.11 = (f32[128,6]{0,1:T(8,128)S(1)}, f32[128,6]{0,1:T(8,128)}, u32[]{:S(2)}) copy-start(f32[128,6]{0,1:T(8,128)} %param.14) | copy-start | bytes 9220
  227.7 32.4 %all-to-all-start.1 = ((bf16[2,32,14,512]{3,0,2,1:T(2,128)(2,1)}), bf16[2,32,14,512]{3,0,2,1:T(2,128)(2,1)}, u32[]{:S(2)}, u32[]{:S(2)}) async-start(bf16[2,32,14,512]{3,0,2,1:T(2,128)(2,1)} %copy.76), calls=%async_computation.2 | async-start | bytes 1835008 | tf_op jit(solution)/shard_map/all_to_all | solution.py:19
  236.7 123.2 %all-gather.5.cloned.1.call-start = ((), (), s32[]{:S(2)}) async-start(), calls=%async_computation.8 | async-start | bytes 4587520 | tf_op jit(solution)/shard_map/all_gather | solution.py:163
  267.1 4.8 copy-start.9
  313.5 109.0 %reduce-scatter.5.cloned.1.call-start = ((), (), s32[]{:S(2)}) async-start(), calls=%async_computation.9 | async-start | bytes 4587520 | tf_op jit(solution)/shard_map/reduce_scatter | solution.py:176
  367.0 4.2 copy-start.7
  386.5 130.0 %collective-permute-start.8 = (bf16[2,2,1024,352]{2,3,0,1:T(8,128)(2,1)}, bf16[2,2,1024,352]{2,3,0,1:T(8,128)(2,1)}, u32[]{:S(2)}, u32[]{:S(2)}) collective-permute-start(bf16[2,2,1024,352]{2,3,0,1:T(8,128)(2,1)} %broadcast_select_fusion), channel_id=1, source_target_pairs={{0,128},{128,0},{1,129},{129,1},{2,130},{130,2},{3,131},{131,3},{4... | collective-permute-start | bytes 8650760 | tf_op jit(solution)/shard_map/ppermute | solution.py:77
  425.5 48.6 %all-to-all-start.3 = ((bf16[2,32,14,512]{3,0,2,1:T(2,128)(2,1)}), bf16[2,32,14,512]{3,0,2,1:T(2,128)(2,1)S(1)}, u32[]{:S(2)}, u32[]{:S(2)}) async-start(bf16[2,32,14,512]{3,0,2,1:T(2,128)(2,1)} %copy.81), calls=%async_computation.5 | async-start | bytes 1835008 | tf_op jit(solution)/shard_map/all_to_all | solution.py:19
  441.6 74.9 %collective-permute-start.9 = (bf16[2,352,1024]{2,1,0:T(8,128)(2,1)}, bf16[2,352,1024]{2,1,0:T(8,128)(2,1)}, u32[]{:S(2)}, u32[]{:S(2)}) collective-permute-start(bf16[2,352,1024]{2,1,0:T(8,128)(2,1)} %broadcast_select_fusion.1), channel_id=1, source_target_pairs={{0,128},{128,0},{1,129},{129,1},{2,130},{130,2},{3,131},{131,3},{4... | collective-permute-start | bytes 4325384 | tf_op jit(solution)/shard_map/ppermute | solution.py:77
  501.3 15.2 %copy-start.5 = (bf16[2,352,2048]{2,1,0:T(8,128)(2,1)S(1)}, bf16[2,352,2048]{2,1,0:T(8,128)(2,1)}, u32[]{:S(2)}) copy-start(bf16[2,352,2048]{2,1,0:T(8,128)(2,1)} %copy-done.4) | copy-start | bytes 8650756
  (8 other events, 22.9 us)
Sparse Core Ops, SparseCore 0:
  77.0 42.9 all-gather.2
  183.5 41.0 reduce-scatter.2
  313.6 46.2 all-gather.4
  377.0 45.3 reduce-scatter.4

commit v6 on v5

--- a/solution.py
+++ b/solution.py
@@ -107,10 +107,7 @@
     expert_range = jnp.arange(EXPERTS, dtype=jnp.int32)
     slot_order = expert_range % local_experts * expert_ranks + expert_range // local_experts
     dp_first = lax.axis_index("dp") == 0
-    gate_up_full, down_full = (
-        dp_joined(w_gate_up, dp_first, 2),
-        dp_joined(w_down, dp_first, 2),
-    )
+    down_other = lax.ppermute(w_down, "dp", DP_SWAP)
     partial_attn = jnp.dot(context, wo_rows, preferred_element_type=jnp.float32)
     attn_cols = tensor_scattered(partial_attn.astype(jnp.bfloat16))
     hidden_cols = lax.dynamic_slice_in_dim(residual, col_start, col_count, 1).astype(
@@ -136,6 +133,13 @@
     row_gate = gate_pad[row_entry]
     normed_pad = jnp.concatenate([normed, jnp.zeros((1, col_count), jnp.bfloat16)], axis=0)
     outgoing = normed_pad[row_token].reshape(local_experts, expert_ranks, CAP, col_count)
+    down_other, outgoing = lax.optimization_barrier((down_other, outgoing))
+    gate_up_full = dp_joined(w_gate_up, dp_first, 2)
+    down_full = jnp.where(
+        dp_first,
+        jnp.concatenate([w_down, down_other], axis=2),
+        jnp.concatenate([down_other, w_down], axis=2),
+    )
     arrived = lax.all_gather(to_experts(outgoing), "tensor", axis=3, tiled=True)
     gate_full = gate_up_full[:, 0]
     up_full = gate_up_full[:, 1]

time: 544 us -> 542 us (level)
    ppermute x2 -> x1, waiting for transfers between devices: 76.2 us -> 64.4 us  [dp_joined(): other = lax.ppermute(own, 'dp', DP_SWAP)]
    ppermute x0 -> x1, waiting for transfers between devices: none -> 11.5 us  [per_device(): down_other = lax.ppermute(w_down, 'dp', DP_SWAP)]
where the time goes in v6:
time: 542 us; the launch traced here: 533 us
  waiting for transfers between devices  247 us (46%)
  blocking collectives  97.2 us (18%)
  local copies, waits for them, and re-layouts  64.3 us (12%)
  matrix products  44.7 us (8%)
  other arithmetic  32.9 us (6%)
  starting transfers between devices  32 us (6%)
  between operations  14.7 us (3%)
    all_to_all x2, blocking collectives, to_experts(): lax.all_to_all(outgoing, 'expert', split_axis=1, concat_axis=1, tiled=True)  67.4 us
    ppermute x1, waiting for transfers between devices, dp_joined(): other = lax.ppermute(own, 'dp', DP_SWAP)  64.4 us
    all_to_all x2, waiting for transfers between devices, to_tokens(): lax.all_to_all(outgoing, 'expert', split_axis=1, concat_axis=1, tiled=True)  49.9 us
    all_gather x1, waiting for transfers between devices, per_device(): lax.all_gather(to_experts(grad_slot), 'tensor', axis=3, tiled=True)  46.2 us
    reduce_scatter x1, waiting for transfers between devices, per_device(): lax.psum_scatter(partial_out.astype(jnp.bfloat16), 'tensor', scatter_dime...  39 us
    reduce_scatter x1, waiting for transfers between devices, per_device(): lax.psum_scatter(d_entry_part.astype(jnp.bfloat16), 'tensor', scatter_dim...  35.4 us
    all_to_all x2, starting transfers between devices, to_tokens(): lax.all_to_all(outgoing, 'expert', split_axis=1, concat_axis=1, tiled=True)  18.3 us
    psum x1, blocking collectives, per_device(): norm_dots, gate_prob_grad = lax.psum((norm_partial, gate_partial), 'tensor')  16.3 us
  transfers between devices with their start and end apart: 16, of which 9 were waited for; matrix products, arithmetic and copies ran while one was open for 11% of the time, Pallas kernels for 0%

profile of v6, /device:TPU:32, one launch (start us, length us, event | category | flops | bytes accessed | tf_op | source)
XLA Modules:
  0.0 532.8 jit_solution(11993811084369296172)
XLA Ops:
  31.1 4.0 gather_fusion.2
  37.2 11.5 %collective-permute-done.3 = bf16[2,352,1024]{2,1,0:T(8,128)(2,1)} collective-permute-done((bf16[2,352,1024]{2,1,0:T(8,128)(2,1)}, bf16[2,352,1024]{2,1,0:T(8,128)(2,1)}, u32[]{:S(2)}, u32[]{:S(2)}) %collective-permute-start.3) | collective-permute-done | bytes 1441824 | tf_op jit(solution)/shard_map/ppermute | solution.py:110
  50.9 37.0 %all_to_all.20 = bf16[2,32,14,512]{3,0,2,1:T(2,128)(2,1)S(1)} all-to-all(bf16[2,32,14,512]{3,0,2,1:T(2,128)(2,1)S(1)} %copy.71), channel_id=1, replica_groups=mesh['dp'=2,'expert'=32,'tensor'=4] {'expert'}, dimensions={1} | all-to-all | bytes 1835008 | tf_op jit(solution)/shard_map/all_to_all | solution.py:15
  93.5 64.4 %collective-permute-done.7 = bf16[2,2,1024,352]{2,3,0,1:T(8,128)(2,1)} collective-permute-done((bf16[2,2,1024,352]{2,3,0,1:T(8,128)(2,1)}, bf16[2,2,1024,352]{2,3,0,1:T(8,128)(2,1)}, u32[]{:S(2)}, u32[]{:S(2)}) %collective-permute-start.7) | collective-permute-done | bytes 2883616 | tf_op jit(solution)/shard_map/ppermute | solution.py:64
  157.9 8.5 %maximum_select_fusion = bf16[2,2,2048,352]{2,3,0,1:T(8,128)(2,1)} fusion(bf16[2,2,1024,352]{2,3,0,1:T(8,128)(2,1)} %collective-permute-done.7, pred[]{:T(512)S(6)} %eq.45, bf16[2,2,1024,352]{2,3,1,0:T(8,128)(2,1)} %param.16), kind=kLoop, calls=%fused_computation.10 | loop fusion | flops 25952256 | bytes 11534337 | tf_op jit(solution)/shard_map/jit(_where)/select_n | solution.py:65
  166.5 5.1 fusion.1
  176.2 7.0 %convolution_convert_fusion = bf16[2,32,14,2048]{3,1,2,0:T(8,128)(2,1)} fusion(bf16[2,32,14,352]{3,1,2,0:T(8,128)(2,1)S(1)} %get-tuple-element.54, bf16[2,352,1024]{2,1,0:T(8,128)(2,1)} %collective-permute-done.3, bf16[2,352,1024]{2,1,0:T(8,128)(2,1)} %param.17, pred[]{:T(512)S(6)} %eq.45), kind=kOutput, calls=%fused_computation.15 | convolution fusion | flops 1306656768 | bytes 7184385 | tf_op jit(solution)/shard_map/escf,efd->escd/dot_general | solution.py:149
  183.2 39.0 %reduce-scatter.3.cloned.1.call-done = bf16[2,32,14,512]{3,1,2,0:T(8,128)(2,1)} async-done(((bf16[2,32,14,2048]{3,1,2,0:T(8,128)(2,1)}), bf16[2,32,14,512]{3,1,2,0:T(8,128)(2,1)}) %reduce-scatter.3.cloned.1.call-update) | async-done | bytes 917520 | tf_op jit(solution)/shard_map/reduce_scatter | solution.py:152
  225.3 9.1 %all-to-all-start.1 = ((bf16[2,32,14,512]{3,0,2,1:T(2,128)(2,1)}), bf16[2,32,14,512]{3,0,2,1:T(2,128)(2,1)}, u32[]{:S(2)}, u32[]{:S(2)}) async-start(bf16[2,32,14,512]{3,0,2,1:T(2,128)(2,1)} %copy.76), calls=%async_computation.2 | async-start | bytes 1835008 | tf_op jit(solution)/shard_map/all_to_all | solution.py:19
  238.5 19.1 %all-to-all-done.1 = bf16[2,32,14,512]{3,0,2,1:T(2,128)(2,1)} async-done(((bf16[2,32,14,512]{3,0,2,1:T(2,128)(2,1)}), bf16[2,32,14,512]{3,0,2,1:T(2,128)(2,1)}, u32[]{:S(2)}, u32[]{:S(2)}) %all-to-all-start.1) | async-done | bytes 917536 | tf_op jit(solution)/shard_map/all_to_all | solution.py:19
  270.4 4.0 gather_fusion.5
  279.6 30.3 %all_to_all.21 = bf16[2,32,14,512]{3,0,2,1:T(2,128)(2,1)S(1)} all-to-all(bf16[2,32,14,512]{3,0,2,1:T(2,128)(2,1)S(1)} %copy.79), channel_id=1, replica_groups=mesh['dp'=2,'expert'=32,'tensor'=4] {'expert'}, dimensions={1} | all-to-all | bytes 1835008 | tf_op jit(solution)/shard_map/all_to_all | solution.py:15
  311.4 46.2 %all-gather.5.cloned.1.call-done = bf16[2,32,14,2048]{3,1,2,0:T(8,128)(2,1)} async-done(((bf16[2,32,14,512]{3,1,2,0:T(8,128)(2,1)}), bf16[2,32,14,2048]{3,1,2,0:T(8,128)(2,1)}) %all-gather.5.cloned.1.call-update) | async-done | bytes 3670032 | tf_op jit(solution)/shard_map/all_gather | solution.py:167
  357.6 7.0 %multiply_convert_fusion.2 = (bf16[2,32,14,352]{3,1,2,0:T(8,128)(2,1)S(1)}, bf16[2,32,14,352]{3,1,2,0:T(8,128)(2,1)S(1)}) fusion(f32[2,32,14,352]{3,1,2,0:T(8,128)} %copy-done.14, f32[2,32,14,352]{3,1,2,0:T(8,128)} %get-tuple-element.55, bf16[2,32,14,2048]{3,1,2,0:T(8,128)(2,1)} %all-gather.5.cloned.1.call-done, ...), kind=kOutput, calls=%fused_computation.32 | convolution fusion | flops 1308921856 | bytes 10338305 | tf_op jit(solution)/shard_map/escd,efd->escf/dot_general | solution.py:168
  364.6 4.2 fusion.2
  368.8 5.7 %add_convert_fusion = bf16[2,32,14,2048]{3,1,2,0:T(8,128)(2,1)} fusion(f32[2,32,14,2048]{3,1,2,0:T(8,128)S(1)} %fusion.2, bf16[2,32,14,352]{3,1,2,0:T(8,128)(2,1)S(1)} %get-tuple-element.46, bf16[2,2,2048,352]{2,3,0,1:T(8,128)(2,1)} %maximum_select_fusion), kind=kOutput, calls=%fused_computation.9 | convolution fusion | flops 1295515648 | bytes 14524416 | tf_op jit(solution)/shard_map/escf,edf->escd/dot_general | solution.py:174
  374.6 3.9 convolution_bitcast_fusion.1
  384.6 35.4 %reduce-scatter.5.cloned.1.call-done = bf16[2,32,14,512]{3,1,2,0:T(8,128)(2,1)} async-done(((bf16[2,32,14,2048]{3,1,2,0:T(8,128)(2,1)}), bf16[2,32,14,512]{3,1,2,0:T(8,128)(2,1)}) %reduce-scatter.5.cloned.1.call-update) | async-done | bytes 917520 | tf_op jit(solution)/shard_map/reduce_scatter | solution.py:180
  423.2 9.2 %all-to-all-start.3 = ((bf16[2,32,14,512]{3,0,2,1:T(2,128)(2,1)}), bf16[2,32,14,512]{3,0,2,1:T(2,128)(2,1)S(1)}, u32[]{:S(2)}, u32[]{:S(2)}) async-start(bf16[2,32,14,512]{3,0,2,1:T(2,128)(2,1)} %copy.81), calls=%async_computation.5 | async-start | bytes 1835008 | tf_op jit(solution)/shard_map/all_to_all | solution.py:19
  432.4 4.0 bitcast_convert_fusion
  441.0 30.8 %all-to-all-done.3 = bf16[2,32,14,512]{3,0,2,1:T(2,128)(2,1)S(1)} async-done(((bf16[2,32,14,512]{3,0,2,1:T(2,128)(2,1)}), bf16[2,32,14,512]{3,0,2,1:T(2,128)(2,1)S(1)}, u32[]{:S(2)}, u32[]{:S(2)}) %all-to-all-start.3) | async-done | bytes 917536 | tf_op jit(solution)/shard_map/all_to_all | solution.py:19
  482.7 16.3 %all-reduce.2 = (f32[128]{0:T(128)S(1)}, f32[128,6]{1,0:T(8,128)S(1)}) all-reduce(f32[128]{0:T(128)S(1)} %multiply_reduce_fusion.2, f32[128,6]{1,0:T(8,128)S(1)} %multiply_reduce_fusion), channel_id=1, replica_groups=mesh['dp'=2,'expert'=32,'tensor'=4] {'tensor'}, use_global_device_ids=true, to_apply=%region_11.12 | all-reduce | flops 896 | bytes 7168 | tf_op jit(solution)/shard_map/psum | solution.py:189
  499.1 13.6 %all_gather.11 = bf16[128,2048]{1,0:T(8,128)(2,1)S(1)} all-gather(bf16[128,512]{1,0:T(8,128)(2,1)S(1)} %subtract_convert_fusion), channel_id=1, replica_groups=mesh['dp'=2,'expert'=32,'tensor'=4] {'tensor'}, dimensions={1}, use_global_device_ids=true | all-gather | bytes 655360 | tf_op jit(solution)/shard_map/all_gather | solution.py:197
  517.6 5.7 %add_convert_fusion.1 = bf16[2,2,1024,352]{2,3,0,1:T(8,128)(2,1)S(1)} fusion(bf16[2,2,1024,352]{2,3,0,1:T(8,128)(2,1)} %collective-permute-done.8, pred[]{:T(512)S(6)} %eq.45, bf16[2,2,2048,352]{2,3,0,1:T(8,128)(2,1)} %copy-done.1), kind=kLoop, calls=%fused_computation.12 | loop fusion | flops 7208960 | bytes 11534337 | tf_op jit(solution)/shard_map/convert_element_type | solution.py:82
  (130 shorter events, 97.0 us)
Async XLA Ops:
  7.2 8.9 %copy-start.10 = (s32[128,6]{0,1:T(8,128)S(1)}, s32[128,6]{0,1:T(8,128)}, u32[]{:S(2)}) copy-start(s32[128,6]{0,1:T(8,128)} %param.15) | copy-start | bytes 9220
  7.2 159.3 %all-gather.3.cloned.1.call-start = ((), (), s32[]{:S(2)}) async-start(), calls=%async_computation.6 | async-start | bytes 4587520 | tf_op jit(solution)/shard_map/all_gather | solution.py:143
  10.2 12.0 %collective-permute-start = (bf16[128,512]{1,0:T(8,128)(2,1)S(1)}, bf16[128,512]{1,0:T(8,128)(2,1)S(1)}, u32[]{:S(2)}, u32[]{:S(2)}) collective-permute-start(bf16[128,512]{1,0:T(8,128)(2,1)S(1)} %get-tuple-element.51), channel_id=1, source_target_pairs={{0,1},{1,2},{2,3},{3,0},{4,5},{5,6},{6,7},{7,4},{8,9},{9,10},{10,1... | collective-permute-start | bytes 393224 | tf_op jit(solution)/shard_map/ppermute | solution.py:26
  11.7 10.5 %collective-permute-start.1 = (bf16[128,512]{1,0:T(8,128)(2,1)S(1)}, bf16[128,512]{1,0:T(8,128)(2,1)S(1)}, u32[]{:S(2)}, u32[]{:S(2)}) collective-permute-start(bf16[128,512]{1,0:T(8,128)(2,1)S(1)} %get-tuple-element.50), channel_id=1, source_target_pairs={{0,2},{1,3},{2,0},{3,1},{4,6},{5,7},{6,4},{7,5},{8,10},{9,11},{10,... | collective-permute-start | bytes 393224 | tf_op jit(solution)/shard_map/ppermute | solution.py:26
  14.5 7.8 %collective-permute-start.2 = (bf16[128,512]{1,0:T(8,128)(2,1)S(1)}, bf16[128,512]{1,0:T(8,128)(2,1)S(1)}, u32[]{:S(2)}, u32[]{:S(2)}) collective-permute-start(bf16[128,512]{1,0:T(8,128)(2,1)S(1)} %get-tuple-element.49), channel_id=1, source_target_pairs={{0,3},{1,0},{2,1},{3,2},{4,7},{5,4},{6,5},{7,6},{8,11},{9,8},{10,9... | collective-permute-start | bytes 393224 | tf_op jit(solution)/shard_map/ppermute | solution.py:26
  15.9 32.8 %collective-permute-start.3 = (bf16[2,352,1024]{2,1,0:T(8,128)(2,1)}, bf16[2,352,1024]{2,1,0:T(8,128)(2,1)}, u32[]{:S(2)}, u32[]{:S(2)}) collective-permute-start(bf16[2,352,1024]{2,1,0:T(8,128)(2,1)} %param.17), channel_id=1, source_target_pairs={{0,128},{128,0},{1,129},{129,1},{2,130},{130,2},{3,131},{131,3},{4... | collective-permute-start | bytes 4325384 | tf_op jit(solution)/shard_map/ppermute | solution.py:110
  24.1 5.7 %collective-permute-start.4 = (f32[128,1]{0,1:T(1,128)S(1)}, f32[128,1]{0,1:T(1,128)S(1)}, u32[]{:S(2)}, u32[]{:S(2)}) collective-permute-start(f32[128,1]{0,1:T(1,128)S(1)} %bitcast.107), channel_id=1, source_target_pairs={{0,1},{1,2},{2,3},{3,0},{4,5},{5,6},{6,7},{7,4},{8,9},{9,10},{10,1... | collective-permute-start | bytes 1544 | tf_op jit(solution)/shard_map/ppermute | solution.py:26
  24.8 5.1 collective-permute-start.5
  26.5 3.8 collective-permute-start.6
  89.1 133.2 %reduce-scatter.3.cloned.1.call-start = ((), (), s32[]{:S(2)}) async-start(), calls=%async_computation.7 | async-start | bytes 4587520 | tf_op jit(solution)/shard_map/reduce_scatter | solution.py:152
  92.8 65.2 %collective-permute-start.7 = (bf16[2,2,1024,352]{2,3,0,1:T(8,128)(2,1)}, bf16[2,2,1024,352]{2,3,0,1:T(8,128)(2,1)}, u32[]{:S(2)}, u32[]{:S(2)}) collective-permute-start(bf16[2,2,1024,352]{2,3,0,1:T(8,128)(2,1)} %copy.74), channel_id=1, source_target_pairs={{0,128},{128,0},{1,129},{129,1},{2,130},{130,2},{3,131},{131,3},{4... | collective-permute-start | bytes 8650760 | tf_op jit(solution)/shard_map/ppermute | solution.py:64
  166.5 5.1 copy-start.2
  166.5 5.7 %copy-start.12 = (bf16[2,32,14,2048]{3,1,2,0:T(8,128)(2,1)S(1)}, bf16[2,32,14,2048]{3,1,2,0:T(8,128)(2,1)}, u32[]{:S(2)}) copy-start(bf16[2,32,14,2048]{3,1,2,0:T(8,128)(2,1)} %all-gather.3.cloned.1.call-done) | copy-start | bytes 11010052
  183.2 51.2 %copy-start.11 = (f32[128,6]{0,1:T(8,128)S(1)}, f32[128,6]{0,1:T(8,128)}, u32[]{:S(2)}) copy-start(f32[128,6]{0,1:T(8,128)} %param.14) | copy-start | bytes 9220
  225.3 32.3 %all-to-all-start.1 = ((bf16[2,32,14,512]{3,0,2,1:T(2,128)(2,1)}), bf16[2,32,14,512]{3,0,2,1:T(2,128)(2,1)}, u32[]{:S(2)}, u32[]{:S(2)}) async-start(bf16[2,32,14,512]{3,0,2,1:T(2,128)(2,1)} %copy.76), calls=%async_computation.2 | async-start | bytes 1835008 | tf_op jit(solution)/shard_map/all_to_all | solution.py:19
  234.4 123.2 %all-gather.5.cloned.1.call-start = ((), (), s32[]{:S(2)}) async-start(), calls=%async_computation.8 | async-start | bytes 4587520 | tf_op jit(solution)/shard_map/all_gather | solution.py:167
  264.7 4.8 copy-start.9
  311.1 109.0 %reduce-scatter.5.cloned.1.call-start = ((), (), s32[]{:S(2)}) async-start(), calls=%async_computation.9 | async-start | bytes 4587520 | tf_op jit(solution)/shard_map/reduce_scatter | solution.py:180
  364.6 4.2 copy-start.7
  374.6 3.9 copy-start.8
  384.2 130.0 %collective-permute-start.8 = (bf16[2,2,1024,352]{2,3,0,1:T(8,128)(2,1)}, bf16[2,2,1024,352]{2,3,0,1:T(8,128)(2,1)}, u32[]{:S(2)}, u32[]{:S(2)}) collective-permute-start(bf16[2,2,1024,352]{2,3,0,1:T(8,128)(2,1)} %broadcast_select_fusion), channel_id=1, source_target_pairs={{0,128},{128,0},{1,129},{129,1},{2,130},{130,2},{3,131},{131,3},{4... | collective-permute-start | bytes 8650760 | tf_op jit(solution)/shard_map/ppermute | solution.py:77
  423.2 48.6 %all-to-all-start.3 = ((bf16[2,32,14,512]{3,0,2,1:T(2,128)(2,1)}), bf16[2,32,14,512]{3,0,2,1:T(2,128)(2,1)S(1)}, u32[]{:S(2)}, u32[]{:S(2)}) async-start(bf16[2,32,14,512]{3,0,2,1:T(2,128)(2,1)} %copy.81), calls=%async_computation.5 | async-start | bytes 1835008 | tf_op jit(solution)/shard_map/all_to_all | solution.py:19
  439.2 74.9 %collective-permute-start.9 = (bf16[2,352,1024]{2,1,0:T(8,128)(2,1)}, bf16[2,352,1024]{2,1,0:T(8,128)(2,1)}, u32[]{:S(2)}, u32[]{:S(2)}) collective-permute-start(bf16[2,352,1024]{2,1,0:T(8,128)(2,1)} %broadcast_select_fusion.1), channel_id=1, source_target_pairs={{0,128},{128,0},{1,129},{129,1},{2,130},{130,2},{3,131},{131,3},{4... | collective-permute-start | bytes 4325384 | tf_op jit(solution)/shard_map/ppermute | solution.py:77
  498.9 15.2 %copy-start.5 = (bf16[2,352,2048]{2,1,0:T(8,128)(2,1)S(1)}, bf16[2,352,2048]{2,1,0:T(8,128)(2,1)}, u32[]{:S(2)}) copy-start(bf16[2,352,2048]{2,1,0:T(8,128)(2,1)} %copy-done.4) | copy-start | bytes 8650756
  (8 other events, 19.9 us)
Sparse Core Ops, SparseCore 0:
  89.2 40.5 all-gather.2
  183.4 38.8 reduce-scatter.2
  311.2 46.2 all-gather.4
  374.7 45.3 reduce-scatter.4

commit v7 on v6

--- a/solution.py
+++ b/solution.py
@@ -133,8 +133,20 @@
     row_gate = gate_pad[row_entry]
     normed_pad = jnp.concatenate([normed, jnp.zeros((1, col_count), jnp.bfloat16)], axis=0)
     outgoing = normed_pad[row_token].reshape(local_experts, expert_ranks, CAP, col_count)
-    down_other, outgoing = lax.optimization_barrier((down_other, outgoing))
-    gate_up_full = dp_joined(w_gate_up, dp_first, 2)
+    first_other = lax.ppermute(w_gate_up[0:1, 0:1], "dp", DP_SWAP)
+    down_other, first_other, outgoing = lax.optimization_barrier(
+        (down_other, first_other, outgoing)
+    )
+    second_other = lax.ppermute(w_gate_up[0:1, 1:2], "dp", DP_SWAP)
+    rest_other = lax.ppermute(w_gate_up[1:], "dp", DP_SWAP)
+    gate_up_other = jnp.concatenate(
+        [jnp.concatenate([first_other, second_other], axis=1), rest_other], axis=0
+    )
+    gate_up_full = jnp.where(
+        dp_first,
+        jnp.concatenate([w_gate_up, gate_up_other], axis=2),
+        jnp.concatenate([gate_up_other, w_gate_up], axis=2),
+    )
     down_full = jnp.where(
         dp_first,
         jnp.concatenate([w_down, down_other], axis=2),

time: 542 us -> 538 us (level)
    ppermute x1 -> x3, waiting for transfers between devices: 64.4 us -> 47.2 us  [the longest x1 47.2 us: per_device(): second_other = lax.ppermute(w_gate_up[0:1, 1:2], 'dp', DP_SWAP)]
    ppermute x1, waiting for transfers between devices: 11.5 us -> 25.3 us  [per_device(): down_other = lax.ppermute(w_down, 'dp', DP_SWAP)]
    unnamed x37 -> x49, local copies, waits for them, and re-layouts: 12.3 us -> 10.2 us
  transfers between devices with their start and end apart: 16 -> 18, of which waited for: 9 -> 9; matrix products, arithmetic and copies ran while one was open for 11% -> 11% of each run, Pallas kernels for 0% -> 0%
where the time goes in v7:
time: 538 us; the launch traced here: 528 us
  waiting for transfers between devices  245 us (46%)
  blocking collectives  96.9 us (18%)
  local copies, waits for them, and re-layouts  60.7 us (11%)
  matrix products  44.9 us (8%)
  starting transfers between devices  34.1 us (6%)
  other arithmetic  32 us (6%)
  between operations  14.6 us (3%)
    all_to_all x2, blocking collectives, to_experts(): lax.all_to_all(outgoing, 'expert', split_axis=1, concat_axis=1, tiled=True)  67.1 us
    all_to_all x2, waiting for transfers between devices, to_tokens(): lax.all_to_all(outgoing, 'expert', split_axis=1, concat_axis=1, tiled=True)  49.7 us
    ppermute x1, waiting for transfers between devices, per_device(): second_other = lax.ppermute(w_gate_up[0:1, 1:2], 'dp', DP_SWAP)  47.2 us
    all_gather x1, waiting for transfers between devices, per_device(): lax.all_gather(to_experts(grad_slot), 'tensor', axis=3, tiled=True)  46.2 us
    reduce_scatter x1, waiting for transfers between devices, per_device(): lax.psum_scatter(partial_out.astype(jnp.bfloat16), 'tensor', scatter_dime...  39.3 us
    reduce_scatter x1, waiting for transfers between devices, per_device(): lax.psum_scatter(d_entry_part.astype(jnp.bfloat16), 'tensor', scatter_dim...  35.4 us
    ppermute x1, waiting for transfers between devices, per_device(): down_other = lax.ppermute(w_down, 'dp', DP_SWAP)  25.3 us
    all_to_all x2, starting transfers between devices, to_tokens(): lax.all_to_all(outgoing, 'expert', split_axis=1, concat_axis=1, tiled=True)  18.1 us
  transfers between devices with their start and end apart: 18, of which 9 were waited for; matrix products, arithmetic and copies ran while one was open for 11% of the time, Pallas kernels for 0%

profile of v7, /device:TPU:32, one launch (start us, length us, event | category | flops | bytes accessed | tf_op | source)
XLA Modules:
  0.0 528.1 jit_solution(13519993543257096513)
XLA Ops:
  34.8 4.0 gather_fusion.2
  40.2 25.3 %collective-permute-done.3 = bf16[2,352,1024]{2,1,0:T(8,128)(2,1)} collective-permute-done((bf16[2,352,1024]{2,1,0:T(8,128)(2,1)}, bf16[2,352,1024]{2,1,0:T(8,128)(2,1)}, u32[]{:S(2)}, u32[]{:S(2)}) %collective-permute-start.3) | collective-permute-done | bytes 1441824 | tf_op jit(solution)/shard_map/ppermute | solution.py:110
  66.5 36.9 %all_to_all.20 = bf16[2,32,14,512]{3,0,2,1:T(2,128)(2,1)S(1)} all-to-all(bf16[2,32,14,512]{3,0,2,1:T(2,128)(2,1)S(1)} %copy.78), channel_id=1, replica_groups=mesh['dp'=2,'expert'=32,'tensor'=4] {'expert'}, dimensions={1} | all-to-all | bytes 1835008 | tf_op jit(solution)/shard_map/all_to_all | solution.py:15
  108.5 47.2 %collective-permute-done.8 = bf16[1,1,1024,352]{2,3,0,1:T(8,128)(2,1)} collective-permute-done((bf16[1,1,1024,352]{2,3,0,1:T(8,128)(2,1)}, bf16[1,1,1024,352]{2,3,0,1:T(8,128)(2,1)}, u32[]{:S(2)}, u32[]{:S(2)}) %collective-permute-start.8) | collective-permute-done | bytes 720928 | tf_op jit(solution)/shard_map/ppermute | solution.py:140
  155.7 7.2 %maximum_select_fusion = bf16[2,2,2048,352]{2,3,0,1:T(8,128)(2,1)} fusion(bf16[1,2,1024,352]{2,3,0,1:T(8,128)(2,1)S(1)} %collective-permute-done.9, bf16[1,1,1024,352]{2,3,0,1:T(8,128)(2,1)} %collective-permute-done.8, bf16[1,1,1024,352]{2,3,0,1:T(8,128)(2,1)} %collective-permute-done.4, pred[]{:T(512)S(6)} %eq.45, bf16[2,2,1024,352]{2,3,1,0:T(8,128)(2,1)} %param.16), kind=kLoop, calls=%fused_computation.10 | loop fusion | flops 49020928 | bytes 11534337 | tf_op jit(solution)/shard_map/jit(_where)/select_n | solution.py:145
  162.9 5.1 fusion.1
  172.6 7.1 %convolution_convert_fusion = bf16[2,32,14,2048]{3,1,2,0:T(8,128)(2,1)} fusion(bf16[2,32,14,352]{3,1,2,0:T(8,128)(2,1)S(1)} %get-tuple-element.58, bf16[2,352,1024]{2,1,0:T(8,128)(2,1)} %collective-permute-done.3, bf16[2,352,1024]{2,1,0:T(8,128)(2,1)} %param.17, pred[]{:T(512)S(6)} %eq.45), kind=kOutput, calls=%fused_computation.15 | convolution fusion | flops 1306656768 | bytes 7184385 | tf_op jit(solution)/shard_map/escf,efd->escd/dot_general | solution.py:161
  179.7 39.3 %reduce-scatter.3.cloned.1.call-done = bf16[2,32,14,512]{3,1,2,0:T(8,128)(2,1)} async-done(((bf16[2,32,14,2048]{3,1,2,0:T(8,128)(2,1)}), bf16[2,32,14,512]{3,1,2,0:T(8,128)(2,1)}) %reduce-scatter.3.cloned.1.call-update) | async-done | bytes 917520 | tf_op jit(solution)/shard_map/reduce_scatter | solution.py:164
  222.0 9.0 %all-to-all-start.1 = ((bf16[2,32,14,512]{3,0,2,1:T(2,128)(2,1)}), bf16[2,32,14,512]{3,0,2,1:T(2,128)(2,1)S(1)}, u32[]{:S(2)}, u32[]{:S(2)}) async-start(bf16[2,32,14,512]{3,0,2,1:T(2,128)(2,1)} %copy.84), calls=%async_computation.2 | async-start | bytes 1835008 | tf_op jit(solution)/shard_map/all_to_all | solution.py:19
  235.6 18.8 %all-to-all-done.1 = bf16[2,32,14,512]{3,0,2,1:T(2,128)(2,1)S(1)} async-done(((bf16[2,32,14,512]{3,0,2,1:T(2,128)(2,1)}), bf16[2,32,14,512]{3,0,2,1:T(2,128)(2,1)S(1)}, u32[]{:S(2)}, u32[]{:S(2)}) %all-to-all-start.1) | async-done | bytes 917536 | tf_op jit(solution)/shard_map/all_to_all | solution.py:19
  266.0 4.0 gather_fusion.5
  275.2 30.2 %all_to_all.21 = bf16[2,32,14,512]{3,0,2,1:T(2,128)(2,1)S(1)} all-to-all(bf16[2,32,14,512]{3,0,2,1:T(2,128)(2,1)S(1)} %copy.87), channel_id=1, replica_groups=mesh['dp'=2,'expert'=32,'tensor'=4] {'expert'}, dimensions={1} | all-to-all | bytes 1835008 | tf_op jit(solution)/shard_map/all_to_all | solution.py:15
  306.8 46.2 %all-gather.5.cloned.1.call-done = bf16[2,32,14,2048]{3,1,2,0:T(8,128)(2,1)} async-done(((bf16[2,32,14,512]{3,1,2,0:T(8,128)(2,1)}), bf16[2,32,14,2048]{3,1,2,0:T(8,128)(2,1)}) %all-gather.5.cloned.1.call-update) | async-done | bytes 3670032 | tf_op jit(solution)/shard_map/all_gather | solution.py:179
  353.0 7.0 %multiply_convert_fusion.2 = (bf16[2,32,14,352]{3,1,2,0:T(8,128)(2,1)S(1)}, bf16[2,32,14,352]{3,1,2,0:T(8,128)(2,1)S(1)}) fusion(f32[2,32,14,352]{3,1,2,0:T(8,128)} %copy-done.20, f32[2,32,14,352]{3,1,2,0:T(8,128)} %get-tuple-element.59, bf16[2,32,14,2048]{3,1,2,0:T(8,128)(2,1)} %all-gather.5.cloned.1.call-done, ...), kind=kOutput, calls=%fused_computation.32 | convolution fusion | flops 1308921856 | bytes 10338305 | tf_op jit(solution)/shard_map/escd,efd->escf/dot_general | solution.py:180
  360.1 4.2 fusion.2
  364.2 5.7 %add_convert_fusion = bf16[2,32,14,2048]{3,1,2,0:T(8,128)(2,1)} fusion(f32[2,32,14,2048]{3,1,2,0:T(8,128)S(1)} %fusion.2, bf16[2,32,14,352]{3,1,2,0:T(8,128)(2,1)S(1)} %get-tuple-element.50, bf16[2,2,2048,352]{2,3,0,1:T(8,128)(2,1)} %maximum_select_fusion), kind=kOutput, calls=%fused_computation.9 | convolution fusion | flops 1295515648 | bytes 14524416 | tf_op jit(solution)/shard_map/escf,edf->escd/dot_general | solution.py:186
  370.0 3.9 convolution_bitcast_fusion.1
  380.1 35.4 %reduce-scatter.5.cloned.1.call-done = bf16[2,32,14,512]{3,1,2,0:T(8,128)(2,1)} async-done(((bf16[2,32,14,2048]{3,1,2,0:T(8,128)(2,1)}), bf16[2,32,14,512]{3,1,2,0:T(8,128)(2,1)}) %reduce-scatter.5.cloned.1.call-update) | async-done | bytes 917520 | tf_op jit(solution)/shard_map/reduce_scatter | solution.py:192
  418.6 9.2 %all-to-all-start.3 = ((bf16[2,32,14,512]{3,0,2,1:T(2,128)(2,1)}), bf16[2,32,14,512]{3,0,2,1:T(2,128)(2,1)S(1)}, u32[]{:S(2)}, u32[]{:S(2)}) async-start(bf16[2,32,14,512]{3,0,2,1:T(2,128)(2,1)} %copy.89), calls=%async_computation.5 | async-start | bytes 1835008 | tf_op jit(solution)/shard_map/all_to_all | solution.py:19
  427.8 4.0 bitcast_convert_fusion
  436.3 30.9 %all-to-all-done.3 = bf16[2,32,14,512]{3,0,2,1:T(2,128)(2,1)S(1)} async-done(((bf16[2,32,14,512]{3,0,2,1:T(2,128)(2,1)}), bf16[2,32,14,512]{3,0,2,1:T(2,128)(2,1)S(1)}, u32[]{:S(2)}, u32[]{:S(2)}) %all-to-all-start.3) | async-done | bytes 917536 | tf_op jit(solution)/shard_map/all_to_all | solution.py:19
  478.2 16.2 %all-reduce.2 = (f32[128]{0:T(128)S(1)}, f32[128,6]{1,0:T(8,128)S(1)}) all-reduce(f32[128]{0:T(128)S(1)} %multiply_reduce_fusion.2, f32[128,6]{1,0:T(8,128)S(1)} %multiply_reduce_fusion), channel_id=1, replica_groups=mesh['dp'=2,'expert'=32,'tensor'=4] {'tensor'}, use_global_device_ids=true, to_apply=%region_11.12 | all-reduce | flops 896 | bytes 7168 | tf_op jit(solution)/shard_map/psum | solution.py:201
  494.6 13.6 %all_gather.11 = bf16[128,2048]{1,0:T(8,128)(2,1)S(1)} all-gather(bf16[128,512]{1,0:T(8,128)(2,1)S(1)} %subtract_convert_fusion), channel_id=1, replica_groups=mesh['dp'=2,'expert'=32,'tensor'=4] {'tensor'}, dimensions={1}, use_global_device_ids=true | all-gather | bytes 655360 | tf_op jit(solution)/shard_map/all_gather | solution.py:209
  513.1 5.7 %add_convert_fusion.1 = bf16[2,2,1024,352]{2,3,0,1:T(8,128)(2,1)S(1)} fusion(bf16[2,2,1024,352]{2,3,0,1:T(8,128)(2,1)} %collective-permute-done.10, pred[]{:T(512)S(6)} %eq.45, bf16[2,2,2048,352]{2,3,0,1:T(8,128)(2,1)} %copy-done.1), kind=kLoop, calls=%fused_computation.12 | loop fusion | flops 7208960 | bytes 11534337 | tf_op jit(solution)/shard_map/convert_element_type | solution.py:82
  (149 shorter events, 97.4 us)
Async XLA Ops:
  7.2 155.7 %all-gather.3.cloned.1.call-start = ((), (), s32[]{:S(2)}) async-start(), calls=%async_computation.6 | async-start | bytes 4587520 | tf_op jit(solution)/shard_map/all_gather | solution.py:155
  8.8 7.3 %copy-start.6 = (bf16[2,2,1024,352]{2,3,1,0:T(8,128)(2,1)S(1)}, bf16[2,2,1024,352]{2,3,1,0:T(8,128)(2,1)}, u32[]{:S(2)}) copy-start(bf16[2,2,1024,352]{2,3,1,0:T(8,128)(2,1)} %param.16) | copy-start | bytes 8650756
  8.8 10.5 %copy-start.15 = (s32[128,6]{0,1:T(8,128)S(1)}, s32[128,6]{0,1:T(8,128)}, u32[]{:S(2)}) copy-start(s32[128,6]{0,1:T(8,128)} %param.15) | copy-start | bytes 9220
  10.3 15.2 %collective-permute-start = (bf16[128,512]{1,0:T(8,128)(2,1)S(1)}, bf16[128,512]{1,0:T(8,128)(2,1)S(1)}, u32[]{:S(2)}, u32[]{:S(2)}) collective-permute-start(bf16[128,512]{1,0:T(8,128)(2,1)S(1)} %get-tuple-element.55), channel_id=1, source_target_pairs={{0,1},{1,2},{2,3},{3,0},{4,5},{5,6},{6,7},{7,4},{8,9},{9,10},{10,1... | collective-permute-start | bytes 393224 | tf_op jit(solution)/shard_map/ppermute | solution.py:26
  11.9 13.6 %collective-permute-start.1 = (bf16[128,512]{1,0:T(8,128)(2,1)S(1)}, bf16[128,512]{1,0:T(8,128)(2,1)S(1)}, u32[]{:S(2)}, u32[]{:S(2)}) collective-permute-start(bf16[128,512]{1,0:T(8,128)(2,1)S(1)} %get-tuple-element.54), channel_id=1, source_target_pairs={{0,2},{1,3},{2,0},{3,1},{4,6},{5,7},{6,4},{7,5},{8,10},{9,11},{10,... | collective-permute-start | bytes 393224 | tf_op jit(solution)/shard_map/ppermute | solution.py:26
  14.6 10.9 %collective-permute-start.2 = (bf16[128,512]{1,0:T(8,128)(2,1)S(1)}, bf16[128,512]{1,0:T(8,128)(2,1)S(1)}, u32[]{:S(2)}, u32[]{:S(2)}) collective-permute-start(bf16[128,512]{1,0:T(8,128)(2,1)S(1)} %get-tuple-element.53), channel_id=1, source_target_pairs={{0,3},{1,0},{2,1},{3,2},{4,7},{5,4},{6,5},{7,6},{8,11},{9,8},{10,9... | collective-permute-start | bytes 393224 | tf_op jit(solution)/shard_map/ppermute | solution.py:26
  17.3 22.9 %collective-permute-start.4 = (bf16[1,1,1024,352]{2,3,0,1:T(8,128)(2,1)}, bf16[1,1,1024,352]{2,3,0,1:T(8,128)(2,1)}, u32[]{:S(2)}, u32[]{:S(2)}) collective-permute-start(bf16[1,1,1024,352]{2,3,0,1:T(8,128)(2,1)} %get-tuple-element.49), channel_id=1, source_target_pairs={{0,128},{128,0},{1,129},{129,1},{2,130},{130,2},{3,131},{131,3},{4... | collective-permute-start | bytes 2162696 | tf_op jit(solution)/shard_map/ppermute | solution.py:136
  17.4 48.1 %collective-permute-start.3 = (bf16[2,352,1024]{2,1,0:T(8,128)(2,1)}, bf16[2,352,1024]{2,1,0:T(8,128)(2,1)}, u32[]{:S(2)}, u32[]{:S(2)}) collective-permute-start(bf16[2,352,1024]{2,1,0:T(8,128)(2,1)} %param.17), channel_id=1, source_target_pairs={{0,128},{128,0},{1,129},{129,1},{2,130},{130,2},{3,131},{131,3},{4... | collective-permute-start | bytes 4325384 | tf_op jit(solution)/shard_map/ppermute | solution.py:110
  27.4 4.9 collective-permute-start.5
  28.1 5.1 collective-permute-start.6
  28.9 4.2 collective-permute-start.7
  104.5 114.5 %reduce-scatter.3.cloned.1.call-start = ((), (), s32[]{:S(2)}) async-start(), calls=%async_computation.7 | async-start | bytes 4587520 | tf_op jit(solution)/shard_map/reduce_scatter | solution.py:164
  106.3 49.4 %collective-permute-start.9 = (bf16[1,2,1024,352]{2,3,0,1:T(8,128)(2,1)}, bf16[1,2,1024,352]{2,3,0,1:T(8,128)(2,1)S(1)}, u32[]{:S(2)}, u32[]{:S(2)}) collective-permute-start(bf16[1,2,1024,352]{2,3,0,1:T(8,128)(2,1)} %copy.105), channel_id=1, source_target_pairs={{0,128},{128,0},{1,129},{129,1},{2,130},{130,2},{3,131},{131,3},{4... | collective-permute-start | bytes 4325384 | tf_op jit(solution)/shard_map/ppermute | solution.py:141
  107.2 48.5 %collective-permute-start.8 = (bf16[1,1,1024,352]{2,3,0,1:T(8,128)(2,1)}, bf16[1,1,1024,352]{2,3,0,1:T(8,128)(2,1)}, u32[]{:S(2)}, u32[]{:S(2)}) collective-permute-start(bf16[1,1,1024,352]{2,3,0,1:T(8,128)(2,1)} %get-tuple-element.48), channel_id=1, source_target_pairs={{0,128},{128,0},{1,129},{129,1},{2,130},{130,2},{3,131},{131,3},{4... | collective-permute-start | bytes 2162696 | tf_op jit(solution)/shard_map/ppermute | solution.py:140
  179.7 51.8 %copy-start.16 = (f32[128,6]{0,1:T(8,128)S(1)}, f32[128,6]{0,1:T(8,128)}, u32[]{:S(2)}) copy-start(f32[128,6]{0,1:T(8,128)} %param.14) | copy-start | bytes 9220
  222.0 32.3 %all-to-all-start.1 = ((bf16[2,32,14,512]{3,0,2,1:T(2,128)(2,1)}), bf16[2,32,14,512]{3,0,2,1:T(2,128)(2,1)S(1)}, u32[]{:S(2)}, u32[]{:S(2)}) async-start(bf16[2,32,14,512]{3,0,2,1:T(2,128)(2,1)} %copy.84), calls=%async_computation.2 | async-start | bytes 1835008 | tf_op jit(solution)/shard_map/all_to_all | solution.py:19
  231.0 122.0 %all-gather.5.cloned.1.call-start = ((), (), s32[]{:S(2)}) async-start(), calls=%async_computation.8 | async-start | bytes 4587520 | tf_op jit(solution)/shard_map/all_gather | solution.py:179
  306.6 109.0 %reduce-scatter.5.cloned.1.call-start = ((), (), s32[]{:S(2)}) async-start(), calls=%async_computation.9 | async-start | bytes 4587520 | tf_op jit(solution)/shard_map/reduce_scatter | solution.py:192
  379.6 130.0 %collective-permute-start.10 = (bf16[2,2,1024,352]{2,3,0,1:T(8,128)(2,1)}, bf16[2,2,1024,352]{2,3,0,1:T(8,128)(2,1)}, u32[]{:S(2)}, u32[]{:S(2)}) collective-permute-start(bf16[2,2,1024,352]{2,3,0,1:T(8,128)(2,1)} %broadcast_select_fusion), channel_id=1, source_target_pairs={{0,128},{128,0},{1,129},{129,1},{2,130},{130,2},{3,131},{131,3},{4... | collective-permute-start | bytes 8650760 | tf_op jit(solution)/shard_map/ppermute | solution.py:77
  418.6 48.6 %all-to-all-start.3 = ((bf16[2,32,14,512]{3,0,2,1:T(2,128)(2,1)}), bf16[2,32,14,512]{3,0,2,1:T(2,128)(2,1)S(1)}, u32[]{:S(2)}, u32[]{:S(2)}) async-start(bf16[2,32,14,512]{3,0,2,1:T(2,128)(2,1)} %copy.89), calls=%async_computation.5 | async-start | bytes 1835008 | tf_op jit(solution)/shard_map/all_to_all | solution.py:19
  434.6 75.1 %collective-permute-start.11 = (bf16[2,352,1024]{2,1,0:T(8,128)(2,1)}, bf16[2,352,1024]{2,1,0:T(8,128)(2,1)}, u32[]{:S(2)}, u32[]{:S(2)}) collective-permute-start(bf16[2,352,1024]{2,1,0:T(8,128)(2,1)} %broadcast_select_fusion.1), channel_id=1, source_target_pairs={{0,128},{128,0},{1,129},{129,1},{2,130},{130,2},{3,131},{131,3},{4... | collective-permute-start | bytes 4325384 | tf_op jit(solution)/shard_map/ppermute | solution.py:77
  473.2 21.2 %copy-start.14 = (f32[128]{0:T(128)S(1)}, f32[128]{0:T(128)}, u32[]{:S(2)}) copy-start(f32[128]{0:T(128)} %copy-done.13) | copy-start | bytes 1540
  473.2 21.2 %copy-start.17 = (f32[128]{0:T(128)S(1)}, f32[128]{0:T(128)}, u32[]{:S(2)}) copy-start(f32[128]{0:T(128)} %get-tuple-element.41) | copy-start | bytes 1540
  494.4 15.3 %copy-start.5 = (bf16[2,352,2048]{2,1,0:T(8,128)(2,1)S(1)}, bf16[2,352,2048]{2,1,0:T(8,128)(2,1)}, u32[]{:S(2)}) copy-start(bf16[2,352,2048]{2,1,0:T(8,128)(2,1)} %copy-done.4) | copy-start | bytes 8650756
  (17 other events, 57.6 us)
Sparse Core Ops, SparseCore 0:
  104.6 40.7 all-gather.2
  179.8 39.1 reduce-scatter.2
  306.7 46.2 all-gather.4
  370.1 45.3 reduce-scatter.4

commit v8 on v7

--- a/solution.py
+++ b/solution.py
@@ -155,8 +155,29 @@
     arrived = lax.all_gather(to_experts(outgoing), "tensor", axis=3, tiled=True)
     gate_full = gate_up_full[:, 0]
     up_full = gate_up_full[:, 1]
-    pre_gate = jnp.einsum("escd,edf->escf", arrived, gate_full, preferred_element_type=jnp.float32)
-    pre_up = jnp.einsum("escd,edf->escf", arrived, up_full, preferred_element_type=jnp.float32)
+    half_count = feature_count // 2
+    dp_index = lax.axis_index("dp")
+    own_rows = lax.dynamic_slice_in_dim(arrived, dp_index * half_count, half_count, 3)
+    other_rows = lax.dynamic_slice_in_dim(arrived, (1 - dp_index) * half_count, half_count, 3)
+    other_pieces = ((first_other[0, 0], second_other[0, 0]), (rest_other[0, 0], rest_other[0, 1]))
+
+    def projected(which):
+        return jnp.stack(
+            [
+                jnp.einsum(
+                    "scd,df->scf", own_rows[e], w_gate_up[e, which],
+                    preferred_element_type=jnp.float32,
+                )
+                + jnp.einsum(
+                    "scd,df->scf", other_rows[e], other_pieces[e][which],
+                    preferred_element_type=jnp.float32,
+                )
+                for e in range(local_experts)
+            ]
+        )
+
+    pre_gate = projected(0)
+    pre_up = projected(1)
     activation = (jax.nn.silu(pre_gate) * pre_up).astype(jnp.bfloat16)
     partial_out = jnp.einsum(
         "escf,efd->escd", activation, down_full, preferred_element_type=jnp.float32

time: 538 us -> 531 us (0.987)
  waiting for transfers between devices: 245 us -> 230 us
  local copies, waits for them, and re-layouts: 60.7 us -> 66.3 us
    ppermute x1, waiting for transfers between devices: 47.2 us -> 0.01 us  [per_device(): second_other = lax.ppermute(w_gate_up[0:1, 1:2], 'dp', DP_SWAP)]
    all_gather x1, waiting for transfers between devices: 0.01 us -> 36.1 us  [per_device(): arrived = lax.all_gather(to_experts(outgoing), 'tensor', axis=3, tiled=True)]
    all_gather x1, waiting for transfers between devices: 46.2 us -> 38.6 us  [per_device(): lax.all_gather(to_experts(grad_slot), 'tensor', axis=3, tiled=True)]
    reduce_scatter x1, waiting for transfers between devices: 39.3 us -> 45.5 us  [per_device(): lax.psum_scatter(partial_out.astype(jnp.bfloat16), 'tensor', scatter_dime...]
    dot_general x2 -> x8, matrix products: 8.3 us -> 12.9 us  [the longest x4 7.32 us: projected(): jnp.einsum('scd,df->scf', other_rows[e], other_pieces[e][which], preferre...]
  transfers between devices with their start and end apart: 18 -> 18, of which waited for: 9 -> 9; matrix products, arithmetic and copies ran while one was open for 11% -> 14% of each run, Pallas kernels for 0% -> 0%
where the time goes in v8:
time: 531 us; the launch traced here: 522 us
  waiting for transfers between devices  230 us (43%)
  blocking collectives  96.9 us (18%)
  local copies, waits for them, and re-layouts  66.3 us (12%)
  matrix products  45.5 us (9%)
  other arithmetic  34.5 us (6%)
  starting transfers between devices  33.9 us (6%)
  between operations  14.7 us (3%)
    all_to_all x2, blocking collectives, to_experts(): lax.all_to_all(outgoing, 'expert', split_axis=1, concat_axis=1, tiled=True)  67.1 us
    all_to_all x2, waiting for transfers between devices, to_tokens(): lax.all_to_all(outgoing, 'expert', split_axis=1, concat_axis=1, tiled=True)  50 us
    reduce_scatter x1, waiting for transfers between devices, per_device(): lax.psum_scatter(partial_out.astype(jnp.bfloat16), 'tensor', scatter_dime...  45.5 us
    all_gather x1, waiting for transfers between devices, per_device(): lax.all_gather(to_experts(grad_slot), 'tensor', axis=3, tiled=True)  38.6 us
    all_gather x1, waiting for transfers between devices, per_device(): arrived = lax.all_gather(to_experts(outgoing), 'tensor', axis=3, tiled=True)  36.1 us
    reduce_scatter x1, waiting for transfers between devices, per_device(): lax.psum_scatter(d_entry_part.astype(jnp.bfloat16), 'tensor', scatter_dim...  35.4 us
    ppermute x1, waiting for transfers between devices, per_device(): down_other = lax.ppermute(w_down, 'dp', DP_SWAP)  22.6 us
    all_to_all x2, starting transfers between devices, to_tokens(): lax.all_to_all(outgoing, 'expert', split_axis=1, concat_axis=1, tiled=True)  18 us
  transfers between devices with their start and end apart: 18, of which 9 were waited for; matrix products, arithmetic and copies ran while one was open for 14% of the time, Pallas kernels for 0%

profile of v8, /device:TPU:32, one launch (start us, length us, event | category | flops | bytes accessed | tf_op | source)
XLA Modules:
  0.0 521.6 jit_solution(2365264565536121640)
XLA Ops:
  37.5 4.0 gather_fusion.2
  43.6 22.6 %collective-permute-done.3 = bf16[2,352,1024]{2,1,0:T(8,128)(2,1)} collective-permute-done((bf16[2,352,1024]{2,1,0:T(8,128)(2,1)}, bf16[2,352,1024]{2,1,0:T(8,128)(2,1)}, u32[]{:S(2)}, u32[]{:S(2)}) %collective-permute-start.3) | collective-permute-done | bytes 1441824 | tf_op jit(solution)/shard_map/ppermute | solution.py:110
  68.3 36.9 %all_to_all.20 = bf16[2,32,14,512]{3,0,2,1:T(2,128)(2,1)S(1)} all-to-all(bf16[2,32,14,512]{3,0,2,1:T(2,128)(2,1)S(1)} %copy.62), channel_id=1, replica_groups=mesh['dp'=2,'expert'=32,'tensor'=4] {'expert'}, dimensions={1} | all-to-all | bytes 1835008 | tf_op jit(solution)/shard_map/all_to_all | solution.py:15
  111.2 36.1 %all-gather.3.cloned.1.call-done = bf16[2,32,14,2048]{3,1,2,0:T(8,128)(2,1)} async-done(((bf16[2,32,14,512]{3,1,2,0:T(8,128)(2,1)}), bf16[2,32,14,2048]{3,1,2,0:T(8,128)(2,1)}) %all-gather.3.cloned.1.call-update) | async-done | bytes 3670032 | tf_op jit(solution)/shard_map/all_gather | solution.py:155
  162.6 7.0 %convolution_convert_fusion = bf16[2,32,14,2048]{3,1,2,0:T(8,128)(2,1)} fusion(bf16[2,32,14,352]{3,1,2,0:T(8,128)(2,1)S(1)} %multiply_convert_fusion.3, bf16[2,352,1024]{2,1,0:T(8,128)(2,1)} %collective-permute-done.3, bf16[2,352,1024]{2,1,0:T(8,128)(2,1)} %param.17, pred[]{:T(512)S(6)} %eq.45), kind=kOutput, calls=%fused_computation.15 | convolution fusion | flops 1306656768 | bytes 7184385 | tf_op jit(solution)/shard_map/escf,efd->escd/dot_general | solution.py:182
  169.6 45.5 %reduce-scatter.3.cloned.1.call-done = bf16[2,32,14,512]{3,1,2,0:T(8,128)(2,1)} async-done(((bf16[2,32,14,2048]{3,1,2,0:T(8,128)(2,1)}), bf16[2,32,14,512]{3,1,2,0:T(8,128)(2,1)}) %reduce-scatter.3.cloned.1.call-update) | async-done | bytes 917520 | tf_op jit(solution)/shard_map/reduce_scatter | solution.py:185
  218.1 9.1 %all-to-all-start.1 = ((bf16[2,32,14,512]{3,0,2,1:T(2,128)(2,1)}), bf16[2,32,14,512]{3,0,2,1:T(2,128)(2,1)}, u32[]{:S(2)}, u32[]{:S(2)}) async-start(bf16[2,32,14,512]{3,0,2,1:T(2,128)(2,1)} %copy.64), calls=%async_computation.2 | async-start | bytes 1835008 | tf_op jit(solution)/shard_map/all_to_all | solution.py:19
  227.9 3.7 gather_fusion.4
  231.8 18.8 %all-to-all-done.1 = bf16[2,32,14,512]{3,0,2,1:T(2,128)(2,1)} async-done(((bf16[2,32,14,512]{3,0,2,1:T(2,128)(2,1)}), bf16[2,32,14,512]{3,0,2,1:T(2,128)(2,1)}, u32[]{:S(2)}, u32[]{:S(2)}) %all-to-all-start.1) | async-done | bytes 917536 | tf_op jit(solution)/shard_map/all_to_all | solution.py:19
  263.3 4.0 gather_fusion.5
  272.6 30.2 %all_to_all.21 = bf16[2,32,14,512]{3,0,2,1:T(2,128)(2,1)S(1)} all-to-all(bf16[2,32,14,512]{3,0,2,1:T(2,128)(2,1)S(1)} %copy.67), channel_id=1, replica_groups=mesh['dp'=2,'expert'=32,'tensor'=4] {'expert'}, dimensions={1} | all-to-all | bytes 1835008 | tf_op jit(solution)/shard_map/all_to_all | solution.py:15
  304.2 7.6 %maximum_select_fusion = bf16[2,2,2048,352]{2,3,1,0:T(8,128)(2,1)} fusion(bf16[1,2,1024,352]{2,3,1,0:T(8,128)(2,1)} %collective-permute-done.8, bf16[1,1,1024,352]{2,3,1,0:T(8,128)(2,1)} %collective-permute-done.9, bf16[1,1,1024,352]{2,3,1,0:T(8,128)(2,1)S(1)} %copy-done.11, bf16[2,2,1024,352]{2,3,1,0:T(8,128)(2,1)} %param.16, pred[]{:T(512)S(6)} %eq.45), kind=kLoop, calls=%fused_computation.10 | loop fusion | flops 49020928 | bytes 11534337 | tf_op jit(solution)/shard_map/jit(_where)/select_n | solution.py:145
  311.7 38.6 %all-gather.5.cloned.1.call-done = bf16[2,32,14,2048]{3,1,2,0:T(8,128)(2,1)} async-done(((bf16[2,32,14,512]{3,1,2,0:T(8,128)(2,1)}), bf16[2,32,14,2048]{3,1,2,0:T(8,128)(2,1)}) %all-gather.5.cloned.1.call-update) | async-done | bytes 3670032 | tf_op jit(solution)/shard_map/all_gather | solution.py:200
  350.4 7.0 %multiply_convert_fusion.2 = (bf16[2,32,14,352]{3,1,2,0:T(8,128)(2,1)S(1)}, bf16[2,32,14,352]{3,1,2,0:T(8,128)(2,1)S(1)}) fusion(f32[1,32,14,352]{3,1,2,0:T(8,128)} %copy-done.14, f32[1,32,14,352]{3,1,2,0:T(8,128)} %copy-done.15, f32[1,32,14,352]{3,1,2,0:T(8,128)} %copy-done.13, f32[1,32,14,352]{3,1,2,0:T(8,128)} %copy-done.12, ...), kind=kOutput, calls=%fused_computation.32 | convolution fusion | flops 1309552640 | bytes 10338305 | tf_op jit(solution)/shard_map/escd,efd->escf/dot_general | solution.py:201
  359.6 3.9 add_convert_fusion
  363.5 3.9 convolution_bitcast_fusion.1
  373.6 35.4 %reduce-scatter.5.cloned.1.call-done = bf16[2,32,14,512]{3,1,2,0:T(8,128)(2,1)} async-done(((bf16[2,32,14,2048]{3,1,2,0:T(8,128)(2,1)}), bf16[2,32,14,512]{3,1,2,0:T(8,128)(2,1)}) %reduce-scatter.5.cloned.1.call-update) | async-done | bytes 917520 | tf_op jit(solution)/shard_map/reduce_scatter | solution.py:213
  412.1 9.0 %all-to-all-start.3 = ((bf16[2,32,14,512]{3,0,2,1:T(2,128)(2,1)}), bf16[2,32,14,512]{3,0,2,1:T(2,128)(2,1)S(1)}, u32[]{:S(2)}, u32[]{:S(2)}) async-start(bf16[2,32,14,512]{3,0,2,1:T(2,128)(2,1)} %copy.69), calls=%async_computation.5 | async-start | bytes 1835008 | tf_op jit(solution)/shard_map/all_to_all | solution.py:19
  421.1 4.0 bitcast_convert_fusion
  429.6 31.2 %all-to-all-done.3 = bf16[2,32,14,512]{3,0,2,1:T(2,128)(2,1)S(1)} async-done(((bf16[2,32,14,512]{3,0,2,1:T(2,128)(2,1)}), bf16[2,32,14,512]{3,0,2,1:T(2,128)(2,1)S(1)}, u32[]{:S(2)}, u32[]{:S(2)}) %all-to-all-start.3) | async-done | bytes 917536 | tf_op jit(solution)/shard_map/all_to_all | solution.py:19
  471.7 16.2 %all-reduce.2 = (f32[128]{0:T(128)S(1)}, f32[128,6]{1,0:T(8,128)S(1)}) all-reduce(f32[128]{0:T(128)S(1)} %multiply_reduce_fusion.2, f32[128,6]{1,0:T(8,128)S(1)} %multiply_reduce_fusion), channel_id=1, replica_groups=mesh['dp'=2,'expert'=32,'tensor'=4] {'tensor'}, use_global_device_ids=true, to_apply=%region_11.12 | all-reduce | flops 896 | bytes 7168 | tf_op jit(solution)/shard_map/psum | solution.py:222
  488.1 13.6 %all_gather.11 = bf16[128,2048]{1,0:T(8,128)(2,1)S(1)} all-gather(bf16[128,512]{1,0:T(8,128)(2,1)S(1)} %subtract_convert_fusion), channel_id=1, replica_groups=mesh['dp'=2,'expert'=32,'tensor'=4] {'tensor'}, dimensions={1}, use_global_device_ids=true | all-gather | bytes 655360 | tf_op jit(solution)/shard_map/all_gather | solution.py:230
  503.2 3.4 add_convert_fusion.2
  506.6 5.7 %add_convert_fusion.1 = bf16[2,2,1024,352]{2,3,0,1:T(8,128)(2,1)S(1)} fusion(bf16[2,2,1024,352]{2,3,0,1:T(8,128)(2,1)} %collective-permute-done.10, pred[]{:T(512)S(6)} %eq.45, bf16[2,2,2048,352]{2,3,0,1:T(8,128)(2,1)} %copy-done.1), kind=kLoop, calls=%fused_computation.12 | loop fusion | flops 7208960 | bytes 11534337 | tf_op jit(solution)/shard_map/convert_element_type | solution.py:82
  (156 shorter events, 109.6 us)
Async XLA Ops:
  7.2 140.1 %all-gather.3.cloned.1.call-start = ((), (), s32[]{:S(2)}) async-start(), calls=%async_computation.6 | async-start | bytes 4587520 | tf_op jit(solution)/shard_map/all_gather | solution.py:155
  8.8 11.2 %copy-start.21 = (s32[128,6]{0,1:T(8,128)S(1)}, s32[128,6]{0,1:T(8,128)}, u32[]{:S(2)}) copy-start(s32[128,6]{0,1:T(8,128)} %param.15) | copy-start | bytes 9220
  11.0 15.1 %collective-permute-start = (bf16[128,512]{1,0:T(8,128)(2,1)}, bf16[128,512]{1,0:T(8,128)(2,1)}, u32[]{:S(2)}, u32[]{:S(2)}) collective-permute-start(bf16[128,512]{1,0:T(8,128)(2,1)} %get-tuple-element.55), channel_id=1, source_target_pairs={{0,1},{1,2},{2,3},{3,0},{4,5},{5,6},{6,7},{7,4},{8,9},{9,10},{10,1... | collective-permute-start | bytes 393224 | tf_op jit(solution)/shard_map/ppermute | solution.py:26
  12.5 13.6 %collective-permute-start.1 = (bf16[128,512]{1,0:T(8,128)(2,1)}, bf16[128,512]{1,0:T(8,128)(2,1)}, u32[]{:S(2)}, u32[]{:S(2)}) collective-permute-start(bf16[128,512]{1,0:T(8,128)(2,1)} %get-tuple-element.54), channel_id=1, source_target_pairs={{0,2},{1,3},{2,0},{3,1},{4,6},{5,7},{6,4},{7,5},{8,10},{9,11},{10,... | collective-permute-start | bytes 393224 | tf_op jit(solution)/shard_map/ppermute | solution.py:26
  15.3 10.9 %collective-permute-start.2 = (bf16[128,512]{1,0:T(8,128)(2,1)S(1)}, bf16[128,512]{1,0:T(8,128)(2,1)}, u32[]{:S(2)}, u32[]{:S(2)}) collective-permute-start(bf16[128,512]{1,0:T(8,128)(2,1)S(1)} %get-tuple-element.53), channel_id=1, source_target_pairs={{0,3},{1,0},{2,1},{3,2},{4,7},{5,4},{6,5},{7,6},{8,11},{9,8},{10,9... | collective-permute-start | bytes 393224 | tf_op jit(solution)/shard_map/ppermute | solution.py:26
  17.9 25.7 %collective-permute-start.4 = (bf16[1,1,1024,352]{2,3,1,0:T(8,128)(2,1)}, bf16[1,1,1024,352]{2,3,1,0:T(8,128)(2,1)S(1)}, u32[]{:S(2)}, u32[]{:S(2)}) collective-permute-start(bf16[1,1,1024,352]{2,3,1,0:T(8,128)(2,1)} %get-tuple-element.49), channel_id=1, source_target_pairs={{0,128},{128,0},{1,129},{129,1},{2,130},{130,2},{3,131},{131,3},{4... | collective-permute-start | bytes 2162696 | tf_op jit(solution)/shard_map/ppermute | solution.py:136
  18.0 48.1 %collective-permute-start.3 = (bf16[2,352,1024]{2,1,0:T(8,128)(2,1)}, bf16[2,352,1024]{2,1,0:T(8,128)(2,1)}, u32[]{:S(2)}, u32[]{:S(2)}) collective-permute-start(bf16[2,352,1024]{2,1,0:T(8,128)(2,1)} %param.17), channel_id=1, source_target_pairs={{0,128},{128,0},{1,129},{129,1},{2,130},{130,2},{3,131},{131,3},{4... | collective-permute-start | bytes 4325384 | tf_op jit(solution)/shard_map/ppermute | solution.py:110
  31.0 4.8 collective-permute-start.5
  31.6 5.1 collective-permute-start.6
  32.5 4.2 collective-permute-start.7
  43.6 105.9 %copy-start.10 = (bf16[1,1,1024,352]{2,3,1,0:T(8,128)(2,1)}, bf16[1,1,1024,352]{2,3,1,0:T(8,128)(2,1)S(1)}, u32[]{:S(2)}) copy-start(bf16[1,1,1024,352]{2,3,1,0:T(8,128)(2,1)S(1)} %collective-permute-done.4) | copy-start | bytes 2162692
  106.4 108.7 %reduce-scatter.3.cloned.1.call-start = ((), (), s32[]{:S(2)}) async-start(), calls=%async_computation.7 | async-start | bytes 4587520 | tf_op jit(solution)/shard_map/reduce_scatter | solution.py:185
  109.0 44.6 %collective-permute-start.8 = (bf16[1,2,1024,352]{2,3,1,0:T(8,128)(2,1)}, bf16[1,2,1024,352]{2,3,1,0:T(8,128)(2,1)}, u32[]{:S(2)}, u32[]{:S(2)}) collective-permute-start(bf16[1,2,1024,352]{2,3,1,0:T(8,128)(2,1)} %slice.107), channel_id=1, source_target_pairs={{0,128},{128,0},{1,129},{129,1},{2,130},{130,2},{3,131},{131,3},{4... | collective-permute-start | bytes 4325384 | tf_op jit(solution)/shard_map/ppermute | solution.py:141
  109.9 48.7 %collective-permute-start.9 = (bf16[1,1,1024,352]{2,3,1,0:T(8,128)(2,1)}, bf16[1,1,1024,352]{2,3,1,0:T(8,128)(2,1)}, u32[]{:S(2)}, u32[]{:S(2)}) collective-permute-start(bf16[1,1,1024,352]{2,3,1,0:T(8,128)(2,1)} %get-tuple-element.48), channel_id=1, source_target_pairs={{0,128},{128,0},{1,129},{129,1},{2,130},{130,2},{3,131},{131,3},{4... | collective-permute-start | bytes 2162696 | tf_op jit(solution)/shard_map/ppermute | solution.py:140
  151.5 8.8 %copy-start.12 = (f32[1,32,14,352]{3,1,2,0:T(8,128)}, f32[1,32,14,352]{3,1,2,0:T(8,128)S(1)}, u32[]{:S(2)}) copy-start(f32[1,32,14,352]{3,1,2,0:T(8,128)S(1)} %fusion.8) | copy-start | bytes 1892356
  169.5 58.1 %copy-start.22 = (f32[128,6]{0,1:T(8,128)S(1)}, f32[128,6]{0,1:T(8,128)}, u32[]{:S(2)}) copy-start(f32[128,6]{0,1:T(8,128)} %param.14) | copy-start | bytes 9220
  218.1 32.4 %all-to-all-start.1 = ((bf16[2,32,14,512]{3,0,2,1:T(2,128)(2,1)}), bf16[2,32,14,512]{3,0,2,1:T(2,128)(2,1)}, u32[]{:S(2)}, u32[]{:S(2)}) async-start(bf16[2,32,14,512]{3,0,2,1:T(2,128)(2,1)} %copy.64), calls=%async_computation.2 | async-start | bytes 1835008 | tf_op jit(solution)/shard_map/all_to_all | solution.py:19
  227.2 123.2 %all-gather.5.cloned.1.call-start = ((), (), s32[]{:S(2)}) async-start(), calls=%async_computation.8 | async-start | bytes 4587520 | tf_op jit(solution)/shard_map/all_gather | solution.py:200
  271.6 32.6 %copy-start.11 = (bf16[1,1,1024,352]{2,3,1,0:T(8,128)(2,1)S(1)}, bf16[1,1,1024,352]{2,3,1,0:T(8,128)(2,1)}, u32[]{:S(2)}) copy-start(bf16[1,1,1024,352]{2,3,1,0:T(8,128)(2,1)} %copy-done.10) | copy-start | bytes 2162692
  303.9 105.1 %reduce-scatter.5.cloned.1.call-start = ((), (), s32[]{:S(2)}) async-start(), calls=%async_computation.9 | async-start | bytes 4587520 | tf_op jit(solution)/shard_map/reduce_scatter | solution.py:213
  373.2 130.0 %collective-permute-start.10 = (bf16[2,2,1024,352]{2,3,0,1:T(8,128)(2,1)}, bf16[2,2,1024,352]{2,3,0,1:T(8,128)(2,1)}, u32[]{:S(2)}, u32[]{:S(2)}) collective-permute-start(bf16[2,2,1024,352]{2,3,0,1:T(8,128)(2,1)} %broadcast_select_fusion), channel_id=1, source_target_pairs={{0,128},{128,0},{1,129},{129,1},{2,130},{130,2},{3,131},{131,3},{4... | collective-permute-start | bytes 8650760 | tf_op jit(solution)/shard_map/ppermute | solution.py:77
  412.1 48.7 %all-to-all-start.3 = ((bf16[2,32,14,512]{3,0,2,1:T(2,128)(2,1)}), bf16[2,32,14,512]{3,0,2,1:T(2,128)(2,1)S(1)}, u32[]{:S(2)}, u32[]{:S(2)}) async-start(bf16[2,32,14,512]{3,0,2,1:T(2,128)(2,1)} %copy.69), calls=%async_computation.5 | async-start | bytes 1835008 | tf_op jit(solution)/shard_map/all_to_all | solution.py:19
  427.9 75.3 %collective-permute-start.11 = (bf16[2,352,1024]{2,1,0:T(8,128)(2,1)}, bf16[2,352,1024]{2,1,0:T(8,128)(2,1)}, u32[]{:S(2)}, u32[]{:S(2)}) collective-permute-start(bf16[2,352,1024]{2,1,0:T(8,128)(2,1)} %broadcast_select_fusion.1), channel_id=1, source_target_pairs={{0,128},{128,0},{1,129},{129,1},{2,130},{130,2},{3,131},{131,3},{4... | collective-permute-start | bytes 4325384 | tf_op jit(solution)/shard_map/ppermute | solution.py:77
  487.9 15.3 %copy-start.5 = (bf16[2,352,2048]{2,1,0:T(8,128)(2,1)S(1)}, bf16[2,352,2048]{2,1,0:T(8,128)(2,1)}, u32[]{:S(2)}) copy-start(bf16[2,352,2048]{2,1,0:T(8,128)(2,1)} %copy-done.4) | copy-start | bytes 8650756
  (17 other events, 59.2 us)
Sparse Core Ops, SparseCore 0:
  106.5 40.7 all-gather.2
  169.7 45.3 reduce-scatter.2
  304.1 46.2 all-gather.4
  363.6 45.3 reduce-scatter.4
